TPU v7x, 512 devices: a whole 4x4x16 slice. The times are simulated.
512 devices in a mesh: grp: 16 (over z), wrk: 32 (over y, x, core).
Axes of the slice: x: 4, y: 4, z: 16, core: 2. Of those that a mesh axis runs over, the one named last changes fastest.
Arguments:
- orbitals: bfloat16 [512, 32, 1024], P(('grp', 'wrk')), may hold values from -6 to 6
- offsets: int32 [512, 3], replicated, may hold values from 0 to 135, as said below
- pair_slots: int32 [16, 32, 6, 2], P('grp', 'wrk'), may hold values from 0 to 511, as said below
- pair_count: int32 [16, 32], P('grp', 'wrk'), may hold values from 0 to 6, as said below
Outputs:
- exchange_fields: float32 [512, 32, 1024], P(('grp', 'wrk'))
Inputs may be any that keep to these rules, and one draw needn't show every extreme that they name: Row o gives the grid point of the first cell of orbital o's box; offsets of orbitals of the same or adjacent groups differ by less than 32 in each coordinate. Every slot of pair_slots[g, w] holds an orbital a of group g (numbers g * 32 to g * 32 + 31) and an orbital b other than a of group g or g + 1, with offsets of a and b differing by less than 32 in each coordinate; slots at or past pair_count[g, w] hold entries of the same kind that are not pairs. `pair_count`: the counts of every group sum to 96; in every group one worker has 6 pairs and one has none.
All inputs are finite; a program needn't handle non-finite values.
Results may differ from a plain program's by a relative error of at most 0.0003.
Values may be sent and summed in bfloat16 or wider, within the bound.
No kernel may reach another device: no remote copies, remote signals or barrier semaphores. Data moves between devices by JAX's collectives and lax.ppermute only.
A program may use at most 64 MiB of HBM per device.

v0:
```python
import jax
import jax.numpy as jnp
from jax import lax
from jax.sharding import PartitionSpec as P

screen_shift = 0.05
highest = lax.Precision.HIGHEST


def passed_along(value, axis, steps):
    count = lax.axis_size(axis)
    initial, last = (max(0, -steps), min(count, count - steps))
    return lax.ppermute(value, axis, [(source, source + steps) for source in range(initial, last)])


def sine_table(box_edge):
    counting = jnp.arange(box_edge, dtype=jnp.float32) + 1.0
    scaling = jnp.sqrt(2.0 / (box_edge + 1.0))
    return scaling * jnp.sin(jnp.pi * counting[:, None] * counting[None, :] / (box_edge + 1.0))


def inverse_symbol(box_edge):
    counting = jnp.arange(box_edge, dtype=jnp.float32) + 1.0
    eigen_one = 4.0 * jnp.sin(jnp.pi * counting / (2.0 * (box_edge + 1.0))) ** 2
    eigen_sum = eigen_one[:, None, None] + eigen_one[None, :, None] + eigen_one[None, None, :]
    return 1.0 / (eigen_sum + screen_shift)


def box_window(offset_diff, box_edge):
    cell_index = jnp.arange(box_edge, dtype=jnp.int32)
    plane_index = jnp.arange(box_edge * box_edge, dtype=jnp.int32)
    row_cell = cell_index - offset_diff[0]
    col_second = plane_index // box_edge - offset_diff[1]
    col_third = plane_index % box_edge - offset_diff[2]
    row_inside = (row_cell >= 0) & (row_cell < box_edge)
    col_inside = (
        (col_second >= 0) & (col_second < box_edge) & (col_third >= 0) & (col_third < box_edge)
    )
    return row_inside[:, None] & col_inside[None, :]


def move_box(single_box, offset_diff):
    box_edge, plane_size = single_box.shape
    doubled = jnp.concatenate([single_box, single_box], axis=0)
    row_start = jnp.mod(box_edge - offset_diff[0], box_edge)
    rolled = lax.dynamic_slice_in_dim(doubled, row_start, box_edge, 0)
    doubled = jnp.concatenate([rolled, rolled], axis=1)
    col_start = jnp.mod(plane_size - offset_diff[1] * box_edge - offset_diff[2], plane_size)
    rolled = lax.dynamic_slice_in_dim(doubled, col_start, plane_size, 1)
    inside = box_window(offset_diff, box_edge)
    return jnp.where(inside, rolled, jnp.zeros_like(rolled))


def solve_boxes(density, sine_rows, plane_sines, symbol):
    count_boxes, box_edge, plane_size = density.shape

    def apply_sines(field_block):
        along_first = jnp.einsum("kx,nxf->nkf", sine_rows, field_block, precision=highest)
        flat_rows = along_first.reshape(count_boxes * box_edge, plane_size)
        along_plane = jnp.dot(
            flat_rows, plane_sines, precision=highest, preferred_element_type=jnp.float32
        )
        return along_plane.reshape(count_boxes, box_edge, plane_size)

    spectrum = apply_sines(density) * symbol
    return apply_sines(spectrum)


def corner_of(orbital, offsets):
    listing = jnp.arange(offsets.shape[0], dtype=jnp.int32)
    chosen = orbital[:, None] == listing[None, :]
    return jnp.sum(jnp.where(chosen[:, :, None], offsets[None, :, :], 0), axis=1, dtype=jnp.int32)


def local(orbitals, offsets, pair_slots, pair_count):
    orb_dev, box_edge, plane_size = orbitals.shape
    workers = lax.axis_size("wrk")
    group_index = lax.axis_index("grp")
    grp_orbs = orb_dev * workers
    upper_set = passed_along(orbitals, "grp", -1)
    local_set = jnp.stack([orbitals, upper_set], axis=0)
    group_set = lax.all_gather(local_set, "wrk", axis=1, tiled=True)
    group_set = group_set.reshape(2 * grp_orbs, box_edge, plane_size)
    pair_list = pair_slots[0, 0]
    slot_cap = pair_list.shape[0]
    weights = (jnp.arange(slot_cap, dtype=jnp.int32) < pair_count[0, 0]).astype(jnp.float32)
    left_orb = pair_list[:, 0]
    right_orb = pair_list[:, 1]
    offset_diff = corner_of(right_orb, offsets) - corner_of(left_orb, offsets)
    left_row = left_orb - group_index * grp_orbs
    right_row = right_orb - group_index * grp_orbs
    left_boxes = jnp.take(group_set, left_row, axis=0)
    right_boxes = jnp.take(group_set, right_row, axis=0)
    moved_right = lax.map(lambda packed: move_box(packed[0], packed[1]), (right_boxes, offset_diff))
    sine_rows = sine_table(box_edge)
    plane_sines = (sine_rows[:, None, :, None] * sine_rows[None, :, None, :]).reshape(
        plane_size, plane_size
    )
    symbol = inverse_symbol(box_edge).reshape(box_edge, plane_size)
    left_field = left_boxes.astype(jnp.float32)
    right_field = moved_right.astype(jnp.float32)
    potential = solve_boxes(left_field * right_field, sine_rows, plane_sines, symbol)
    weighted = potential * weights[:, None, None]
    to_left = weighted * right_field
    to_right = lax.map(
        lambda packed: move_box(packed[0], -packed[1]), (weighted * left_field, offset_diff)
    )
    partial_sums = jnp.zeros((2 * grp_orbs, box_edge, plane_size), jnp.float32)
    partial_sums = partial_sums.at[left_row].add(to_left).at[right_row].add(to_right)
    sectioned = partial_sums.reshape(2, grp_orbs, box_edge, plane_size)
    from_below = passed_along(sectioned[1], "grp", 1)
    combined = sectioned[0] + from_below
    return lax.psum_scatter(combined, "wrk", scatter_dimension=0, tiled=True)


def solution(mesh):
    return jax.shard_map(
        local,
        mesh=mesh,
        in_specs=(P(("grp", "wrk"), None, None), P(), P("grp", "wrk", None, None), P("grp", "wrk")),
        out_specs=P(("grp", "wrk"), None, None),
        check_vma=False,
    )
```

profile of v0, /device:TPU:1, one launch (start us, length us, event | category | flops | bytes accessed | tf_op | source)
XLA Modules:
  0.0 378.2 jit_solution(14464792177218286480)
XLA Ops:
  6.5 1.3 collective-permute-start
  7.8 4.9 %collective-permute-done = bf16[1,32,1024]{2,1,0:T(8,128)(2,1)S(1)} collective-permute-done((bf16[1,32,1024]{2,1,0:T(8,128)(2,1)}, bf16[1,32,1024]{2,1,0:T(8,128)(2,1)S(1)}, u32[]{:S(2)}, u32[]{:S(2)}) %collective-permute-start) | collective-permute-done | bytes 65568 | tf_op jit(solution)/shard_map/ppermute | solution.py:13
  12.7 1.5 pad_maximum_fusion
  14.5 8.0 %broadcast_multiply_fusion = f32[32,32,32,32]{3,2,1,0:T(8,128)} fusion(f32[32,32]{1,0:T(8,128)S(1)} %sine_multiply_fusion), kind=kLoop, calls=%fused_computation.68 | loop fusion | flops 1048576 | bytes 4198400 | tf_op jit(solution)/shard_map/mul | solution.py:96
  22.5 13.7 %reshape.349 = f32[1024,1024,1]{1,0,2:T(8,128)} reshape(f32[32,32,32,32]{3,2,1,0:T(8,128)} %broadcast_multiply_fusion) | data formatting | bytes 8388608 | tf_op jit(solution)/shard_map/mul | solution.py:96
  36.4 0.2 add.221
  36.6 0.2 add.222
  37.7 0.2 select_reduce_fusion
  38.0 43.7 %all-gather.2.cloned.1.call-done = bf16[2,32,32,1024]{3,2,1,0:T(8,128)(2,1)} async-done(((bf16[2,1,32,1024]{3,2,1,0:T(8,128)(2,1)}), bf16[2,32,32,1024]{3,2,1,0:T(8,128)(2,1)}) %all-gather.2.cloned.1.call-update) | async-done | bytes 4194320 | tf_op jit(solution)/shard_map/all_gather | solution.py:82
  81.6 2.8 gather_fusion.1
  84.5 29.5 %while.26 = (s32[]{:T(128)}, bf16[6,32,1024]{2,1,0:T(8,128)(2,1)S(1)}, s32[6,3]{0,1:T(4,128)S(1)}, bf16[6,32,1024]{2,1,0:T(8,128)(2,1)S(1)}, s32[]{:T(128)}, /*i...) while((s32[]{:T(128)}, ...), condition=%wide.region_3.5_spmd, body=%wide.region_2.4_spmd.sunk | while | flops 349346 | bytes 396339 | solution.py:94
  84.6 0.6 fusion.73
  87.3 1.3 fusion.75
  88.6 0.7 compare_and_fusion.6
  89.2 0.2 fusion.76
  89.5 0.6 fusion.73
  92.2 1.3 fusion.75
  93.5 0.7 compare_and_fusion.6
  94.4 0.6 fusion.73
  97.1 1.3 fusion.75
  98.4 0.7 compare_and_fusion.6
  99.3 0.6 fusion.73
  102.0 1.3 fusion.75
  103.3 0.7 compare_and_fusion.6
  104.0 0.2 fusion.76
  104.2 0.6 fusion.73
  106.9 1.3 fusion.75
  108.2 0.7 compare_and_fusion.6
  108.9 0.2 fusion.76
  109.2 0.6 fusion.73
  111.8 1.3 fusion.75
  113.2 0.7 compare_and_fusion.6
  114.0 2.8 gather_fusion
  116.8 1.0 convolution_bitcast_fusion.1
  117.8 5.2 %convolution_multiply_fusion.1 = f32[6,32,1024]{2,1,0:T(8,128)S(1)} fusion(f32[6,32,1024]{2,1,0:T(8,128)S(1)} %convolution_bitcast_fusion.1, f32[1024,1024,1]{1,0,2:T(8,128)} %reshape.349, f32[32,1024]{1,0:T(8,128)S(1)} %add_divide_fusion), kind=kOutput, calls=%fused_computation.73 | convolution fusion | flops 2416115712 | bytes 5898240 | tf_op jit(solution)/shard_map/dot_general | solution.py:60
  123.0 0.9 convolution_bitcast_fusion
  124.0 3.0 convert_multiply_fusion.2
  126.9 29.4 %while.27 = (s32[]{:T(128)}, f32[6,32,1024]{2,1,0:T(8,128)S(1)}, s32[6,3]{0,1:T(4,128)S(1)}, f32[6,32,1024]{2,1,0:T(8,128)S(1)}, s32[]{:T(128)}, /*index=5*/s32[...) while((s32[]{:T(128)}, f32[6,32,1024]{2,1,0:T(8,128)S(1)}, ...), condition=%wide.region_6.8_spmd, body=%wide.region_5.7_spmd.sunk | while | flops 152741 | bytes 789555 | solution.py:105
  127.0 0.6 fusion.77
  129.7 1.3 fusion.79
  131.0 0.7 compare_and_fusion.7
  131.9 0.6 fusion.77
  134.6 1.3 fusion.79
  135.9 0.7 compare_and_fusion.7
  136.8 0.6 fusion.77
  139.5 1.3 fusion.79
  140.8 0.7 compare_and_fusion.7
  141.7 0.6 fusion.77
  144.4 1.3 fusion.79
  145.7 0.7 compare_and_fusion.7
  146.6 0.6 fusion.77
  149.2 1.3 fusion.79
  150.6 0.7 compare_and_fusion.7
  151.5 0.6 fusion.77
  154.1 1.3 fusion.79
  155.5 0.7 compare_and_fusion.7
  156.3 4.3 %broadcast_in_dim.83 = f32[64,32,1024]{2,1,0:T(8,128)} broadcast(f32[]{:T(128)} %constant.259.clone.1), dimensions={} | broadcast | bytes 8388612 | tf_op jit(solution)/shard_map/broadcast_in_dim | solution.py:108
  160.6 3.1 scatter_fusion
  163.7 3.0 scatter_fusion.1
  166.7 2.7 slice.77
  169.4 3.8 collective-permute-start.1
  173.1 89.3 %collective-permute-done.1 = f32[32,32,1024]{2,1,0:T(8,128)S(1)} collective-permute-done((f32[32,32,1024]{2,1,0:T(8,128)S(1)}, f32[32,32,1024]{2,1,0:T(8,128)S(1)}, u32[]{:S(2)}, u32[]{:S(2)}) %collective-permute-start.1) | collective-permute-done | bytes 4194336 | tf_op jit(solution)/shard_map/ppermute | solution.py:13
  262.5 2.9 slice_add_fusion
  265.4 106.0 %reduce-scatter.2.cloned.1.call-done = f32[1,32,1024]{2,1,0:T(8,128)} async-done(((f32[32,32,1024]{2,1,0:T(8,128)}), f32[1,32,1024]{2,1,0:T(8,128)}) %reduce-scatter.2.cloned.1.call-update) | async-done | bytes 131088 | tf_op jit(solution)/shard_map/reduce_scatter | solution.py:113
  (73 shorter events, 3.9 us)
Async XLA Ops:
  6.5 75.1 %all-gather.2.cloned.1.call-start = ((), (), s32[]{:S(2)}) async-start(), calls=%async_computation.1 | async-start | bytes 4325376 | tf_op jit(solution)/shard_map/all_gather | solution.py:82
  6.5 6.2 %collective-permute-start = (bf16[1,32,1024]{2,1,0:T(8,128)(2,1)}, bf16[1,32,1024]{2,1,0:T(8,128)(2,1)S(1)}, u32[]{:S(2)}, u32[]{:S(2)}) collective-permute-start(bf16[1,32,1024]{2,1,0:T(8,128)(2,1)} %param.10), channel_id=1, source_target_pairs={{32,0},{64,32},{96,64},{128,96},{160,128},{192,160},{224,192},{256... | collective-permute-start | bytes 196616 | tf_op jit(solution)/shard_map/ppermute | solution.py:13
  14.3 357.1 %reduce-scatter.2.cloned.1.call-start = ((), (), s32[]{:S(2)}) async-start(), calls=%async_computation.2 | async-start | bytes 4325376 | tf_op jit(solution)/shard_map/reduce_scatter | solution.py:113
  22.5 15.1 %copy-start.3 = (s32[1,1,6,2]{2,3,1,0:T(2,128)S(1)}, s32[1,1,6,2]{2,3,1,0:T(2,128)}, u32[]{:S(2)}) copy-start(s32[1,1,6,2]{2,3,1,0:T(2,128)} %param.12) | copy-start | bytes 148
  22.5 15.2 %copy-start.2 = (s32[512,3]{0,1:T(4,128)S(1)}, s32[512,3]{0,1:T(4,128)}, u32[]{:S(2)}) copy-start(s32[512,3]{0,1:T(4,128)} %param.11) | copy-start | bytes 18436
  116.8 7.2 %copy-start.1 = (f32[1024,1024,1]{1,0,2:T(8,128)S(1)}, f32[1024,1024,1]{1,0,2:T(8,128)}, u32[]{:S(2)}) copy-start(f32[1024,1024,1]{1,0,2:T(8,128)} %reshape.349) | copy-start | bytes 12582916
  166.7 95.8 %copy-start = (f32[64,32,1024]{2,1,0:T(8,128)S(1)}, f32[64,32,1024]{2,1,0:T(8,128)}, u32[]{:S(2)}) copy-start(f32[64,32,1024]{2,1,0:T(8,128)} %scatter_fusion.1) | copy-start | bytes 25165828
  169.4 93.1 %collective-permute-start.1 = (f32[32,32,1024]{2,1,0:T(8,128)S(1)}, f32[32,32,1024]{2,1,0:T(8,128)S(1)}, u32[]{:S(2)}, u32[]{:S(2)}) collective-permute-start(f32[32,32,1024]{2,1,0:T(8,128)S(1)} %slice.77), channel_id=1, source_target_pairs={{0,32},{32,64},{64,96},{96,128},{128,160},{160,192},{192,224},{224... | collective-permute-start | bytes 12582920 | tf_op jit(solution)/shard_map/ppermute | solution.py:13
Sparse Core Ops, SparseCore 0:
  14.4 67.1 all-gather.1
  265.5 105.8 reduce-scatter.1
where the time goes:
time: 380 us; the launch traced here: 378 us
  waiting for transfers between devices  244 us (64%)
  other arithmetic  45.8 us (12%)
  local copies, waits for them, and re-layouts  34.4 us (9%)
  loops' own time  24.5 us (6%)
  between operations  14.3 us (4%)
  matrix products  10.1 us (3%)
  starting transfers between devices  5.09 us (1%)
    reduce_scatter x1, waiting for transfers between devices, local(): return lax.psum_scatter(combined, 'wrk', scatter_dimension=0, tiled=True)  106 us
    ppermute x2, waiting for transfers between devices, passed_along(): lax.ppermute(value, axis, [(source, source + steps) for source in range(i...  94.3 us
    all_gather x1, waiting for transfers between devices, local(): group_set = lax.all_gather(local_set, 'wrk', axis=1, tiled=True)  43.7 us
    and x12, other arithmetic, box_window(): (col_second >= 0) & (col_second < box_edge) & (col_third >= 0)  15.8 us
    mul x1, local copies, waits for them, and re-layouts, local(): sine_rows[:, None, :, None] * sine_rows[None, :, None, :]  13.7 us
    another operation x1, loops' own time, local(): lax.map(lambda packed: move_box(packed[0], -packed[1]), (weighted * left_...  12.3 us
    another operation x1, loops' own time, local(): lax.map(lambda packed: move_box(packed[0], packed[1]), (right_boxes, offs...  12.3 us
    dot_general x2, matrix products, apply_sines(): jnp.dot(flat_rows, plane_sines, precision=highest, preferred_element_type...  8.15 us
  transfers between devices with their start and end apart: 4, of which 4 were waited for; matrix products, arithmetic and copies ran while one was open for 6% of the time, Pallas kernels for 0%

commit v1 on v0

v1 whole, which is shorter than its diff:
```python
import jax
import jax.numpy as jnp
from jax import lax
from jax.sharding import PartitionSpec as P

screen_shift = 0.05
highest = lax.Precision.HIGHEST


def passed_along(value, axis, steps):
    count = lax.axis_size(axis)
    initial, last = (max(0, -steps), min(count, count - steps))
    return lax.ppermute(value, axis, [(source, source + steps) for source in range(initial, last)])


def sine_table(box_edge):
    counting = jnp.arange(box_edge, dtype=jnp.float32) + 1.0
    scaling = jnp.sqrt(2.0 / (box_edge + 1.0))
    return scaling * jnp.sin(jnp.pi * counting[:, None] * counting[None, :] / (box_edge + 1.0))


def inverse_symbol(box_edge):
    counting = jnp.arange(box_edge, dtype=jnp.float32) + 1.0
    eigen_one = 4.0 * jnp.sin(jnp.pi * counting / (2.0 * (box_edge + 1.0))) ** 2
    eigen_sum = eigen_one[:, None, None] + eigen_one[None, :, None] + eigen_one[None, None, :]
    return 1.0 / (eigen_sum + screen_shift)


def shift_matrices(offset_diff, box_edge):
    cell = jnp.arange(box_edge, dtype=jnp.int32)

    def one_axis(shift):
        return cell[None, None, :] == (cell[None, :, None] - shift[:, None, None])

    row_shift = one_axis(offset_diff[:, 0])
    along_y = one_axis(offset_diff[:, 1])
    along_z = one_axis(offset_diff[:, 2])
    count = offset_diff.shape[0]
    plane_shift = (along_y[:, :, None, :, None] & along_z[:, None, :, None, :]).reshape(
        count, box_edge * box_edge, box_edge * box_edge
    )
    return row_shift.astype(jnp.float32), plane_shift.astype(jnp.bfloat16)


def move_bf16(boxes, row_shift, plane_shift):
    planes = jnp.einsum("pxc,pyc->pxy", boxes, plane_shift, preferred_element_type=jnp.float32)
    return jnp.einsum("pxa,pac->pxc", row_shift, planes, precision=highest)


def unmove_f32(fields, row_shift, plane_shift):
    rows = jnp.einsum("pax,pac->pxc", row_shift, fields, precision=highest)
    high = lax.reduce_precision(rows, exponent_bits=8, mantissa_bits=7)
    rest = rows - high
    middle = lax.reduce_precision(rest, exponent_bits=8, mantissa_bits=7)
    low = rest - middle
    parts = jnp.concatenate([high, middle, low], axis=1).astype(jnp.bfloat16)
    moved = jnp.einsum("pxc,pcy->pxy", parts, plane_shift, preferred_element_type=jnp.float32)
    box_edge = fields.shape[1]
    return (moved[:, :box_edge] + moved[:, box_edge : 2 * box_edge]) + moved[:, 2 * box_edge :]


def solve_boxes(density, sine_rows, plane_sines, symbol):
    count_boxes, box_edge, plane_size = density.shape

    def apply_sines(field_block):
        along_first = jnp.einsum("kx,nxf->nkf", sine_rows, field_block, precision=highest)
        flat_rows = along_first.reshape(count_boxes * box_edge, plane_size)
        along_plane = jnp.dot(
            flat_rows, plane_sines, precision=highest, preferred_element_type=jnp.float32
        )
        return along_plane.reshape(count_boxes, box_edge, plane_size)

    spectrum = apply_sines(density) * symbol
    return apply_sines(spectrum)


def corner_of(orbital, offsets):
    listing = jnp.arange(offsets.shape[0], dtype=jnp.int32)
    chosen = orbital[:, None] == listing[None, :]
    return jnp.sum(jnp.where(chosen[:, :, None], offsets[None, :, :], 0), axis=1, dtype=jnp.int32)


def rows_to_orbitals(fields, rows, count):
    chosen = rows[:, None] == jnp.arange(count, dtype=jnp.int32)[None, :]
    return jnp.sum(
        jnp.where(chosen[:, :, None, None], fields[:, None, :, :], 0.0), axis=0
    )


def local(orbitals, offsets, pair_slots, pair_count):
    orb_dev, box_edge, plane_size = orbitals.shape
    workers = lax.axis_size("wrk")
    group_index = lax.axis_index("grp")
    worker_index = lax.axis_index("wrk")
    grp_orbs = orb_dev * workers
    upper_set = passed_along(orbitals, "grp", -1)
    local_set = jnp.stack([orbitals, upper_set], axis=0)
    group_set = lax.all_gather(local_set, "wrk", axis=1, tiled=True)
    group_set = group_set.reshape(2 * grp_orbs, box_edge, plane_size)

    slot_cap = pair_slots.shape[2]
    per_worker = (slot_cap + 1) // 2
    group_slots = lax.all_gather(pair_slots[0, 0], "wrk").reshape(-1, 2)
    group_count = lax.all_gather(pair_count[0], "wrk").reshape(-1)
    in_use = (jnp.arange(slot_cap, dtype=jnp.int32)[None, :] < group_count[:, None]).reshape(-1)
    rank = jnp.cumsum(in_use.astype(jnp.int32)) - 1
    wanted = worker_index * per_worker + jnp.arange(per_worker, dtype=jnp.int32)
    match = in_use[None, :] & (rank[None, :] == wanted[:, None])
    pair_list = jnp.sum(jnp.where(match[:, :, None], group_slots[None, :, :], 0), axis=1)
    weights = jnp.any(match, axis=1).astype(jnp.float32)

    base = group_index * grp_orbs
    left_orb = jnp.where(weights > 0, pair_list[:, 0], base)
    right_orb = jnp.where(weights > 0, pair_list[:, 1], base)
    offset_diff = corner_of(right_orb, offsets) - corner_of(left_orb, offsets)
    left_row = jnp.clip(left_orb - base, 0, 2 * grp_orbs - 1)
    right_row = jnp.clip(right_orb - base, 0, 2 * grp_orbs - 1)
    left_boxes = jnp.take(group_set, left_row, axis=0)
    right_boxes = jnp.take(group_set, right_row, axis=0)
    row_shift, plane_shift = shift_matrices(offset_diff, box_edge)
    right_field = move_bf16(right_boxes, row_shift, plane_shift)

    sine_rows = sine_table(box_edge)
    plane_sines = (sine_rows[:, None, :, None] * sine_rows[None, :, None, :]).reshape(
        plane_size, plane_size
    )
    symbol = inverse_symbol(box_edge).reshape(box_edge, plane_size)
    left_field = left_boxes.astype(jnp.float32)
    potential = solve_boxes(left_field * right_field, sine_rows, plane_sines, symbol)
    weighted = potential * weights[:, None, None]
    to_left = weighted * right_field
    to_right = unmove_f32(weighted * left_field, row_shift, plane_shift)

    upper = right_row >= grp_orbs
    sent_fields = jnp.where(upper[:, None, None], to_right, 0.0)
    sent_rows = jnp.where(upper, right_row - grp_orbs, 0)
    got_fields = passed_along(sent_fields, "grp", 1)
    got_rows = passed_along(sent_rows, "grp", 1)

    kept_right = jnp.where(upper[:, None, None], 0.0, to_right)
    kept_rows = jnp.where(upper, 0, right_row)
    fields = jnp.concatenate([to_left, kept_right, got_fields], axis=0)
    rows = jnp.concatenate([left_row, kept_rows, got_rows], axis=0)
    combined = rows_to_orbitals(fields, rows, grp_orbs)
    return lax.psum_scatter(combined, "wrk", scatter_dimension=0, tiled=True)


def solution(mesh):
    return jax.shard_map(
        local,
        mesh=mesh,
        in_specs=(P(("grp", "wrk"), None, None), P(), P("grp", "wrk", None, None), P("grp", "wrk")),
        out_specs=P(("grp", "wrk"), None, None),
        check_vma=False,
    )
```

time: 380 us -> 273 us (0.72)
  waiting for transfers between devices: 244 us -> 112 us
  blocking collectives: 0 us -> 42.9 us
  loops' own time: 24.5 us -> 0 us
  local copies, waits for them, and re-layouts: 34.4 us -> 52.4 us
  other arithmetic: 45.8 us -> 30.7 us
    ppermute x2 -> x3, waiting for transfers between devices: 94.3 us -> 6.07 us  [passed_along(): lax.ppermute(value, axis, [(source, source + steps) for source in range(i...]
    all_gather x1, waiting for transfers between devices: 43.7 us -> 0.01 us  [local(): group_set = lax.all_gather(local_set, 'wrk', axis=1, tiled=True)]
    all_gather x0 -> x1, blocking collectives: none -> 28.5 us  [local(): group_slots = lax.all_gather(pair_slots[0, 0], 'wrk').reshape(-1, 2)]
    and x0 -> x1, local copies, waits for them, and re-layouts: none -> 28 us  [shift_matrices(): along_y[:, :, None, :, None] & along_z[:, None, :, None, :]]
    another operation x2 -> x0, loops' own time: 24.5 us -> none  [the longest x1 12.3 us: local(): lax.map(lambda packed: move_box(packed[0], -packed[1]), (weighted * left_...]
    and x24 -> x2, other arithmetic: 23.6 us -> 8.4 us  [the longest x1 7.82 us: shift_matrices(): along_y[:, :, None, :, None] & along_z[:, None, :, None, :]]
    unnamed x0 -> x1, blocking collectives: none -> 14.5 us
    slice x13 -> x2, local copies, waits for them, and re-layouts: 9.71 us -> 0.26 us  [the longest x1 0.18 us: shift_matrices(): row_shift = one_axis(offset_diff[:, 0])]
  transfers between devices with their start and end apart: 4 -> 5, of which waited for: 4 -> 2; matrix products, arithmetic and copies ran while one was open for 6% -> 25% of each run, Pallas kernels for 0% -> 0%
where the time goes in v1:
time: 273 us; the launch traced here: 272 us
  waiting for transfers between devices  112 us (41%)
  local copies, waits for them, and re-layouts  52.4 us (19%)
  blocking collectives  42.9 us (16%)
  other arithmetic  30.7 us (11%)
  between operations  14.4 us (5%)
  matrix products  11.7 us (4%)
  starting transfers between devices  7.87 us (3%)
    reduce_scatter x1, waiting for transfers between devices, local(): return lax.psum_scatter(combined, 'wrk', scatter_dimension=0, tiled=True)  105 us
    all_gather x1, blocking collectives, local(): group_slots = lax.all_gather(pair_slots[0, 0], 'wrk').reshape(-1, 2)  28.5 us
    and x1, local copies, waits for them, and re-layouts, shift_matrices(): along_y[:, :, None, :, None] & along_z[:, None, :, None, :]  28 us
    unnamed x1, blocking collectives  14.5 us
    mul x1, local copies, waits for them, and re-layouts, local(): sine_rows[:, None, :, None] * sine_rows[None, :, None, :]  13.9 us
    mul x1, other arithmetic, local(): sine_rows[:, None, :, None] * sine_rows[None, :, None, :]  7.97 us
    ppermute x3, starting transfers between devices, passed_along(): lax.ppermute(value, axis, [(source, source + steps) for source in range(i...  7.83 us
    and x1, other arithmetic, shift_matrices(): along_y[:, :, None, :, None] & along_z[:, None, :, None, :]  7.82 us
  transfers between devices with their start and end apart: 5, of which 2 were waited for; matrix products, arithmetic and copies ran while one was open for 25% of the time, Pallas kernels for 0%

profile of v1, /device:TPU:1, one launch (start us, length us, event | category | flops | bytes accessed | tf_op | source)
XLA Modules:
  0.0 271.6 jit_solution(14688250579499402019)
XLA Ops:
  6.5 0.0 all-gather.3.cloned.1.call-start
  6.5 1.3 collective-permute-start.1
  8.5 1.3 dynamic-slice
  9.8 0.7 bitcast_dynamic-update-slice_fusion
  10.5 14.5 %all-reduce.1 = s32[32]{0:T(128)S(1)} all-reduce(s32[32]{0:T(128)S(1)} %bitcast_dynamic-update-slice_fusion), channel_id=1, replica_groups=mesh['grp'=16,'wrk'=32] {'wrk'}, use_global_device_ids=true, to_apply=%add.1 | all-reduce | flops 32 | bytes 256
  24.9 0.1 iota_compare_fusion.5
  25.0 0.1 lt.30
  25.1 0.3 reduce-window.9
  25.4 0.1 slice.40
  25.5 0.1 slice_reduce_fusion.5
  25.7 0.1 add_bitcast_fusion
  25.7 0.2 fusion.35
  25.9 0.1 copy.20
  26.0 28.5 %all-gather = s32[32,1,6,2]{2,3,1,0:T(2,128)S(1)} all-gather(s32[1,1,6,2]{2,3,1,0:T(2,128)} %param.8), channel_id=2, replica_groups=mesh['grp'=16,'wrk'=32] {'wrk'}, dimensions={0}, use_global_device_ids=true | all-gather | bytes 1584 | tf_op jit(solution)/shard_map/all_gather | solution.py:103
  54.5 0.1 broadcast_in_dim.146
  54.6 0.1 select_reduce_fusion.3
  54.8 0.2 select_reduce_fusion.4
  55.0 0.1 iota_compare_fusion.6
  55.1 0.9 select_reduce_fusion.1
  56.0 0.2 slice_reduce_fusion.2
  56.2 0.0 collective-permute-done.1
  56.2 1.5 pad_maximum_fusion.1
  57.7 0.0 all-gather.3.cloned.1.call-update
  57.7 0.0 reduce-scatter.2.cloned.1.call-start
  57.8 0.1 iota_subtract_fusion
  57.8 0.1 iota_subtract_fusion.1
  57.9 0.1 iota_compare_fusion
  58.0 0.1 iota_compare_fusion.1
  58.1 7.8 %broadcast_and_fusion = pred[3,32,32,32,32]{4,3,2,1,0:T(32,128)(4,1)} fusion(pred[3,32,32]{2,1,0:T(8,128)(4,1)S(1)} %iota_compare_fusion, pred[3,32,32]{2,1,0:T(8,128)(4,1)S(1)} %iota_compare_fusion.1), kind=kLoop, calls=%fused_computation.3 | loop fusion | flops 3145728 | bytes 3151872 | tf_op jit(solution)/shard_map/and | solution.py:39
  65.9 28.0 %and.40 = pred[3,1024,1024]{2,1,0:T(32,128)(4,1)S(1)} reshape(pred[3,32,32,32,32]{4,3,2,1,0:T(32,128)(4,1)} %broadcast_and_fusion) | data formatting | bytes 6291456 | tf_op jit(solution)/shard_map/and | solution.py:39
  93.9 0.1 sine_multiply_fusion
  94.1 8.0 %broadcast_multiply_fusion = f32[32,32,32,32]{3,2,1,0:T(8,128)} fusion(f32[32,32]{1,0:T(8,128)S(1)} %sine_multiply_fusion), kind=kLoop, calls=%fused_computation.4 | loop fusion | flops 1048576 | bytes 4198400 | tf_op jit(solution)/shard_map/mul | solution.py:124
  102.0 13.9 %reshape.464 = f32[1024,1024,1]{1,0,2:T(8,128)} reshape(f32[32,32,32,32]{3,2,1,0:T(8,128)} %broadcast_multiply_fusion) | data formatting | bytes 8388608 | tf_op jit(solution)/shard_map/mul | solution.py:124
  116.0 0.1 broadcast_add_fusion
  116.1 1.0 add.110
  117.1 1.3 add.111
  118.3 0.1 add.112
  118.4 0.5 broadcast_select_fusion.5
  118.9 0.6 add_select_fusion
  119.5 0.5 compare_and_fusion.2
  120.1 0.6 compare_and_fusion.1
  120.7 0.1 iota_subtract_fusion.2
  120.7 0.7 add_divide_fusion
  121.4 2.7 %gather_fusion.1 = bf16[3,32,1024]{2,1,0:T(8,128)(2,1)S(1)} fusion(bf16[64,32,1024]{2,1,0:T(8,128)(2,1)} %bitcast.39, s32[1024]{0:T(1024)S(1)} %pad_clamp_fusion), kind=kCustom, calls=%fused_computation.1.clone | custom fusion | bytes 393228 | tf_op jit(solution)/shard_map/jit(_take)/gather | solution.py:119
  124.1 2.7 %gather_fusion = bf16[3,32,1024]{2,1,0:T(8,128)(2,1)S(1)} fusion(bf16[64,32,1024]{2,1,0:T(8,128)(2,1)} %bitcast.40, s32[1024]{0:T(1024)S(1)} %pad_clamp_fusion.1), kind=kCustom, calls=%fused_computation.clone | custom fusion | bytes 393228 | tf_op jit(solution)/shard_map/jit(_take)/gather | solution.py:118
  126.9 2.8 %fusion.8 = f32[3,32,1024]{2,1,0:T(8,128)S(1)} fusion(pred[3,1024,1024]{2,1,0:T(32,128)(4,1)S(1)} %and.40, bf16[3,32,1024]{2,1,0:T(8,128)(2,1)S(1)} %gather_fusion.1, pred[3]{0:T(512)(128)(4,1)} %get-tuple-element.29), kind=kOutput, calls=%fused_computation.26 | convolution fusion | flops 201424896 | bytes 3735555 | tf_op jit(solution)/shard_map/pxc,pyc->pxy/dot_general | solution.py:46
  129.7 0.4 fusion.12
  130.1 0.6 convolution_bitcast_fusion.1
  130.8 2.6 convolution_multiply_fusion.1
  133.3 0.6 convolution_bitcast_fusion
  133.9 2.6 fusion.36
  136.5 0.5 reduce-precision_convert_fusion.1
  137.1 1.8 fusion
  138.8 0.1 broadcast_select_fusion.1
  139.0 4.4 %collective-permute-start.2 = (f32[3,32,1024]{2,1,0:T(8,128)S(1)}, f32[3,32,1024]{2,1,0:T(8,128)S(1)}, u32[]{:S(2)}, u32[]{:S(2)}) collective-permute-start(f32[3,32,1024]{2,1,0:T(8,128)S(1)} %get-tuple-element.22), channel_id=1, source_target_pairs={{0,32},{32,64},{64,96},{96,128},{128,160},{160,192},{192,224},{224... | collective-permute-start | bytes 1179656 | tf_op jit(solution)/shard_map/ppermute | solution.py:13
  143.4 2.1 collective-permute-start
  145.6 6.1 %collective-permute-done = s32[3]{0:T(128)S(1)} collective-permute-done((s32[3]{0:T(128)S(1)}, s32[3]{0:T(128)S(1)}, u32[]{:S(2)}, u32[]{:S(2)}) %collective-permute-start) | collective-permute-done | bytes 44 | tf_op jit(solution)/shard_map/ppermute | solution.py:13
  151.6 0.1 pad_add_fusion
  151.7 0.1 iota_compare_fusion.8
  151.8 0.0 collective-permute-done.2
  151.8 0.1 pad_maximum_fusion
  151.9 7.4 %select_reduce_fusion = f32[32,32,1024]{2,1,0:T(8,128)} fusion(f32[9,32,1024]{2,1,0:T(8,128)S(1)} %pad_maximum_fusion, pred[9,32]{1,0:T(8,128)(4,1)S(1)} %iota_compare_fusion.8), kind=kLoop, calls=%fused_computation.2 | loop fusion | flops 17825792 | bytes 5374240 | tf_op jit(solution)/shard_map/reduce_sum | solution.py:85
  159.3 0.0 reduce-scatter.2.cloned.1.call-update
  159.3 105.4 %reduce-scatter.2.cloned.1.call-done = f32[1,32,1024]{2,1,0:T(8,128)} async-done(((f32[32,32,1024]{2,1,0:T(8,128)}), f32[1,32,1024]{2,1,0:T(8,128)}) %reduce-scatter.2.cloned.1.call-update) | async-done | bytes 131088 | tf_op jit(solution)/shard_map/reduce_scatter | solution.py:145
  (33 shorter events, 0.2 us)
Async XLA Ops:
  6.5 114.9 %all-gather.3.cloned.1.call-start = ((), (), s32[]{:S(2)}) async-start(), calls=%async_computation.1 | async-start | bytes 4325376 | tf_op jit(solution)/shard_map/all_gather | solution.py:98
  6.5 49.6 %collective-permute-start.1 = (bf16[1,32,1024]{2,1,0:T(8,128)(2,1)}, bf16[1,32,1024]{2,1,0:T(8,128)(2,1)S(1)}, u32[]{:S(2)}, u32[]{:S(2)}) collective-permute-start(bf16[1,32,1024]{2,1,0:T(8,128)(2,1)} %param.6), channel_id=1, source_target_pairs={{32,0},{64,32},{96,64},{128,96},{160,128},{192,160},{224,192},{256... | collective-permute-start | bytes 196616 | tf_op jit(solution)/shard_map/ppermute | solution.py:13
  57.7 207.1 %reduce-scatter.2.cloned.1.call-start = ((), (), s32[]{:S(2)}) async-start(), calls=%async_computation.2 | async-start | bytes 4325376 | tf_op jit(solution)/shard_map/reduce_scatter | solution.py:145
  120.1 1.3 copy-start.5
  126.9 3.2 %copy-start.2 = (pred[3]{0:T(512)(128)(4,1)S(1)}, pred[3]{0:T(512)(128)(4,1)}, u32[]{:S(2)}) copy-start(pred[3]{0:T(512)(128)(4,1)} %get-tuple-element.17) | copy-start | bytes 13
  126.9 3.8 %copy-start = (f32[1024,1024,1]{1,0,2:T(8,128)S(1)}, f32[1024,1024,1]{1,0,2:T(8,128)}, u32[]{:S(2)}) copy-start(f32[1024,1024,1]{1,0,2:T(8,128)} %reshape.464) | copy-start | bytes 12582916
  126.9 3.8 %copy-start.1 = (f32[32,1024]{1,0:T(8,128)S(1)}, f32[32,1024]{1,0:T(8,128)}, u32[]{:S(2)}) copy-start(f32[32,1024]{1,0:T(8,128)} %add_divide_fusion) | copy-start | bytes 393220
  130.8 3.2 %copy-start.3 = (f32[3]{0:T(128)S(1)}, f32[3]{0:T(128)}, u32[]{:S(2)}) copy-start(f32[3]{0:T(128)} %get-tuple-element.28) | copy-start | bytes 40
  136.5 2.3 copy-start.7
  137.0 6.4 %copy-start.8 = (s32[3]{0:T(128)S(1)}, s32[3]{0:T(128)}, u32[]{:S(2)}) copy-start(s32[3]{0:T(128)} %get-tuple-element.26) | copy-start | bytes 40
  137.0 14.6 %copy-start.4 = (s32[3]{0:T(128)S(1)}, s32[3]{0:T(128)}, u32[]{:S(2)}) copy-start(s32[3]{0:T(128)} %get-tuple-element.15) | copy-start | bytes 40
  137.0 14.6 %copy-start.6 = (s32[3]{0:T(128)S(1)}, s32[3]{0:T(128)}, u32[]{:S(2)}) copy-start(s32[3]{0:T(128)} %copy-done.5) | copy-start | bytes 40
  139.0 12.8 %collective-permute-start.2 = (f32[3,32,1024]{2,1,0:T(8,128)S(1)}, f32[3,32,1024]{2,1,0:T(8,128)S(1)}, u32[]{:S(2)}, u32[]{:S(2)}) collective-permute-start(f32[3,32,1024]{2,1,0:T(8,128)S(1)} %get-tuple-element.22), channel_id=1, source_target_pairs={{0,32},{32,64},{64,96},{96,128},{128,160},{160,192},{192,224},{224... | collective-permute-start | bytes 1179656 | tf_op jit(solution)/shard_map/ppermute | solution.py:13
  143.4 8.2 %collective-permute-start = (s32[3]{0:T(128)S(1)}, s32[3]{0:T(128)S(1)}, u32[]{:S(2)}, u32[]{:S(2)}) collective-permute-start(s32[3]{0:T(128)S(1)} %copy-done.8), channel_id=1, source_target_pairs={{0,32},{32,64},{64,96},{96,128},{128,160},{160,192},{192,224},{224... | collective-permute-start | bytes 44 | tf_op jit(solution)/shard_map/ppermute | solution.py:13
Sparse Core Ops, SparseCore 0:
  57.8 61.8 all-gather.2
  159.5 105.2 reduce-scatter.1

commit v2 on v1

--- a/solution.py
+++ b/solution.py
@@ -5,6 +5,7 @@
 
 screen_shift = 0.05
 highest = lax.Precision.HIGHEST
+EXCHANGE = "all_to_all"
 
 
 def passed_along(value, axis, steps):
@@ -28,16 +29,14 @@
 
 def shift_matrices(offset_diff, box_edge):
     cell = jnp.arange(box_edge, dtype=jnp.int32)
-
-    def one_axis(shift):
-        return cell[None, None, :] == (cell[None, :, None] - shift[:, None, None])
-
-    row_shift = one_axis(offset_diff[:, 0])
-    along_y = one_axis(offset_diff[:, 1])
-    along_z = one_axis(offset_diff[:, 2])
-    count = offset_diff.shape[0]
-    plane_shift = (along_y[:, :, None, :, None] & along_z[:, None, :, None, :]).reshape(
-        count, box_edge * box_edge, box_edge * box_edge
+    row_shift = cell[None, None, :] == (cell[None, :, None] - offset_diff[:, 0, None, None])
+    plane = jnp.arange(box_edge * box_edge, dtype=jnp.int32)
+    out_y = (plane // box_edge)[None, :, None]
+    out_z = (plane % box_edge)[None, :, None]
+    in_y = (plane // box_edge)[None, None, :]
+    in_z = (plane % box_edge)[None, None, :]
+    plane_shift = (in_y == out_y - offset_diff[:, 1, None, None]) & (
+        in_z == out_z - offset_diff[:, 2, None, None]
     )
     return row_shift.astype(jnp.float32), plane_shift.astype(jnp.bfloat16)
 
@@ -91,28 +90,18 @@
     orb_dev, box_edge, plane_size = orbitals.shape
     workers = lax.axis_size("wrk")
     group_index = lax.axis_index("grp")
-    worker_index = lax.axis_index("wrk")
     grp_orbs = orb_dev * workers
-    upper_set = passed_along(orbitals, "grp", -1)
-    local_set = jnp.stack([orbitals, upper_set], axis=0)
-    group_set = lax.all_gather(local_set, "wrk", axis=1, tiled=True)
-    group_set = group_set.reshape(2 * grp_orbs, box_edge, plane_size)
+    own_set = lax.all_gather(orbitals, "wrk", axis=0, tiled=True)
+    upper_set = lax.all_gather(passed_along(orbitals, "grp", -1), "wrk", axis=0, tiled=True)
+    group_set = jnp.concatenate([own_set, upper_set], axis=0)
 
-    slot_cap = pair_slots.shape[2]
-    per_worker = (slot_cap + 1) // 2
-    group_slots = lax.all_gather(pair_slots[0, 0], "wrk").reshape(-1, 2)
-    group_count = lax.all_gather(pair_count[0], "wrk").reshape(-1)
-    in_use = (jnp.arange(slot_cap, dtype=jnp.int32)[None, :] < group_count[:, None]).reshape(-1)
-    rank = jnp.cumsum(in_use.astype(jnp.int32)) - 1
-    wanted = worker_index * per_worker + jnp.arange(per_worker, dtype=jnp.int32)
-    match = in_use[None, :] & (rank[None, :] == wanted[:, None])
-    pair_list = jnp.sum(jnp.where(match[:, :, None], group_slots[None, :, :], 0), axis=1)
-    weights = jnp.any(match, axis=1).astype(jnp.float32)
-
+    pair_list = pair_slots[0, 0]
+    slot_cap = pair_list.shape[0]
+    weights = (jnp.arange(slot_cap, dtype=jnp.int32) < pair_count[0, 0]).astype(jnp.float32)
+    left_orb = pair_list[:, 0]
+    right_orb = pair_list[:, 1]
+    offset_diff = corner_of(right_orb, offsets) - corner_of(left_orb, offsets)
     base = group_index * grp_orbs
-    left_orb = jnp.where(weights > 0, pair_list[:, 0], base)
-    right_orb = jnp.where(weights > 0, pair_list[:, 1], base)
-    offset_diff = corner_of(right_orb, offsets) - corner_of(left_orb, offsets)
     left_row = jnp.clip(left_orb - base, 0, 2 * grp_orbs - 1)
     right_row = jnp.clip(right_orb - base, 0, 2 * grp_orbs - 1)
     left_boxes = jnp.take(group_set, left_row, axis=0)
@@ -142,6 +131,9 @@
     fields = jnp.concatenate([to_left, kept_right, got_fields], axis=0)
     rows = jnp.concatenate([left_row, kept_rows, got_rows], axis=0)
     combined = rows_to_orbitals(fields, rows, grp_orbs)
+    if EXCHANGE == "all_to_all":
+        pieces = lax.all_to_all(combined, "wrk", 0, 0, tiled=True)
+        return jnp.sum(pieces, axis=0, keepdims=True)
     return lax.psum_scatter(combined, "wrk", scatter_dimension=0, tiled=True)
 
 

time: 273 us -> 275 us (level)
  local copies, waits for them, and re-layouts: 52.4 us -> 26.8 us
  blocking collectives: 42.9 us -> 57 us
  matrix products: 11.7 us -> 23.2 us
    reduce_scatter x1 -> x0, waiting for transfers between devices: 105 us -> none  [local(): return lax.psum_scatter(combined, 'wrk', scatter_dimension=0, tiled=True)]
    all_gather x1 -> x2, waiting for transfers between devices: 0.01 us -> 95.5 us  [the longest x1 58.3 us: local(): lax.all_gather(passed_along(orbitals, 'grp', -1), 'wrk', axis=0, tiled=True)]
    all_to_all x0 -> x1, blocking collectives: none -> 57 us  [local(): pieces = lax.all_to_all(combined, 'wrk', 0, 0, tiled=True)]
    all_gather x1 -> x0, blocking collectives: 28.5 us -> none  [local(): group_slots = lax.all_gather(pair_slots[0, 0], 'wrk').reshape(-1, 2)]
    and x1 -> x0, local copies, waits for them, and re-layouts: 28 us -> none  [shift_matrices(): along_y[:, :, None, :, None] & along_z[:, None, :, None, :]]
    unnamed x1 -> x0, blocking collectives: 14.5 us -> none
    ppermute x3, waiting for transfers between devices: 6.07 us -> 18.2 us  [passed_along(): lax.ppermute(value, axis, [(source, source + steps) for source in range(i...]
    reduce_sum x1, other arithmetic: 7.42 us -> 18.2 us  [rows_to_orbitals(): jnp.sum(jnp.where(chosen[:, :, None, None], fields[:, None, :, :], 0.0),...]
  transfers between devices with their start and end apart: 5 -> 5, of which waited for: 2 -> 4; matrix products, arithmetic and copies ran while one was open for 25% -> 10% of each run, Pallas kernels for 0% -> 0%
where the time goes in v2:
time: 275 us; the launch traced here: 274 us
  waiting for transfers between devices  114 us (41%)
  blocking collectives  57 us (21%)
  other arithmetic  30.8 us (11%)
  local copies, waits for them, and re-layouts  26.8 us (10%)
  matrix products  23.2 us (8%)
  between operations  14.3 us (5%)
  starting transfers between devices  7.69 us (3%)
    all_gather x1, waiting for transfers between devices, local(): lax.all_gather(passed_along(orbitals, 'grp', -1), 'wrk', axis=0, tiled=True)  58.3 us
    all_to_all x1, blocking collectives, local(): pieces = lax.all_to_all(combined, 'wrk', 0, 0, tiled=True)  57 us
    all_gather x1, waiting for transfers between devices, local(): own_set = lax.all_gather(orbitals, 'wrk', axis=0, tiled=True)  37.2 us
    reduce_sum x1, other arithmetic, rows_to_orbitals(): jnp.sum(jnp.where(chosen[:, :, None, None], fields[:, None, :, :], 0.0),...  18.2 us
    ppermute x3, waiting for transfers between devices, passed_along(): lax.ppermute(value, axis, [(source, source + steps) for source in range(i...  18.2 us
    mul x1, local copies, waits for them, and re-layouts, local(): sine_rows[:, None, :, None] * sine_rows[None, :, None, :]  13.7 us
    mul x1, other arithmetic, local(): sine_rows[:, None, :, None] * sine_rows[None, :, None, :]  8 us
    ppermute x3, starting transfers between devices, passed_along(): lax.ppermute(value, axis, [(source, source + steps) for source in range(i...  7.65 us
  transfers between devices with their start and end apart: 5, of which 4 were waited for; matrix products, arithmetic and copies ran while one was open for 10% of the time, Pallas kernels for 0%

profile of v2, /device:TPU:1, one launch (start us, length us, event | category | flops | bytes accessed | tf_op | source)
XLA Modules:
  0.0 274.2 jit_solution(15588823203964607802)
XLA Ops:
  6.5 0.0 all-gather.3.cloned.1.call-start
  6.5 0.7 all-gather.3.cloned.1.call-update
  7.3 0.0 all-gather.5.cloned.1.call-start
  7.3 1.3 collective-permute-start.1
  8.6 0.1 sine_multiply_fusion
  8.8 4.8 %collective-permute-done.1 = bf16[1,32,1024]{2,1,0:T(8,128)(2,1)S(1)} collective-permute-done((bf16[1,32,1024]{2,1,0:T(8,128)(2,1)}, bf16[1,32,1024]{2,1,0:T(8,128)(2,1)S(1)}, u32[]{:S(2)}, u32[]{:S(2)}) %collective-permute-start.1) | collective-permute-done | bytes 65568 | tf_op jit(solution)/shard_map/ppermute | solution.py:14
  13.5 0.0 copy-start.1
  13.5 0.6 copy-done.1
  14.2 0.0 all-gather.5.cloned.1.call-update
  14.2 8.0 %broadcast_multiply_fusion = f32[32,32,32,32]{3,2,1,0:T(8,128)} fusion(f32[32,32]{1,0:T(8,128)S(1)} %sine_multiply_fusion), kind=kLoop, calls=%fused_computation.14 | loop fusion | flops 1048576 | bytes 4198400 | tf_op jit(solution)/shard_map/mul | solution.py:113
  22.2 0.0 copy-start.3
  22.2 0.0 copy-start.2
  22.2 13.7 %reshape.409 = f32[1024,1024,1]{1,0,2:T(8,128)} reshape(f32[32,32,32,32]{3,2,1,0:T(8,128)} %broadcast_multiply_fusion) | data formatting | bytes 8388608 | tf_op jit(solution)/shard_map/mul | solution.py:113
  35.9 0.1 broadcast_add_fusion
  36.0 0.2 add.123
  36.2 0.2 add.124
  36.5 0.1 add.125
  37.2 0.0 copy-done.3
  37.2 0.1 iota_compare_fusion.3
  37.3 0.0 copy-done.2
  37.3 0.2 select_reduce_fusion.1
  37.6 0.1 iota_subtract_fusion
  37.7 0.1 broadcast_subtract_fusion
  37.8 0.1 broadcast_subtract_fusion.1
  37.9 37.2 %all-gather.3.cloned.1.call-done = bf16[32,32,1024]{2,1,0:T(8,128)(2,1)} async-done(((bf16[1,32,1024]{2,1,0:T(8,128)(2,1)}), bf16[32,32,1024]{2,1,0:T(8,128)(2,1)}) %all-gather.3.cloned.1.call-update) | async-done | bytes 2097168 | tf_op jit(solution)/shard_map/all_gather | solution.py:94
  75.1 3.2 %constant_dynamic-update-slice_fusion.1 = bf16[64,32,1024]{2,1,0:T(8,128)(2,1)} fusion(bf16[32,32,1024]{2,1,0:T(8,128)(2,1)} %all-gather.3.cloned.1.call-done), kind=kLoop, calls=%fused_computation.79 | loop fusion | bytes 4194304
  78.3 58.3 %all-gather.5.cloned.1.call-done = bf16[32,32,1024]{2,1,0:T(8,128)(2,1)} async-done(((bf16[1,32,1024]{2,1,0:T(8,128)(2,1)}), bf16[32,32,1024]{2,1,0:T(8,128)(2,1)}) %all-gather.5.cloned.1.call-update) | async-done | bytes 2097168 | tf_op jit(solution)/shard_map/all_gather | solution.py:95
  136.6 3.2 %constant_dynamic-update-slice_fusion = bf16[64,32,1024]{2,1,0:T(8,128)(2,1)} fusion(bf16[64,32,1024]{2,1,0:T(8,128)(2,1)} %constant_dynamic-update-slice_fusion.1, bf16[32,32,1024]{2,1,0:T(8,128)(2,1)} %all-gather.5.cloned.1.call-done), kind=kLoop, calls=%fused_computation.78 | loop fusion | bytes 4194304 | tf_op jit(solution)/shard_map/concatenate | solution.py:96
  139.8 2.8 %gather_fusion.1 = bf16[6,32,1024]{2,1,0:T(8,128)(2,1)S(1)} fusion(bf16[64,32,1024]{2,1,0:T(8,128)(2,1)} %constant_dynamic-update-slice_fusion, s32[1024]{0:T(1024)S(1)} %pad_clamp_fusion), kind=kCustom, calls=%fused_computation.1.clone | custom fusion | bytes 786456 | tf_op jit(solution)/shard_map/jit(_take)/gather | solution.py:108
  142.5 2.8 %gather_fusion = bf16[6,32,1024]{2,1,0:T(8,128)(2,1)S(1)} fusion(bf16[64,32,1024]{2,1,0:T(8,128)(2,1)} %constant_dynamic-update-slice_fusion, s32[1024]{0:T(1024)S(1)} %pad_clamp_fusion.1), kind=kCustom, calls=%fused_computation.clone | custom fusion | bytes 786456 | tf_op jit(solution)/shard_map/jit(_take)/gather | solution.py:107
  145.3 0.0 copy-start
  145.3 7.0 %fusion.1 = f32[6,32,1024]{2,1,0:T(8,128)S(1)} fusion(s32[6,1024]{1,0:T(8,128)S(1)} %broadcast_subtract_fusion, s32[1024]{0:T(1024)S(1)} %get-tuple-element.30, s32[6,1024]{1,0:T(8,128)S(1)} %broadcast_subtract_fusion.1, s32[1024]{0:T(1024)S(1)} %get-tuple-element.31, bf16[6,32,1024]{2,1,0:T(8,128)(2,1)S(1)} %gather_fusion.1, ...), kind=kOutput, calls=%fused_computation.5 | convolution fusion | flops 421724160 | bytes 1236998 | tf_op jit(solution)/shard_map/pxc,pyc->pxy/dot_general | solution.py:45
  152.3 0.5 fusion.20
  152.8 1.0 convolution_bitcast_fusion.1
  153.8 0.0 copy-done
  153.9 2.9 %convolution_multiply_fusion.1 = f32[6,32,1024]{2,1,0:T(8,128)S(1)} fusion(f32[6,32,1024]{2,1,0:T(8,128)S(1)} %convolution_bitcast_fusion.1, f32[1024,1024,1]{1,0,2:T(8,128)S(1)} %copy-done, f32[32,1024]{1,0:T(8,128)S(1)} %add_divide_fusion), kind=kOutput, calls=%fused_computation.19 | convolution fusion | flops 2416115712 | bytes 5898240 | tf_op jit(solution)/shard_map/dot_general | solution.py:67
  156.8 0.9 convolution_bitcast_fusion
  157.7 2.9 %fusion.48 = (f32[6,32,1024]{2,1,0:T(8,128)S(1)}, f32[6,32,1024]{2,1,0:T(8,128)S(1)}) fusion(f32[6,32,1024]{2,1,0:T(8,128)S(1)} %fusion.20, f32[6]{0:T(128)S(1)} %compare_convert_fusion, f32[6,32,1024]{2,1,0:T(8,128)S(1)} %convolution_bitcast_fusion, f32[1024,1024,1]{1,0,2:T(8,128)S(1)} %copy-done), kind=kOutput, calls=%fused_computation.108 | convolution fusion | flops 2416312320 | bytes 7340056 | tf_op jit(solution)/shard_map/dot_general | solution.py:67
  160.6 0.8 reduce-precision_convert_fusion.1
  161.5 7.1 %fusion = f32[6,96,1024]{2,1,0:T(8,128)S(1)} fusion(s32[6,1024]{1,0:T(8,128)S(1)} %broadcast_subtract_fusion, s32[1024]{0:T(1024)S(1)} %get-tuple-element.30, s32[6,1024]{1,0:T(8,128)S(1)} %broadcast_subtract_fusion.1, s32[1024]{0:T(1024)S(1)} %get-tuple-element.31, bf16[6,32,1024]{2,1,0:T(8,128)(2,1)S(1)} %get-tuple-element.15, ...), kind=kOutput, calls=%fused_computation.4 | convolution fusion | flops 1230372864 | bytes 3596288 | tf_op jit(solution)/shard_map/pxc,pcy->pxy/dot_general | solution.py:56
  168.6 0.3 broadcast_select_fusion.1
  168.8 3.2 %collective-permute-start.2 = (f32[6,32,1024]{2,1,0:T(8,128)S(1)}, f32[6,32,1024]{2,1,0:T(8,128)S(1)}, u32[]{:S(2)}, u32[]{:S(2)}) collective-permute-start(f32[6,32,1024]{2,1,0:T(8,128)S(1)} %get-tuple-element.13), channel_id=1, source_target_pairs={{0,32},{32,64},{64,96},{96,128},{128,160},{160,192},{192,224},{224... | collective-permute-start | bytes 2359304 | tf_op jit(solution)/shard_map/ppermute | solution.py:14
  172.1 3.1 %collective-permute-start = (s32[6]{0:T(128)S(1)}, s32[6]{0:T(128)S(1)}, u32[]{:S(2)}, u32[]{:S(2)}) collective-permute-start(s32[6]{0:T(128)S(1)} %get-tuple-element.22), channel_id=1, source_target_pairs={{0,32},{32,64},{64,96},{96,128},{128,160},{160,192},{192,224},{224... | collective-permute-start | bytes 80 | tf_op jit(solution)/shard_map/ppermute | solution.py:14
  175.2 13.4 %collective-permute-done = s32[6]{0:T(128)S(1)} collective-permute-done((s32[6]{0:T(128)S(1)}, s32[6]{0:T(128)S(1)}, u32[]{:S(2)}, u32[]{:S(2)}) %collective-permute-start) | collective-permute-done | bytes 56 | tf_op jit(solution)/shard_map/ppermute | solution.py:14
  188.7 0.1 pad_add_fusion
  188.7 0.1 iota_compare_fusion.5
  188.8 0.0 collective-permute-done.2
  188.8 0.3 pad_maximum_fusion
  189.1 18.2 %select_reduce_fusion = f32[32,32,1024]{2,1,0:T(8,128)} fusion(f32[18,32,1024]{2,1,0:T(8,128)S(1)} %pad_maximum_fusion, pred[18,32]{1,0:T(8,128)(4,1)S(1)} %iota_compare_fusion.5), kind=kLoop, calls=%fused_computation.2 | loop fusion | flops 36700160 | bytes 6554176 | tf_op jit(solution)/shard_map/reduce_sum | solution.py:84
  207.3 57.0 %all_to_all.5 = f32[32,32,1024]{2,1,0:T(8,128)} all-to-all(f32[32,32,1024]{2,1,0:T(8,128)} %select_reduce_fusion), channel_id=1, replica_groups=mesh['grp'=16,'wrk'=32] {'wrk'}, dimensions={0} | all-to-all | bytes 8388608 | tf_op jit(solution)/shard_map/all_to_all | solution.py:135
  264.3 3.1 %reduce_sum.39 = f32[32,1024]{1,0:T(8,128)} reduce(f32[32,32,1024]{2,1,0:T(8,128)} %all_to_all.5, f32[]{:T(128)} %constant.85.clone.1), dimensions={0}, to_apply=%region_3.5 | reduce | flops 1015808 | bytes 4325380 | tf_op jit(solution)/shard_map/reduce_sum | solution.py:136
  (16 shorter events, 0.2 us)
Async XLA Ops:
  6.5 68.6 %all-gather.3.cloned.1.call-start = ((), (), s32[]{:S(2)}) async-start(), calls=%async_computation.1 | async-start | bytes 2162688 | tf_op jit(solution)/shard_map/all_gather | solution.py:94
  7.3 129.3 %all-gather.5.cloned.1.call-start = ((), (), s32[]{:S(2)}) async-start(), calls=%async_computation.2 | async-start | bytes 2162688 | tf_op jit(solution)/shard_map/all_gather | solution.py:95
  7.3 6.2 %collective-permute-start.1 = (bf16[1,32,1024]{2,1,0:T(8,128)(2,1)}, bf16[1,32,1024]{2,1,0:T(8,128)(2,1)S(1)}, u32[]{:S(2)}, u32[]{:S(2)}) collective-permute-start(bf16[1,32,1024]{2,1,0:T(8,128)(2,1)} %param.6), channel_id=1, source_target_pairs={{32,0},{64,32},{96,64},{128,96},{160,128},{192,160},{224,192},{256... | collective-permute-start | bytes 196616 | tf_op jit(solution)/shard_map/ppermute | solution.py:14
  13.5 0.6 copy-start.1
  22.2 15.0 %copy-start.3 = (s32[1,1,6,2]{2,3,1,0:T(2,128)S(1)}, s32[1,1,6,2]{2,3,1,0:T(2,128)}, u32[]{:S(2)}) copy-start(s32[1,1,6,2]{2,3,1,0:T(2,128)} %param.8) | copy-start | bytes 148
  22.2 15.1 %copy-start.2 = (s32[512,3]{0,1:T(4,128)S(1)}, s32[512,3]{0,1:T(4,128)}, u32[]{:S(2)}) copy-start(s32[512,3]{0,1:T(4,128)} %param.7) | copy-start | bytes 18436
  145.3 8.6 %copy-start = (f32[1024,1024,1]{1,0,2:T(8,128)S(1)}, f32[1024,1024,1]{1,0,2:T(8,128)}, u32[]{:S(2)}) copy-start(f32[1024,1024,1]{1,0,2:T(8,128)} %reshape.409) | copy-start | bytes 12582916
  168.8 20.0 %collective-permute-start.2 = (f32[6,32,1024]{2,1,0:T(8,128)S(1)}, f32[6,32,1024]{2,1,0:T(8,128)S(1)}, u32[]{:S(2)}, u32[]{:S(2)}) collective-permute-start(f32[6,32,1024]{2,1,0:T(8,128)S(1)} %get-tuple-element.13), channel_id=1, source_target_pairs={{0,32},{32,64},{64,96},{96,128},{128,160},{160,192},{192,224},{224... | collective-permute-start | bytes 2359304 | tf_op jit(solution)/shard_map/ppermute | solution.py:14
  172.1 16.6 %collective-permute-start = (s32[6]{0:T(128)S(1)}, s32[6]{0:T(128)S(1)}, u32[]{:S(2)}, u32[]{:S(2)}) collective-permute-start(s32[6]{0:T(128)S(1)} %get-tuple-element.22), channel_id=1, source_target_pairs={{0,32},{32,64},{64,96},{96,128},{128,160},{160,192},{192,224},{224... | collective-permute-start | bytes 80 | tf_op jit(solution)/shard_map/ppermute | solution.py:14
Sparse Core Ops, SparseCore 0:
  10.5 64.5 all-gather.2
  78.2 58.3 all-gather.4

commit v3 on v2

--- a/solution.py
+++ b/solution.py
@@ -80,10 +80,10 @@
 
 
 def rows_to_orbitals(fields, rows, count):
-    chosen = rows[:, None] == jnp.arange(count, dtype=jnp.int32)[None, :]
-    return jnp.sum(
-        jnp.where(chosen[:, :, None, None], fields[:, None, :, :], 0.0), axis=0
-    )
+    chosen = (rows[:, None] == jnp.arange(count, dtype=jnp.int32)[None, :]).astype(jnp.float32)
+    flat = fields.reshape(fields.shape[0], -1)
+    summed = jnp.einsum("po,pf->of", chosen, flat, precision=highest)
+    return summed.reshape((count,) + fields.shape[1:])
 
 
 def local(orbitals, offsets, pair_slots, pair_count):
@@ -91,9 +91,10 @@
     workers = lax.axis_size("wrk")
     group_index = lax.axis_index("grp")
     grp_orbs = orb_dev * workers
-    own_set = lax.all_gather(orbitals, "wrk", axis=0, tiled=True)
-    upper_set = lax.all_gather(passed_along(orbitals, "grp", -1), "wrk", axis=0, tiled=True)
-    group_set = jnp.concatenate([own_set, upper_set], axis=0)
+    upper_set = passed_along(orbitals, "grp", -1)
+    local_set = jnp.stack([orbitals, upper_set], axis=0)
+    group_set = lax.all_gather(local_set, "wrk", axis=1, tiled=True)
+    group_set = group_set.reshape(2 * grp_orbs, box_edge, plane_size)
 
     pair_list = pair_slots[0, 0]
     slot_cap = pair_list.shape[0]
@@ -128,9 +129,9 @@
 
     kept_right = jnp.where(upper[:, None, None], 0.0, to_right)
     kept_rows = jnp.where(upper, 0, right_row)
-    fields = jnp.concatenate([to_left, kept_right, got_fields], axis=0)
-    rows = jnp.concatenate([left_row, kept_rows, got_rows], axis=0)
-    combined = rows_to_orbitals(fields, rows, grp_orbs)
+    fields = jnp.concatenate([to_left, kept_right], axis=0)
+    rows = jnp.concatenate([left_row, kept_rows], axis=0)
+    combined = rows_to_orbitals(fields, rows, grp_orbs) + rows_to_orbitals(got_fields, got_rows, grp_orbs)
     if EXCHANGE == "all_to_all":
         pieces = lax.all_to_all(combined, "wrk", 0, 0, tiled=True)
         return jnp.sum(pieces, axis=0, keepdims=True)

time: 275 us -> 203 us (0.74)
  waiting for transfers between devices: 114 us -> 57.4 us
  other arithmetic: 30.8 us -> 14.6 us
  matrix products: 23.2 us -> 28.1 us
  local copies, waits for them, and re-layouts: 26.8 us -> 22.4 us
    all_gather x2 -> x1, waiting for transfers between devices: 95.5 us -> 39.2 us  [local(): group_set = lax.all_gather(local_set, 'wrk', axis=1, tiled=True)]
    reduce_sum x1 -> x0, other arithmetic: 18.2 us -> none  [rows_to_orbitals(): jnp.sum(jnp.where(chosen[:, :, None, None], fields[:, None, :, :], 0.0),...]
    dot_general x0 -> x2, matrix products: none -> 4.98 us  [rows_to_orbitals(): summed = jnp.einsum('po,pf->of', chosen, flat, precision=highest)]
    unnamed x9 -> x6, local copies, waits for them, and re-layouts: 3.85 us -> 0.01 us
    concatenate x1 -> x0, local copies, waits for them, and re-layouts: 3.19 us -> none  [local(): group_set = jnp.concatenate([own_set, upper_set], axis=0)]
  transfers between devices with their start and end apart: 5 -> 4, of which waited for: 4 -> 3; matrix products, arithmetic and copies ran while one was open for 10% -> 28% of each run, Pallas kernels for 0% -> 0%
where the time goes in v3:
time: 203 us; the launch traced here: 202 us
  waiting for transfers between devices  57.4 us (28%)
  blocking collectives  56.8 us (28%)
  matrix products  28.1 us (14%)
  local copies, waits for them, and re-layouts  22.4 us (11%)
  other arithmetic  14.6 us (7%)
  between operations  14.4 us (7%)
  starting transfers between devices  8.26 us (4%)
    all_to_all x1, blocking collectives, local(): pieces = lax.all_to_all(combined, 'wrk', 0, 0, tiled=True)  56.8 us
    all_gather x1, waiting for transfers between devices, local(): group_set = lax.all_gather(local_set, 'wrk', axis=1, tiled=True)  39.2 us
    ppermute x3, waiting for transfers between devices, passed_along(): lax.ppermute(value, axis, [(source, source + steps) for source in range(i...  18.2 us
    mul x1, local copies, waits for them, and re-layouts, local(): sine_rows[:, None, :, None] * sine_rows[None, :, None, :]  13.8 us
    ppermute x3, starting transfers between devices, passed_along(): lax.ppermute(value, axis, [(source, source + steps) for source in range(i...  8.26 us
    mul x1, other arithmetic, local(): sine_rows[:, None, :, None] * sine_rows[None, :, None, :]  7.99 us
    dot_general x1, matrix products, unmove_f32(): jnp.einsum('pxc,pcy->pxy', parts, plane_shift, preferred_element_type=jnp...  7.1 us
    dot_general x1, matrix products, move_bf16(): jnp.einsum('pxc,pyc->pxy', boxes, plane_shift, preferred_element_type=jnp...  6.99 us
  transfers between devices with their start and end apart: 4, of which 3 were waited for; matrix products, arithmetic and copies ran while one was open for 28% of the time, Pallas kernels for 0%

profile of v3, /device:TPU:1, one launch (start us, length us, event | category | flops | bytes accessed | tf_op | source)
XLA Modules:
  0.0 202.0 jit_solution(2512162057033433406)
XLA Ops:
  6.5 0.0 all-gather.2.cloned.1.call-start
  6.5 1.3 collective-permute-start
  7.8 4.9 %collective-permute-done = bf16[1,32,1024]{2,1,0:T(8,128)(2,1)S(1)} collective-permute-done((bf16[1,32,1024]{2,1,0:T(8,128)(2,1)}, bf16[1,32,1024]{2,1,0:T(8,128)(2,1)S(1)}, u32[]{:S(2)}, u32[]{:S(2)}) %collective-permute-start) | collective-permute-done | bytes 65568 | tf_op jit(solution)/shard_map/ppermute | solution.py:14
  12.7 1.5 pad_maximum_fusion.1
  14.3 0.0 all-gather.2.cloned.1.call-update
  14.3 0.7 add_select_fusion.1
  15.0 3.5 %collective-permute-start.1 = (s32[6]{0:T(128)S(1)}, s32[6]{0:T(128)S(1)}, u32[]{:S(2)}, u32[]{:S(2)}) collective-permute-start(s32[6]{0:T(128)S(1)} %get-tuple-element.8), channel_id=1, source_target_pairs={{0,32},{32,64},{64,96},{96,128},{128,160},{160,192},{192,224},{224... | collective-permute-start | bytes 80 | tf_op jit(solution)/shard_map/ppermute | solution.py:14
  18.5 0.1 sine_multiply_fusion
  18.7 8.0 %broadcast_multiply_fusion = f32[32,32,32,32]{3,2,1,0:T(8,128)} fusion(f32[32,32]{1,0:T(8,128)S(1)} %sine_multiply_fusion), kind=kLoop, calls=%fused_computation.13 | loop fusion | flops 1048576 | bytes 4198400 | tf_op jit(solution)/shard_map/mul | solution.py:114
  26.7 0.0 copy-start.2
  26.7 0.0 copy-start.1
  26.7 13.8 %reshape.405 = f32[1024,1024,1]{1,0,2:T(8,128)} reshape(f32[32,32,32,32]{3,2,1,0:T(8,128)} %broadcast_multiply_fusion) | data formatting | bytes 8388608 | tf_op jit(solution)/shard_map/mul | solution.py:114
  40.4 0.1 multiply_multiply_fusion
  40.5 0.1 broadcast_add_fusion
  40.5 0.2 add.126
  40.7 0.2 add.127
  41.0 0.1 add.128
  41.7 0.0 copy-done.2
  41.7 0.1 iota_compare_fusion.3
  41.8 0.0 copy-done.1
  41.8 0.2 select_reduce_fusion
  42.1 0.1 iota_subtract_fusion
  42.2 0.1 broadcast_subtract_fusion
  42.3 0.1 broadcast_subtract_fusion.1
  42.4 39.2 %all-gather.2.cloned.1.call-done = bf16[2,32,32,1024]{3,2,1,0:T(8,128)(2,1)} async-done(((bf16[2,1,32,1024]{3,2,1,0:T(8,128)(2,1)}), bf16[2,32,32,1024]{3,2,1,0:T(8,128)(2,1)}) %all-gather.2.cloned.1.call-update) | async-done | bytes 4194320 | tf_op jit(solution)/shard_map/all_gather | solution.py:96
  81.6 2.8 %gather_fusion.1 = bf16[6,32,1024]{2,1,0:T(8,128)(2,1)S(1)} fusion(bf16[64,32,1024]{2,1,0:T(8,128)(2,1)} %bitcast.67, s32[1024]{0:T(1024)S(1)} %pad_clamp_fusion), kind=kCustom, calls=%fused_computation.1.clone | custom fusion | bytes 786456 | tf_op jit(solution)/shard_map/jit(_take)/gather | solution.py:109
  84.4 2.8 %gather_fusion = bf16[6,32,1024]{2,1,0:T(8,128)(2,1)S(1)} fusion(bf16[64,32,1024]{2,1,0:T(8,128)(2,1)} %bitcast.68, s32[1024]{0:T(1024)S(1)} %pad_clamp_fusion.1), kind=kCustom, calls=%fused_computation.clone | custom fusion | bytes 786456 | tf_op jit(solution)/shard_map/jit(_take)/gather | solution.py:108
  87.2 0.0 copy-start
  87.2 7.0 %fusion.1 = f32[6,32,1024]{2,1,0:T(8,128)S(1)} fusion(s32[6,1024]{1,0:T(8,128)S(1)} %broadcast_subtract_fusion, s32[1024]{0:T(1024)S(1)} %get-tuple-element.30, s32[6,1024]{1,0:T(8,128)S(1)} %broadcast_subtract_fusion.1, s32[1024]{0:T(1024)S(1)} %get-tuple-element.31, bf16[6,32,1024]{2,1,0:T(8,128)(2,1)S(1)} %gather_fusion.1, ...), kind=kOutput, calls=%fused_computation.4 | convolution fusion | flops 421724160 | bytes 1236998 | tf_op jit(solution)/shard_map/pxc,pyc->pxy/dot_general | solution.py:45
  94.2 0.5 fusion.22
  94.7 1.0 convolution_bitcast_fusion.1
  95.7 0.0 copy-done
  95.7 2.9 %convolution_multiply_fusion.1 = f32[6,32,1024]{2,1,0:T(8,128)S(1)} fusion(f32[6,32,1024]{2,1,0:T(8,128)S(1)} %convolution_bitcast_fusion.1, f32[1024,1024,1]{1,0,2:T(8,128)S(1)} %copy-done, f32[32,1024]{1,0:T(8,128)S(1)} %add_divide_fusion), kind=kOutput, calls=%fused_computation.22 | convolution fusion | flops 2416115712 | bytes 5898240 | tf_op jit(solution)/shard_map/dot_general | solution.py:67
  98.6 0.9 convolution_bitcast_fusion
  99.6 2.9 %fusion.56 = (f32[6,32,1024]{2,1,0:T(8,128)S(1)}, f32[6,32,1024]{2,1,0:T(8,128)S(1)}) fusion(f32[6,32,1024]{2,1,0:T(8,128)S(1)} %fusion.22, f32[6]{0:T(128)S(1)} %compare_convert_fusion, f32[6,32,1024]{2,1,0:T(8,128)S(1)} %convolution_bitcast_fusion, f32[1024,1024,1]{1,0,2:T(8,128)S(1)} %copy-done), kind=kOutput, calls=%fused_computation.115 | convolution fusion | flops 2416312320 | bytes 7340056 | tf_op jit(solution)/shard_map/dot_general | solution.py:67
  102.5 0.8 reduce-precision_convert_fusion.1
  103.3 7.1 %fusion = f32[6,96,1024]{2,1,0:T(8,128)S(1)} fusion(s32[6,1024]{1,0:T(8,128)S(1)} %broadcast_subtract_fusion, s32[1024]{0:T(1024)S(1)} %get-tuple-element.30, s32[6,1024]{1,0:T(8,128)S(1)} %broadcast_subtract_fusion.1, s32[1024]{0:T(1024)S(1)} %get-tuple-element.31, bf16[6,32,1024]{2,1,0:T(8,128)(2,1)S(1)} %get-tuple-element.15, ...), kind=kOutput, calls=%fused_computation.3 | convolution fusion | flops 1230372864 | bytes 3596288 | tf_op jit(solution)/shard_map/pxc,pcy->pxy/dot_general | solution.py:56
  110.4 0.3 broadcast_select_fusion
  110.7 3.4 %collective-permute-start.2 = (f32[6,32,1024]{2,1,0:T(8,128)S(1)}, f32[6,32,1024]{2,1,0:T(8,128)S(1)}, u32[]{:S(2)}, u32[]{:S(2)}) collective-permute-start(f32[6,32,1024]{2,1,0:T(8,128)S(1)} %get-tuple-element.12), channel_id=1, source_target_pairs={{0,32},{32,64},{64,96},{96,128},{128,160},{160,192},{192,224},{224... | collective-permute-start | bytes 2359304 | tf_op jit(solution)/shard_map/ppermute | solution.py:14
  114.1 0.1 pad_add_fusion
  114.2 0.1 pad_maximum_fusion
  114.3 0.2 slice_bitcast_fusion
  114.5 2.7 %fusion.10 = f32[32,32,1024]{2,0,1:T(8,128)S(1)} fusion(f32[32,1024,12]{1,0,2:T(8,128)S(1)} %slice_bitcast_fusion, s32[12]{0:T(128)S(1)} %pad_add_fusion), kind=kOutput, calls=%fused_computation.15 | convolution fusion | flops 150995328 | bytes 5767216 | tf_op jit(solution)/shard_map/po,pf->of/dot_general | solution.py:85
  117.2 0.0 collective-permute-done.1
  117.2 13.2 %collective-permute-done.2 = f32[6,32,1024]{2,1,0:T(8,128)S(1)} collective-permute-done((f32[6,32,1024]{2,1,0:T(8,128)S(1)}, f32[6,32,1024]{2,1,0:T(8,128)S(1)}, u32[]{:S(2)}, u32[]{:S(2)}) %collective-permute-start.2) | collective-permute-done | bytes 786464 | tf_op jit(solution)/shard_map/ppermute | solution.py:14
  130.5 2.3 %convolution_add_fusion = f32[32,32,1024]{2,0,1:T(8,128)S(1)} fusion(f32[32,32,1024]{2,0,1:T(8,128)S(1)} %fusion.10, s32[6]{0:T(128)S(1)} %collective-permute-done.1, f32[1,6,32,1024]{3,2,1,0:T(8,128)S(1)} %bitcast.66), kind=kOutput, calls=%fused_computation.14 | convolution fusion | flops 76546240 | bytes 9175064 | tf_op jit(solution)/shard_map/po,pf->of/dot_general | solution.py:85
  132.8 2.4 %copy.16 = f32[32,32,1024]{2,1,0:T(8,128)S(1)} copy(f32[32,32,1024]{2,0,1:T(8,128)S(1)} %convolution_add_fusion) | data formatting | bytes 8388608 | tf_op jit(solution)/shard_map/add | solution.py:134
  135.2 56.8 %all_to_all.5 = f32[32,32,1024]{2,1,0:T(8,128)} all-to-all(f32[32,32,1024]{2,1,0:T(8,128)S(1)} %copy.16), channel_id=1, replica_groups=mesh['grp'=16,'wrk'=32] {'wrk'}, dimensions={0} | all-to-all | bytes 8388608 | tf_op jit(solution)/shard_map/all_to_all | solution.py:136
  192.0 3.1 %reduce_sum.29 = f32[32,1024]{1,0:T(8,128)} reduce(f32[32,32,1024]{2,1,0:T(8,128)} %all_to_all.5, f32[]{:T(128)} %constant.84.clone.1), dimensions={0}, to_apply=%region_2.4 | reduce | flops 1015808 | bytes 4325380 | tf_op jit(solution)/shard_map/reduce_sum | solution.py:137
  (14 shorter events, 0.1 us)
Async XLA Ops:
  6.5 75.1 %all-gather.2.cloned.1.call-start = ((), (), s32[]{:S(2)}) async-start(), calls=%async_computation.1 | async-start | bytes 4325376 | tf_op jit(solution)/shard_map/all_gather | solution.py:96
  6.5 6.2 %collective-permute-start = (bf16[1,32,1024]{2,1,0:T(8,128)(2,1)}, bf16[1,32,1024]{2,1,0:T(8,128)(2,1)S(1)}, u32[]{:S(2)}, u32[]{:S(2)}) collective-permute-start(bf16[1,32,1024]{2,1,0:T(8,128)(2,1)} %param.6), channel_id=1, source_target_pairs={{32,0},{64,32},{96,64},{128,96},{160,128},{192,160},{224,192},{256... | collective-permute-start | bytes 196616 | tf_op jit(solution)/shard_map/ppermute | solution.py:14
  15.0 102.2 %collective-permute-start.1 = (s32[6]{0:T(128)S(1)}, s32[6]{0:T(128)S(1)}, u32[]{:S(2)}, u32[]{:S(2)}) collective-permute-start(s32[6]{0:T(128)S(1)} %get-tuple-element.8), channel_id=1, source_target_pairs={{0,32},{32,64},{64,96},{96,128},{128,160},{160,192},{192,224},{224... | collective-permute-start | bytes 80 | tf_op jit(solution)/shard_map/ppermute | solution.py:14
  26.7 15.1 %copy-start.2 = (s32[1,1,6,2]{2,3,1,0:T(2,128)S(1)}, s32[1,1,6,2]{2,3,1,0:T(2,128)}, u32[]{:S(2)}) copy-start(s32[1,1,6,2]{2,3,1,0:T(2,128)} %param.8) | copy-start | bytes 148
  26.7 15.2 %copy-start.1 = (s32[512,3]{0,1:T(4,128)S(1)}, s32[512,3]{0,1:T(4,128)}, u32[]{:S(2)}) copy-start(s32[512,3]{0,1:T(4,128)} %param.7) | copy-start | bytes 18436
  87.2 8.6 %copy-start = (f32[1024,1024,1]{1,0,2:T(8,128)S(1)}, f32[1024,1024,1]{1,0,2:T(8,128)}, u32[]{:S(2)}) copy-start(f32[1024,1024,1]{1,0,2:T(8,128)} %reshape.405) | copy-start | bytes 12582916
  110.7 19.8 %collective-permute-start.2 = (f32[6,32,1024]{2,1,0:T(8,128)S(1)}, f32[6,32,1024]{2,1,0:T(8,128)S(1)}, u32[]{:S(2)}, u32[]{:S(2)}) collective-permute-start(f32[6,32,1024]{2,1,0:T(8,128)S(1)} %get-tuple-element.12), channel_id=1, source_target_pairs={{0,32},{32,64},{64,96},{96,128},{128,160},{160,192},{192,224},{224... | collective-permute-start | bytes 2359304 | tf_op jit(solution)/shard_map/ppermute | solution.py:14
Sparse Core Ops, SparseCore 0:
  14.4 67.1 all-gather.1

commit v4 on v3

--- a/solution.py
+++ b/solution.py
@@ -86,27 +86,51 @@
     return summed.reshape((count,) + fields.shape[1:])
 
 
+def table_lanes(pair_slots, pair_count, box_edge, lanes):
+    values = jnp.concatenate([pair_slots[0, 0].reshape(-1), pair_count[0, 0].reshape(1)])
+    digits = jnp.concatenate([values // box_edge, values % box_edge]).astype(jnp.bfloat16)
+    row = jnp.zeros((lanes,), jnp.bfloat16).at[: digits.shape[0]].set(digits)
+    first = (jnp.arange(box_edge, dtype=jnp.int32) == 0)[:, None]
+    return jnp.where(first, row[None, :], jnp.zeros((), jnp.bfloat16))[None]
+
+
 def local(orbitals, offsets, pair_slots, pair_count):
     orb_dev, box_edge, plane_size = orbitals.shape
     workers = lax.axis_size("wrk")
     group_index = lax.axis_index("grp")
+    worker_index = lax.axis_index("wrk")
     grp_orbs = orb_dev * workers
+    lanes = 128
+    slot_cap = pair_slots.shape[2]
+    table = table_lanes(pair_slots, pair_count, box_edge, lanes)
     upper_set = passed_along(orbitals, "grp", -1)
-    local_set = jnp.stack([orbitals, upper_set], axis=0)
-    group_set = lax.all_gather(local_set, "wrk", axis=1, tiled=True)
-    group_set = group_set.reshape(2 * grp_orbs, box_edge, plane_size)
+    own_part = jnp.concatenate([orbitals, table], axis=-1)
+    upper_part = jnp.concatenate([upper_set, jnp.zeros_like(table)], axis=-1)
+    local_set = jnp.stack([own_part, upper_part], axis=0)
+    gathered = lax.all_gather(local_set, "wrk", axis=1, tiled=True)
+    group_set = gathered.reshape(2 * grp_orbs, box_edge, plane_size + lanes)
 
-    pair_list = pair_slots[0, 0]
-    slot_cap = pair_list.shape[0]
-    weights = (jnp.arange(slot_cap, dtype=jnp.int32) < pair_count[0, 0]).astype(jnp.float32)
-    left_orb = pair_list[:, 0]
-    right_orb = pair_list[:, 1]
+    entries = 2 * slot_cap + 1
+    digits = gathered[0, :, 0, plane_size : plane_size + 2 * entries].astype(jnp.int32)
+    values = digits[:, :entries] * box_edge + digits[:, entries:]
+    group_slots = values[:, : 2 * slot_cap].reshape(-1, 2)
+    group_count = values[:, 2 * slot_cap]
+    per_worker = (slot_cap + 1) // 2
+    in_use = (jnp.arange(slot_cap, dtype=jnp.int32)[None, :] < group_count[:, None]).reshape(-1)
+    rank = jnp.cumsum(in_use.astype(jnp.int32)) - 1
+    wanted = worker_index * per_worker + jnp.arange(per_worker, dtype=jnp.int32)
+    match = in_use[None, :] & (rank[None, :] == wanted[:, None])
+    pair_list = jnp.sum(jnp.where(match[:, :, None], group_slots[None, :, :], 0), axis=1)
+    weights = jnp.any(match, axis=1).astype(jnp.float32)
+
+    base = group_index * grp_orbs
+    left_orb = jnp.where(weights > 0, pair_list[:, 0], base)
+    right_orb = jnp.where(weights > 0, pair_list[:, 1], base)
     offset_diff = corner_of(right_orb, offsets) - corner_of(left_orb, offsets)
-    base = group_index * grp_orbs
     left_row = jnp.clip(left_orb - base, 0, 2 * grp_orbs - 1)
     right_row = jnp.clip(right_orb - base, 0, 2 * grp_orbs - 1)
-    left_boxes = jnp.take(group_set, left_row, axis=0)
-    right_boxes = jnp.take(group_set, right_row, axis=0)
+    left_boxes = jnp.take(group_set, left_row, axis=0)[:, :, :plane_size]
+    right_boxes = jnp.take(group_set, right_row, axis=0)[:, :, :plane_size]
     row_shift, plane_shift = shift_matrices(offset_diff, box_edge)
     right_field = move_bf16(right_boxes, row_shift, plane_shift)
 

time: 203 us -> 191 us (0.941)
  matrix products: 28.1 us -> 17.6 us
  waiting for transfers between devices: 57.4 us -> 53.5 us
    ppermute x3, waiting for transfers between devices: 18.2 us -> 7.99 us  [passed_along(): lax.ppermute(value, axis, [(source, source + steps) for source in range(i...]
    all_gather x1, waiting for transfers between devices: 39.2 us -> 45.5 us  [local(): gathered = lax.all_gather(local_set, 'wrk', axis=1, tiled=True)]
    dot_general x1, matrix products: 7.1 us -> 3.05 us  [unmove_f32(): jnp.einsum('pxc,pcy->pxy', parts, plane_shift, preferred_element_type=jnp...]
    dot_general x1, matrix products: 6.99 us -> 3.05 us  [move_bf16(): jnp.einsum('pxc,pyc->pxy', boxes, plane_shift, preferred_element_type=jnp...]
  transfers between devices with their start and end apart: 4 -> 4, of which waited for: 3 -> 3; matrix products, arithmetic and copies ran while one was open for 28% -> 16% of each run, Pallas kernels for 0% -> 0%
where the time goes in v4:
time: 191 us
  blocking collectives  57 us (30%)
  waiting for transfers between devices  53.5 us (28%)
  local copies, waits for them, and re-layouts  24.3 us (13%)
  matrix products  17.6 us (9%)
  other arithmetic  16 us (8%)
  between operations  14.3 us (7%)
  starting transfers between devices  7.88 us (4%)
    all_to_all x1, blocking collectives, local(): pieces = lax.all_to_all(combined, 'wrk', 0, 0, tiled=True)  57 us
    all_gather x1, waiting for transfers between devices, local(): gathered = lax.all_gather(local_set, 'wrk', axis=1, tiled=True)  45.5 us
    mul x1, local copies, waits for them, and re-layouts, local(): sine_rows[:, None, :, None] * sine_rows[None, :, None, :]  13.7 us
    ppermute x3, waiting for transfers between devices, passed_along(): lax.ppermute(value, axis, [(source, source + steps) for source in range(i...  7.99 us
    mul x1, other arithmetic, local(): sine_rows[:, None, :, None] * sine_rows[None, :, None, :]  7.97 us
    ppermute x3, starting transfers between devices, passed_along(): lax.ppermute(value, axis, [(source, source + steps) for source in range(i...  7.88 us
    dot_general x2, matrix products, apply_sines(): jnp.dot(flat_rows, plane_sines, precision=highest, preferred_element_type...  5.12 us
    dot_general x2, matrix products, rows_to_orbitals(): summed = jnp.einsum('po,pf->of', chosen, flat, precision=highest)  4.29 us
  transfers between devices with their start and end apart: 4, of which 3 were waited for; matrix products, arithmetic and copies ran while one was open for 16% of the time, Pallas kernels for 0%

profile of v4, /device:TPU:1, one launch (start us, length us, event | category | flops | bytes accessed | tf_op | source)
XLA Modules:
  0.0 190.5 jit_solution(9204740548761839012)
XLA Ops:
  6.5 0.0 all-gather.2.cloned.1.call-start
  6.5 1.3 collective-permute-start
  8.5 0.8 copy.21
  9.3 0.1 reshape_squeeze.6
  9.3 0.1 fusion.49
  9.4 0.1 fusion.47
  9.5 0.1 broadcast_select_fusion.2
  9.6 0.8 maximum_bitcast_fusion.1
  10.4 2.3 %collective-permute-done = bf16[1,32,1024]{2,1,0:T(8,128)(2,1)S(1)} collective-permute-done((bf16[1,32,1024]{2,1,0:T(8,128)(2,1)}, bf16[1,32,1024]{2,1,0:T(8,128)(2,1)S(1)}, u32[]{:S(2)}, u32[]{:S(2)}) %collective-permute-start) | collective-permute-done | bytes 65568 | tf_op jit(solution)/shard_map/ppermute | solution.py:14
  12.8 0.7 pad_maximum_fusion
  13.4 0.0 all-gather.2.cloned.1.call-update
  13.5 0.1 sine_multiply_fusion
  13.6 8.0 %broadcast_multiply_fusion = f32[32,32,32,32]{3,2,1,0:T(8,128)} fusion(f32[32,32]{1,0:T(8,128)S(1)} %sine_multiply_fusion), kind=kLoop, calls=%fused_computation.5 | loop fusion | flops 1048576 | bytes 4198400 | tf_op jit(solution)/shard_map/mul | solution.py:138
  21.6 13.7 %reshape.583 = f32[1024,1024,1]{1,0,2:T(8,128)} reshape(f32[32,32,32,32]{3,2,1,0:T(8,128)} %broadcast_multiply_fusion) | data formatting | bytes 8388608 | tf_op jit(solution)/shard_map/mul | solution.py:138
  35.3 0.1 broadcast_add_fusion
  35.4 0.2 add.157
  35.6 0.2 add.158
  35.9 0.1 add.159
  36.0 45.5 %all-gather.2.cloned.1.call-done = bf16[2,32,32,1152]{3,2,1,0:T(8,128)(2,1)} async-done(((bf16[2,1,32,1152]{3,2,1,0:T(8,128)(2,1)}), bf16[2,32,32,1152]{3,2,1,0:T(8,128)(2,1)}) %all-gather.2.cloned.1.call-update) | async-done | bytes 4718608 | tf_op jit(solution)/shard_map/all_gather | solution.py:110
  81.5 0.9 slice_convert_fusion
  82.3 0.1 slice_add_fusion.2
  82.4 0.2 slice_reduce_fusion
  82.6 0.1 iota_compare_fusion.3
  82.7 0.1 lt.47
  82.8 0.3 reduce-window.9
  83.1 0.1 slice.76
  83.2 0.1 slice_reduce_fusion.6
  83.4 0.1 add_bitcast_fusion
  83.4 0.2 fusion.59
  83.6 0.1 copy.23
  83.7 0.1 broadcast_in_dim.155
  83.8 0.1 copy.22
  83.9 0.2 select_reduce_fusion.2
  84.1 0.2 select_reduce_fusion.3
  84.4 0.1 pad_add_fusion.1
  84.5 0.1 iota_compare_fusion.4
  84.5 0.0 copy-done.1
  84.5 0.2 select_reduce_fusion
  84.7 0.2 slice_reduce_fusion.3
  84.9 0.1 iota_subtract_fusion
  85.0 2.9 %gather_fusion.1 = bf16[3,32,1152]{2,1,0:T(8,128)(2,1)S(1)} fusion(bf16[64,32,1152]{2,1,0:T(8,128)(2,1)} %bitcast.59, s32[1024]{0:T(1024)S(1)} %pad_clamp_fusion), kind=kCustom, calls=%fused_computation.1.clone | custom fusion | bytes 442380 | tf_op jit(solution)/shard_map/jit(_take)/gather | solution.py:133
  87.9 2.9 %gather_fusion = bf16[3,32,1152]{2,1,0:T(8,128)(2,1)S(1)} fusion(bf16[64,32,1152]{2,1,0:T(8,128)(2,1)} %bitcast.60, s32[1024]{0:T(1024)S(1)} %pad_clamp_fusion.1), kind=kCustom, calls=%fused_computation.clone | custom fusion | bytes 442380 | tf_op jit(solution)/shard_map/jit(_take)/gather | solution.py:132
  90.9 0.1 broadcast_subtract_fusion
  90.9 0.1 broadcast_subtract_fusion.1
  91.0 3.1 %fusion.1 = f32[3,32,1024]{2,1,0:T(8,128)S(1)} fusion(s32[3,1024]{1,0:T(4,128)S(1)} %broadcast_subtract_fusion, s32[1024]{0:T(1024)S(1)} %get-tuple-element.49, s32[3,1024]{1,0:T(4,128)S(1)} %broadcast_subtract_fusion.1, s32[1024]{0:T(1024)S(1)} %get-tuple-element.50, bf16[3,32,1152]{2,1,0:T(8,128)(2,1)S(1)} %gather_fusion.1, ...), kind=kOutput, calls=%fused_computation.4 | convolution fusion | flops 210862080 | bytes 631296 | tf_op jit(solution)/shard_map/pxc,pyc->pxy/dot_general | solution.py:45
  94.1 0.4 fusion.19
  94.5 0.6 convolution_bitcast_fusion.1
  95.1 0.0 copy-done
  95.1 2.6 %convolution_multiply_fusion.1 = f32[3,32,1024]{2,1,0:T(8,128)S(1)} fusion(f32[3,32,1024]{2,1,0:T(8,128)S(1)} %convolution_bitcast_fusion.1, f32[1024,1024,1]{1,0,2:T(8,128)S(1)} %copy-done, f32[32,1024]{1,0:T(8,128)S(1)} %add_divide_fusion), kind=kOutput, calls=%fused_computation.18 | convolution fusion | flops 1208057856 | bytes 5111808 | tf_op jit(solution)/shard_map/dot_general | solution.py:67
  97.7 0.6 convolution_bitcast_fusion
  98.3 2.6 %fusion.60 = (f32[3,32,1024]{2,1,0:T(8,128)S(1)}, f32[3,32,1024]{2,1,0:T(8,128)S(1)}) fusion(f32[3,32,1024]{2,1,0:T(8,128)S(1)} %fusion.19, f32[3]{0:T(128)S(1)} %get-tuple-element.42, f32[3,32,1024]{2,1,0:T(8,128)S(1)} %convolution_bitcast_fusion, f32[1024,1024,1]{1,0,2:T(8,128)S(1)} %copy-done), kind=kOutput, calls=%fused_computation.145 | convolution fusion | flops 1208156160 | bytes 5767180 | tf_op jit(solution)/shard_map/dot_general | solution.py:67
  100.8 0.5 reduce-precision_convert_fusion.1
  101.3 3.4 %collective-permute-start.1 = (s32[3]{0:T(128)S(1)}, s32[3]{0:T(128)S(1)}, u32[]{:S(2)}, u32[]{:S(2)}) collective-permute-start(s32[3]{0:T(128)S(1)} %get-tuple-element.27), channel_id=1, source_target_pairs={{0,32},{32,64},{64,96},{96,128},{128,160},{160,192},{192,224},{224... | collective-permute-start | bytes 44 | tf_op jit(solution)/shard_map/ppermute | solution.py:14
  104.7 3.0 %fusion = f32[3,96,1024]{2,1,0:T(8,128)S(1)} fusion(s32[3,1024]{1,0:T(4,128)S(1)} %broadcast_subtract_fusion, s32[1024]{0:T(1024)S(1)} %get-tuple-element.49, s32[3,1024]{1,0:T(4,128)S(1)} %broadcast_subtract_fusion.1, s32[1024]{0:T(1024)S(1)} %get-tuple-element.50, bf16[3,32,1024]{2,1,0:T(8,128)(2,1)S(1)} %get-tuple-element.38, ...), kind=kOutput, calls=%fused_computation.3 | convolution fusion | flops 615186432 | bytes 1802240 | tf_op jit(solution)/shard_map/pxc,pcy->pxy/dot_general | solution.py:56
  107.8 0.1 broadcast_select_fusion
  107.9 3.2 %collective-permute-start.2 = (f32[3,32,1024]{2,1,0:T(8,128)S(1)}, f32[3,32,1024]{2,1,0:T(8,128)S(1)}, u32[]{:S(2)}, u32[]{:S(2)}) collective-permute-start(f32[3,32,1024]{2,1,0:T(8,128)S(1)} %get-tuple-element.35), channel_id=1, source_target_pairs={{0,32},{32,64},{64,96},{96,128},{128,160},{160,192},{192,224},{224... | collective-permute-start | bytes 1179656 | tf_op jit(solution)/shard_map/ppermute | solution.py:14
  111.1 0.1 maximum_bitcast_fusion
  111.2 2.1 %fusion.40 = f32[32,32,1024]{2,0,1:T(8,128)S(1)} fusion(s32[6]{0:T(128)S(1)} %pad_add_fusion.1, f32[1,6,32,1024]{3,2,1,0:T(8,128)S(1)} %maximum_bitcast_fusion), kind=kOutput, calls=%fused_computation.89 | convolution fusion | flops 75497664 | bytes 4980760 | tf_op jit(solution)/shard_map/po,pf->of/dot_general | solution.py:85
  113.3 0.0 collective-permute-done.1
  113.4 5.7 %collective-permute-done.2 = f32[3,32,1024]{2,1,0:T(8,128)S(1)} collective-permute-done((f32[3,32,1024]{2,1,0:T(8,128)S(1)}, f32[3,32,1024]{2,1,0:T(8,128)S(1)}, u32[]{:S(2)}, u32[]{:S(2)}) %collective-permute-start.2) | collective-permute-done | bytes 393248 | tf_op jit(solution)/shard_map/ppermute | solution.py:14
  119.0 2.2 %convolution_add_fusion = f32[32,32,1024]{2,0,1:T(8,128)S(1)} fusion(f32[32,32,1024]{2,0,1:T(8,128)S(1)} %fusion.40, s32[3]{0:T(128)S(1)} %collective-permute-done.1, f32[1,3,32,1024]{3,2,1,0:T(8,128)S(1)} %bitcast.56), kind=kOutput, calls=%fused_computation.14 | convolution fusion | flops 38797408 | bytes 8781836 | tf_op jit(solution)/shard_map/po,pf->of/dot_general | solution.py:85
  121.2 2.4 %copy.26 = f32[32,32,1024]{2,1,0:T(8,128)S(1)} copy(f32[32,32,1024]{2,0,1:T(8,128)S(1)} %convolution_add_fusion) | data formatting | bytes 8388608 | tf_op jit(solution)/shard_map/add | solution.py:158
  123.6 57.0 %all_to_all.5 = f32[32,32,1024]{2,1,0:T(8,128)} all-to-all(f32[32,32,1024]{2,1,0:T(8,128)S(1)} %copy.26), channel_id=1, replica_groups=mesh['grp'=16,'wrk'=32] {'wrk'}, dimensions={0} | all-to-all | bytes 8388608 | tf_op jit(solution)/shard_map/all_to_all | solution.py:160
  180.6 3.1 %reduce_sum.39 = f32[32,1024]{1,0:T(8,128)} reduce(f32[32,32,1024]{2,1,0:T(8,128)} %all_to_all.5, f32[]{:T(128)} %constant.138.clone.1), dimensions={0}, to_apply=%region_6.8 | reduce | flops 1015808 | bytes 4325380 | tf_op jit(solution)/shard_map/reduce_sum | solution.py:161
  (23 shorter events, 0.2 us)
Async XLA Ops:
  6.5 75.0 %all-gather.2.cloned.1.call-start = ((), (), s32[]{:S(2)}) async-start(), calls=%async_computation.1 | async-start | bytes 4866048 | tf_op jit(solution)/shard_map/all_gather | solution.py:110
  6.5 6.2 %collective-permute-start = (bf16[1,32,1024]{2,1,0:T(8,128)(2,1)}, bf16[1,32,1024]{2,1,0:T(8,128)(2,1)S(1)}, u32[]{:S(2)}, u32[]{:S(2)}) collective-permute-start(bf16[1,32,1024]{2,1,0:T(8,128)(2,1)} %param.8), channel_id=1, source_target_pairs={{32,0},{64,32},{96,64},{128,96},{160,128},{192,160},{224,192},{256... | collective-permute-start | bytes 196616 | tf_op jit(solution)/shard_map/ppermute | solution.py:14
  21.6 63.0 %copy-start.1 = (s32[512,3]{0,1:T(4,128)S(1)}, s32[512,3]{0,1:T(4,128)}, u32[]{:S(2)}) copy-start(s32[512,3]{0,1:T(4,128)} %param.9) | copy-start | bytes 18436
  91.0 4.1 %copy-start = (f32[1024,1024,1]{1,0,2:T(8,128)S(1)}, f32[1024,1024,1]{1,0,2:T(8,128)}, u32[]{:S(2)}) copy-start(f32[1024,1024,1]{1,0,2:T(8,128)} %reshape.583) | copy-start | bytes 12582916
  101.3 12.0 %collective-permute-start.1 = (s32[3]{0:T(128)S(1)}, s32[3]{0:T(128)S(1)}, u32[]{:S(2)}, u32[]{:S(2)}) collective-permute-start(s32[3]{0:T(128)S(1)} %get-tuple-element.27), channel_id=1, source_target_pairs={{0,32},{32,64},{64,96},{96,128},{128,160},{160,192},{192,224},{224... | collective-permute-start | bytes 44 | tf_op jit(solution)/shard_map/ppermute | solution.py:14
  107.9 11.1 %collective-permute-start.2 = (f32[3,32,1024]{2,1,0:T(8,128)S(1)}, f32[3,32,1024]{2,1,0:T(8,128)S(1)}, u32[]{:S(2)}, u32[]{:S(2)}) collective-permute-start(f32[3,32,1024]{2,1,0:T(8,128)S(1)} %get-tuple-element.35), channel_id=1, source_target_pairs={{0,32},{32,64},{64,96},{96,128},{128,160},{160,192},{192,224},{224... | collective-permute-start | bytes 1179656 | tf_op jit(solution)/shard_map/ppermute | solution.py:14
Sparse Core Ops, SparseCore 0:
  13.6 67.8 all-gather.1

commit v5 on v4

--- a/solution.py
+++ b/solution.py
@@ -5,7 +5,7 @@
 
 screen_shift = 0.05
 highest = lax.Precision.HIGHEST
-EXCHANGE = "all_to_all"
+WORKER_AXES = ("yx", "core")
 
 
 def passed_along(value, axis, steps):
@@ -96,9 +96,10 @@
 
 def local(orbitals, offsets, pair_slots, pair_count):
     orb_dev, box_edge, plane_size = orbitals.shape
-    workers = lax.axis_size("wrk")
+    workers = lax.axis_size("yx") * lax.axis_size("core")
     group_index = lax.axis_index("grp")
-    worker_index = lax.axis_index("wrk")
+    core = lax.axis_index("core")
+    worker_index = lax.axis_index("yx") * lax.axis_size("core") + core
     grp_orbs = orb_dev * workers
     lanes = 128
     slot_cap = pair_slots.shape[2]
@@ -107,7 +108,7 @@
     own_part = jnp.concatenate([orbitals, table], axis=-1)
     upper_part = jnp.concatenate([upper_set, jnp.zeros_like(table)], axis=-1)
     local_set = jnp.stack([own_part, upper_part], axis=0)
-    gathered = lax.all_gather(local_set, "wrk", axis=1, tiled=True)
+    gathered = lax.all_gather(local_set, WORKER_AXES, axis=1, tiled=True)
     group_set = gathered.reshape(2 * grp_orbs, box_edge, plane_size + lanes)
 
     entries = 2 * slot_cap + 1
@@ -129,8 +130,9 @@
     offset_diff = corner_of(right_orb, offsets) - corner_of(left_orb, offsets)
     left_row = jnp.clip(left_orb - base, 0, 2 * grp_orbs - 1)
     right_row = jnp.clip(right_orb - base, 0, 2 * grp_orbs - 1)
-    left_boxes = jnp.take(group_set, left_row, axis=0)[:, :, :plane_size]
-    right_boxes = jnp.take(group_set, right_row, axis=0)[:, :, :plane_size]
+    both_boxes = jnp.take(group_set, jnp.concatenate([left_row, right_row]), axis=0)[:, :, :plane_size]
+    left_boxes = both_boxes[:per_worker]
+    right_boxes = both_boxes[per_worker:]
     row_shift, plane_shift = shift_matrices(offset_diff, box_edge)
     right_field = move_bf16(right_boxes, row_shift, plane_shift)
 
@@ -156,17 +158,27 @@
     fields = jnp.concatenate([to_left, kept_right], axis=0)
     rows = jnp.concatenate([left_row, kept_rows], axis=0)
     combined = rows_to_orbitals(fields, rows, grp_orbs) + rows_to_orbitals(got_fields, got_rows, grp_orbs)
-    if EXCHANGE == "all_to_all":
-        pieces = lax.all_to_all(combined, "wrk", 0, 0, tiled=True)
-        return jnp.sum(pieces, axis=0, keepdims=True)
-    return lax.psum_scatter(combined, "wrk", scatter_dimension=0, tiled=True)
+    cores = lax.axis_size("core")
+    by_core = combined.reshape((workers // cores, cores) + combined.shape[1:])
+    mine = lax.dynamic_index_in_dim(by_core, core, axis=1, keepdims=False)
+    theirs = lax.dynamic_index_in_dim(by_core, cores - 1 - core, axis=1, keepdims=False)
+    half = mine + lax.ppermute(theirs, "core", [(0, 1), (1, 0)])
+    pieces = lax.all_to_all(half, "yx", 0, 0, tiled=True)
+    return jnp.sum(pieces, axis=0, keepdims=True)
 
 
 def solution(mesh):
+    groups, workers = mesh.devices.shape
+    split = jax.sharding.Mesh(mesh.devices.reshape(groups, workers // 2, 2), ("grp", "yx", "core"))
     return jax.shard_map(
         local,
-        mesh=mesh,
-        in_specs=(P(("grp", "wrk"), None, None), P(), P("grp", "wrk", None, None), P("grp", "wrk")),
-        out_specs=P(("grp", "wrk"), None, None),
+        mesh=split,
+        in_specs=(
+            P(("grp",) + WORKER_AXES, None, None),
+            P(),
+            P("grp", WORKER_AXES, None, None),
+            P("grp", WORKER_AXES),
+        ),
+        out_specs=P(("grp",) + WORKER_AXES, None, None),
         check_vma=False,
     )

time: 191 us -> 185 us (0.969)
  blocking collectives: 57 us -> 31.9 us
  local copies, waits for them, and re-layouts: 24.3 us -> 34.1 us
  waiting for transfers between devices: 53.5 us -> 57.3 us
  starting transfers between devices: 7.88 us -> 11.2 us
    all_to_all x1, blocking collectives: 57 us -> 31.9 us  [local(): pieces = lax.all_to_all(half, 'yx', 0, 0, tiled=True)]
    dynamic_slice x0 -> x2, local copies, waits for them, and re-layouts: none -> 9.11 us  [the longest x1 7.89 us: local(): mine = lax.dynamic_index_in_dim(by_core, core, axis=1, keepdims=False)]
    reshape x0 -> x1, local copies, waits for them, and re-layouts: none -> 5.82 us  [local(): by_core = combined.reshape((workers // cores, cores) + combined.shape[1:])]
    ppermute x0 -> x1, waiting for transfers between devices: none -> 3.76 us  [local(): half = mine + lax.ppermute(theirs, 'core', [(0, 1), (1, 0)])]
    ppermute x0 -> x1, starting transfers between devices: none -> 3.32 us  [local(): half = mine + lax.ppermute(theirs, 'core', [(0, 1), (1, 0)])]
    gather x2 -> x1, local copies, waits for them, and re-layouts: 5.83 us -> 2.96 us  [local(): jnp.take(group_set, jnp.concatenate([left_row, right_row]), axis=0)]
    add x1 -> x0, local copies, waits for them, and re-layouts: 2.43 us -> none  [local(): rows_to_orbitals(fields, rows, grp_orbs)]
    reduce_sum x1, other arithmetic: 3.09 us -> 0.77 us  [local(): return jnp.sum(pieces, axis=0, keepdims=True)]
  transfers between devices with their start and end apart: 4 -> 5, of which waited for: 3 -> 4; matrix products, arithmetic and copies ran while one was open for 16% -> 16% of each run, Pallas kernels for 0% -> 0%
where the time goes in v5:
time: 185 us; the launch traced here: 183 us
  waiting for transfers between devices  57.3 us (31%)
  local copies, waits for them, and re-layouts  34.1 us (18%)
  blocking collectives  31.9 us (17%)
  matrix products  19 us (10%)
  other arithmetic  15.3 us (8%)
  between operations  14.3 us (8%)
  starting transfers between devices  11.2 us (6%)
    all_gather x1, waiting for transfers between devices, local(): gathered = lax.all_gather(local_set, WORKER_AXES, axis=1, tiled=True)  45.5 us
    all_to_all x1, blocking collectives, local(): pieces = lax.all_to_all(half, 'yx', 0, 0, tiled=True)  31.9 us
    mul x1, local copies, waits for them, and re-layouts, local(): sine_rows[:, None, :, None] * sine_rows[None, :, None, :]  13.7 us
    ppermute x3, waiting for transfers between devices, passed_along(): lax.ppermute(value, axis, [(source, source + steps) for source in range(i...  7.99 us
    mul x1, other arithmetic, local(): sine_rows[:, None, :, None] * sine_rows[None, :, None, :]  7.97 us
    dynamic_slice x1, local copies, waits for them, and re-layouts, local(): mine = lax.dynamic_index_in_dim(by_core, core, axis=1, keepdims=False)  7.89 us
    ppermute x3, starting transfers between devices, passed_along(): lax.ppermute(value, axis, [(source, source + steps) for source in range(i...  7.89 us
    dot_general x2, matrix products, rows_to_orbitals(): summed = jnp.einsum('po,pf->of', chosen, flat, precision=highest)  5.88 us
  transfers between devices with their start and end apart: 5, of which 4 were waited for; matrix products, arithmetic and copies ran while one was open for 16% of the time, Pallas kernels for 0%

profile of v5, /device:TPU:1, one launch (start us, length us, event | category | flops | bytes accessed | tf_op | source)
XLA Modules:
  0.0 183.0 jit_solution(1953266442701793381)
XLA Ops:
  6.5 1.3 collective-permute-start
  8.5 0.8 copy.30
  9.3 0.1 reshape_squeeze.6
  9.3 0.1 fusion.53
  9.4 0.1 fusion.50
  9.5 0.1 broadcast_select_fusion.3
  9.6 0.8 maximum_bitcast_fusion.1
  10.4 2.3 %collective-permute-done = bf16[1,32,1024]{2,1,0:T(8,128)(2,1)S(1)} collective-permute-done((bf16[1,32,1024]{2,1,0:T(8,128)(2,1)}, bf16[1,32,1024]{2,1,0:T(8,128)(2,1)S(1)}, u32[]{:S(2)}, u32[]{:S(2)}) %collective-permute-start) | collective-permute-done | bytes 65568 | tf_op jit(solution)/shard_map/ppermute | solution.py:14
  12.8 0.7 pad_maximum_fusion
  13.5 0.1 sine_multiply_fusion
  13.6 8.0 %broadcast_multiply_fusion = f32[32,32,32,32]{3,2,1,0:T(8,128)} fusion(f32[32,32]{1,0:T(8,128)S(1)} %sine_multiply_fusion), kind=kLoop, calls=%fused_computation.4 | loop fusion | flops 1048576 | bytes 4198400 | tf_op jit(solution)/shard_map/mul | solution.py:140
  21.6 13.7 %reshape.645 = f32[1024,1024,1]{1,0,2:T(8,128)} reshape(f32[32,32,32,32]{3,2,1,0:T(8,128)} %broadcast_multiply_fusion) | data formatting | bytes 8388608 | tf_op jit(solution)/shard_map/mul | solution.py:140
  35.3 0.1 broadcast_add_fusion
  35.4 0.2 add.186
  35.6 0.2 add.187
  35.9 0.1 add.188
  36.0 45.5 %all-gather.2.cloned.1.call-done = bf16[2,32,32,1152]{3,2,1,0:T(8,128)(2,1)} async-done(((bf16[2,1,32,1152]{3,2,1,0:T(8,128)(2,1)}), bf16[2,32,32,1152]{3,2,1,0:T(8,128)(2,1)}) %all-gather.2.cloned.1.call-update) | async-done | bytes 4718608 | tf_op jit(solution)/shard_map/all_gather | solution.py:111
  81.5 0.9 slice_convert_fusion
  82.3 0.1 slice_add_fusion.2
  82.4 0.2 slice_reduce_fusion
  82.6 0.1 iota_compare_fusion.3
  82.7 0.1 lt.66
  82.8 0.3 reduce-window.9
  83.1 0.1 slice.79
  83.2 0.1 slice_reduce_fusion.6
  83.4 0.1 add_bitcast_fusion
  83.4 0.2 fusion.60
  83.6 0.1 copy.32
  83.7 0.1 broadcast_in_dim.156
  83.8 0.1 copy.31
  83.9 0.2 select_reduce_fusion.2
  84.1 0.2 fusion.46
  84.3 0.1 compare_and_fusion.4
  84.4 0.1 pad_add_fusion.1
  84.5 0.1 iota_compare_fusion.4
  84.6 0.2 select_reduce_fusion
  84.8 0.2 slice_reduce_fusion.3
  85.0 0.1 copy.35
  85.1 0.1 copy.34
  85.2 0.1 fusion.52
  85.5 3.0 %gather_fusion = bf16[6,32,1152]{2,1,0:T(8,128)(2,1)S(1)} fusion(bf16[64,32,1152]{2,1,0:T(8,128)(2,1)} %bitcast.69, s32[1024]{0:T(1024)S(1)} %pad_clamp_fusion), kind=kCustom, calls=%fused_computation | custom fusion | bytes 884760 | tf_op jit(solution)/shard_map/jit(_take)/gather | solution.py:133
  88.4 0.1 broadcast_select_fusion
  88.6 3.0 %fusion.1 = f32[3,32,1024]{2,1,0:T(8,128)S(1)} fusion(s32[3,1024]{1,0:T(4,128)S(1)} %broadcast_subtract_fusion, s32[1024]{0:T(1024)S(1)} %get-tuple-element.48, s32[3,1024]{1,0:T(4,128)S(1)} %broadcast_subtract_fusion.1, s32[1024]{0:T(1024)S(1)} %get-tuple-element.49, bf16[6,32,1152]{2,1,0:T(8,128)(2,1)S(1)} %broadcast_select_fusion), kind=kOutput, calls=%fused_computation.3 | convolution fusion | flops 210763776 | bytes 630784 | tf_op jit(solution)/shard_map/pxc,pyc->pxy/dot_general | solution.py:45
  91.5 0.4 fusion.20
  91.9 0.6 convolution_bitcast_fusion.1
  92.5 2.5 %convolution_multiply_fusion.1 = f32[3,32,1024]{2,1,0:T(8,128)S(1)} fusion(f32[3,32,1024]{2,1,0:T(8,128)S(1)} %convolution_bitcast_fusion.1, f32[1024,1024,1]{1,0,2:T(8,128)S(1)} %copy-done, f32[32,1024]{1,0:T(8,128)S(1)} %add_divide_fusion), kind=kOutput, calls=%fused_computation.19 | convolution fusion | flops 1208057856 | bytes 5111808 | tf_op jit(solution)/shard_map/dot_general | solution.py:67
  95.1 0.6 convolution_bitcast_fusion
  95.7 2.6 %fusion.62 = (f32[3,32,1024]{2,1,0:T(8,128)S(1)}, f32[3,32,1024]{2,1,0:T(8,128)S(1)}) fusion(f32[3,32,1024]{2,1,0:T(8,128)S(1)} %fusion.20, f32[3]{0:T(128)S(1)} %get-tuple-element.41, f32[3,32,1024]{2,1,0:T(8,128)S(1)} %convolution_bitcast_fusion, f32[1024,1024,1]{1,0,2:T(8,128)S(1)} %copy-done), kind=kOutput, calls=%fused_computation.149 | convolution fusion | flops 1208156160 | bytes 5767180 | tf_op jit(solution)/shard_map/dot_general | solution.py:67
  98.3 0.4 reduce-precision_convert_fusion.1
  98.6 3.4 %collective-permute-start.1 = (s32[3]{0:T(128)S(1)}, s32[3]{0:T(128)S(1)}, u32[]{:S(2)}, u32[]{:S(2)}) collective-permute-start(s32[3]{0:T(128)S(1)} %get-tuple-element.26), channel_id=1, source_target_pairs={{0,32},{32,64},{64,96},{96,128},{128,160},{160,192},{192,224},{224... | collective-permute-start | bytes 44 | tf_op jit(solution)/shard_map/ppermute | solution.py:14
  102.1 3.1 %fusion = f32[3,96,1024]{2,1,0:T(8,128)S(1)} fusion(s32[3,1024]{1,0:T(4,128)S(1)} %broadcast_subtract_fusion, s32[1024]{0:T(1024)S(1)} %get-tuple-element.48, s32[3,1024]{1,0:T(4,128)S(1)} %broadcast_subtract_fusion.1, s32[1024]{0:T(1024)S(1)} %get-tuple-element.49, bf16[3,32,1024]{2,1,0:T(8,128)(2,1)S(1)} %get-tuple-element.37, ...), kind=kOutput, calls=%fused_computation.2 | convolution fusion | flops 615186432 | bytes 1802240 | tf_op jit(solution)/shard_map/pxc,pcy->pxy/dot_general | solution.py:56
  105.1 0.1 broadcast_select_fusion.1
  105.3 3.2 %collective-permute-start.2 = (f32[3,32,1024]{2,1,0:T(8,128)S(1)}, f32[3,32,1024]{2,1,0:T(8,128)S(1)}, u32[]{:S(2)}, u32[]{:S(2)}) collective-permute-start(f32[3,32,1024]{2,1,0:T(8,128)S(1)} %get-tuple-element.34), channel_id=1, source_target_pairs={{0,32},{32,64},{64,96},{96,128},{128,160},{160,192},{192,224},{224... | collective-permute-start | bytes 1179656 | tf_op jit(solution)/shard_map/ppermute | solution.py:14
  108.5 2.1 %fusion.41 = f32[32,32,1024]{2,0,1:T(8,128)S(1)} fusion(s32[6]{0:T(128)S(1)} %pad_add_fusion.1, f32[1,6,32,1024]{3,2,1,0:T(8,128)S(1)} %maximum_bitcast_fusion), kind=kOutput, calls=%fused_computation.89 | convolution fusion | flops 75497664 | bytes 4980760 | tf_op jit(solution)/shard_map/po,pf->of/dot_general | solution.py:85
  110.7 5.7 %collective-permute-done.2 = f32[3,32,1024]{2,1,0:T(8,128)S(1)} collective-permute-done((f32[3,32,1024]{2,1,0:T(8,128)S(1)}, f32[3,32,1024]{2,1,0:T(8,128)S(1)}, u32[]{:S(2)}, u32[]{:S(2)}) %collective-permute-start.2) | collective-permute-done | bytes 393248 | tf_op jit(solution)/shard_map/ppermute | solution.py:14
  116.4 3.8 %convolution_add_fusion = f32[32,32,1024]{2,0,1:T(8,128)} fusion(f32[32,32,1024]{2,0,1:T(8,128)S(1)} %fusion.41, s32[3]{0:T(128)S(1)} %collective-permute-done.1, f32[1,3,32,1024]{3,2,1,0:T(8,128)S(1)} %bitcast.66), kind=kOutput, calls=%fused_computation.13 | convolution fusion | flops 38797408 | bytes 8781836 | tf_op jit(solution)/shard_map/po,pf->of/dot_general | solution.py:85
  120.1 5.8 %reshape.633 = f32[16,2,32,1024]{3,1,0,2:T(2,128)} reshape(f32[32,32,1024]{2,0,1:T(8,128)} %convolution_add_fusion) | data formatting | bytes 8388608 | tf_op jit(solution)/shard_map/reshape | solution.py:162
  125.9 7.9 %constant_dynamic-slice_fusion.1 = (f32[16,1,32,1024]{3,1,0,2:T(1,128)S(1)}, f32[16,1,32,1024]{3,1,0,2:T(1,128)S(1)}) fusion(f32[16,2,32,1024]{3,1,0,2:T(2,128)} %reshape.633, s32[]{:T(128)S(6)} %select_n.155, s32[]{:T(128)S(6)} %select_n.156), kind=kLoop, calls=%fused_computation.135 | loop fusion | bytes 8388616 | tf_op jit(solution)/shard_map/jit(dynamic_index_in_dim)/dynamic_slice | solution.py:163
  133.8 1.2 copy.52
  135.1 3.3 %collective-permute-start.3 = (f32[16,32,1024]{2,1,0:T(8,128)S(1)}, f32[16,32,1024]{2,1,0:T(8,128)S(1)}, u32[]{:S(2)}, u32[]{:S(2)}) collective-permute-start(f32[16,32,1024]{2,1,0:T(8,128)S(1)} %bitcast.65), channel_id=1, source_target_pairs={{0,1},{1,0},{2,3},{3,2},{4,5},{5,4},{6,7},{7,6},{8,9},{9,8},{10,11... | collective-permute-start | bytes 6291464 | tf_op jit(solution)/shard_map/ppermute | solution.py:165
  138.4 3.8 %collective-permute-done.3 = f32[16,32,1024]{2,1,0:T(8,128)S(1)} collective-permute-done((f32[16,32,1024]{2,1,0:T(8,128)S(1)}, f32[16,32,1024]{2,1,0:T(8,128)S(1)}, u32[]{:S(2)}, u32[]{:S(2)}) %collective-permute-start.3) | collective-permute-done | bytes 2097184 | tf_op jit(solution)/shard_map/ppermute | solution.py:165
  142.2 1.3 bitcast_add_fusion
  143.5 31.9 %all_to_all.5 = f32[16,32,1024]{2,1,0:T(8,128)S(1)} all-to-all(f32[16,32,1024]{2,1,0:T(8,128)S(1)} %bitcast_add_fusion), channel_id=1, replica_groups=mesh['grp'=16,'yx'=16,'core'=2] {'yx'}, dimensions={0} | all-to-all | bytes 4194304 | tf_op jit(solution)/shard_map/all_to_all | solution.py:166
  175.4 0.8 reduce_sum.39
  (29 shorter events, 0.5 us)
Async XLA Ops:
  6.5 75.0 %all-gather.2.cloned.1.call-start = ((), (), s32[]{:S(2)}) async-start(), calls=%async_computation.1 | async-start | bytes 4866048 | tf_op jit(solution)/shard_map/all_gather | solution.py:111
  6.5 6.2 %collective-permute-start = (bf16[1,32,1024]{2,1,0:T(8,128)(2,1)}, bf16[1,32,1024]{2,1,0:T(8,128)(2,1)S(1)}, u32[]{:S(2)}, u32[]{:S(2)}) collective-permute-start(bf16[1,32,1024]{2,1,0:T(8,128)(2,1)} %param.6), channel_id=1, source_target_pairs={{32,0},{64,32},{96,64},{128,96},{160,128},{192,160},{224,192},{256... | collective-permute-start | bytes 196616 | tf_op jit(solution)/shard_map/ppermute | solution.py:14
  21.6 63.0 %copy-start.1 = (s32[512,3]{0,1:T(4,128)S(1)}, s32[512,3]{0,1:T(4,128)}, u32[]{:S(2)}) copy-start(s32[512,3]{0,1:T(4,128)} %param.7) | copy-start | bytes 18436
  88.6 4.0 %copy-start = (f32[1024,1024,1]{1,0,2:T(8,128)S(1)}, f32[1024,1024,1]{1,0,2:T(8,128)}, u32[]{:S(2)}) copy-start(f32[1024,1024,1]{1,0,2:T(8,128)} %reshape.645) | copy-start | bytes 12582916
  98.6 12.0 %collective-permute-start.1 = (s32[3]{0:T(128)S(1)}, s32[3]{0:T(128)S(1)}, u32[]{:S(2)}, u32[]{:S(2)}) collective-permute-start(s32[3]{0:T(128)S(1)} %get-tuple-element.26), channel_id=1, source_target_pairs={{0,32},{32,64},{64,96},{96,128},{128,160},{160,192},{192,224},{224... | collective-permute-start | bytes 44 | tf_op jit(solution)/shard_map/ppermute | solution.py:14
  105.3 11.1 %collective-permute-start.2 = (f32[3,32,1024]{2,1,0:T(8,128)S(1)}, f32[3,32,1024]{2,1,0:T(8,128)S(1)}, u32[]{:S(2)}, u32[]{:S(2)}) collective-permute-start(f32[3,32,1024]{2,1,0:T(8,128)S(1)} %get-tuple-element.34), channel_id=1, source_target_pairs={{0,32},{32,64},{64,96},{96,128},{128,160},{160,192},{192,224},{224... | collective-permute-start | bytes 1179656 | tf_op jit(solution)/shard_map/ppermute | solution.py:14
  135.1 7.1 %collective-permute-start.3 = (f32[16,32,1024]{2,1,0:T(8,128)S(1)}, f32[16,32,1024]{2,1,0:T(8,128)S(1)}, u32[]{:S(2)}, u32[]{:S(2)}) collective-permute-start(f32[16,32,1024]{2,1,0:T(8,128)S(1)} %bitcast.65), channel_id=1, source_target_pairs={{0,1},{1,0},{2,3},{3,2},{4,5},{5,4},{6,7},{7,6},{8,9},{9,8},{10,11... | collective-permute-start | bytes 6291464 | tf_op jit(solution)/shard_map/ppermute | solution.py:165
Sparse Core Ops, SparseCore 0:
  13.6 67.8 all-gather.1

commit v6 on v5

--- a/solution.py
+++ b/solution.py
@@ -155,13 +155,19 @@
 
     kept_right = jnp.where(upper[:, None, None], 0.0, to_right)
     kept_rows = jnp.where(upper, 0, right_row)
+    cores = lax.axis_size("core")
+    halves = workers // cores
+
+    def add_into(target, fields, rows, on_core):
+        keep = (rows % cores) == on_core
+        placed = jnp.where(keep[:, None, None], fields, 0.0)
+        return target.at[rows // cores].add(placed)
+
     fields = jnp.concatenate([to_left, kept_right], axis=0)
     rows = jnp.concatenate([left_row, kept_rows], axis=0)
-    combined = rows_to_orbitals(fields, rows, grp_orbs) + rows_to_orbitals(got_fields, got_rows, grp_orbs)
-    cores = lax.axis_size("core")
-    by_core = combined.reshape((workers // cores, cores) + combined.shape[1:])
-    mine = lax.dynamic_index_in_dim(by_core, core, axis=1, keepdims=False)
-    theirs = lax.dynamic_index_in_dim(by_core, cores - 1 - core, axis=1, keepdims=False)
+    empty = jnp.zeros((halves, box_edge, plane_size), jnp.float32)
+    theirs = add_into(add_into(empty, fields, rows, cores - 1 - core), got_fields, got_rows, cores - 1 - core)
+    mine = add_into(add_into(empty, fields, rows, core), got_fields, got_rows, core)
     half = mine + lax.ppermute(theirs, "core", [(0, 1), (1, 0)])
     pieces = lax.all_to_all(half, "yx", 0, 0, tiled=True)
     return jnp.sum(pieces, axis=0, keepdims=True)

time: 185 us -> 173 us (0.935)
  local copies, waits for them, and re-layouts: 34.1 us -> 20.2 us
  other arithmetic: 15.3 us -> 27 us
  matrix products: 19 us -> 13.3 us
  waiting for transfers between devices: 57.3 us -> 53.4 us
    scatter-add x0 -> x4, other arithmetic: none -> 9.42 us  [add_into(): return target.at[rows // cores].add(placed)]
    dynamic_slice x2 -> x0, local copies, waits for them, and re-layouts: 9.11 us -> none  [the longest x1 7.89 us: local(): mine = lax.dynamic_index_in_dim(by_core, core, axis=1, keepdims=False)]
    dot_general x2 -> x0, matrix products: 5.88 us -> none  [rows_to_orbitals(): summed = jnp.einsum('po,pf->of', chosen, flat, precision=highest)]
    reshape x1 -> x0, local copies, waits for them, and re-layouts: 5.82 us -> none  [local(): by_core = combined.reshape((workers // cores, cores) + combined.shape[1:])]
    ppermute x3, waiting for transfers between devices: 7.99 us -> 4.01 us  [passed_along(): lax.ppermute(value, axis, [(source, source + steps) for source in range(i...]
    select_n x0 -> x3, other arithmetic: none -> 3.03 us  [the longest x2 3.01 us: add_into(): placed = jnp.where(keep[:, None, None], fields, 0.0)]
where the time goes in v6:
time: 173 us; the launch traced here: 171 us
  waiting for transfers between devices  53.4 us (31%)
  blocking collectives  32.3 us (19%)
  other arithmetic  27 us (16%)
  local copies, waits for them, and re-layouts  20.2 us (12%)
  between operations  14.3 us (8%)
  matrix products  13.3 us (8%)
  starting transfers between devices  10.7 us (6%)
    all_gather x1, waiting for transfers between devices, local(): gathered = lax.all_gather(local_set, WORKER_AXES, axis=1, tiled=True)  45.5 us
    all_to_all x1, blocking collectives, local(): pieces = lax.all_to_all(half, 'yx', 0, 0, tiled=True)  32.3 us
    mul x1, local copies, waits for them, and re-layouts, local(): sine_rows[:, None, :, None] * sine_rows[None, :, None, :]  13.7 us
    scatter-add x4, other arithmetic, add_into(): return target.at[rows // cores].add(placed)  9.42 us
    mul x1, other arithmetic, local(): sine_rows[:, None, :, None] * sine_rows[None, :, None, :]  7.97 us
    ppermute x3, starting transfers between devices, passed_along(): lax.ppermute(value, axis, [(source, source + steps) for source in range(i...  7.63 us
    dot_general x2, matrix products, apply_sines(): jnp.dot(flat_rows, plane_sines, precision=highest, preferred_element_type...  5.11 us
    ppermute x3, waiting for transfers between devices, passed_along(): lax.ppermute(value, axis, [(source, source + steps) for source in range(i...  4.01 us
  transfers between devices with their start and end apart: 5, of which 4 were waited for; matrix products, arithmetic and copies ran while one was open for 16% of the time, Pallas kernels for 0%

profile of v6, /device:TPU:1, one launch (start us, length us, event | category | flops | bytes accessed | tf_op | source)
XLA Modules:
  0.0 171.3 jit_solution(7030456657966381941)
XLA Ops:
  6.5 1.3 collective-permute-start
  7.8 0.8 copy.21
  8.6 0.1 reshape_squeeze.6
  9.3 0.1 fusion.50
  9.4 0.1 fusion.45
  9.5 0.1 broadcast_select_fusion.5
  9.6 0.8 maximum_bitcast_fusion
  10.4 2.3 %collective-permute-done = bf16[1,32,1024]{2,1,0:T(8,128)(2,1)S(1)} collective-permute-done((bf16[1,32,1024]{2,1,0:T(8,128)(2,1)}, bf16[1,32,1024]{2,1,0:T(8,128)(2,1)S(1)}, u32[]{:S(2)}, u32[]{:S(2)}) %collective-permute-start) | collective-permute-done | bytes 65568 | tf_op jit(solution)/shard_map/ppermute | solution.py:14
  12.8 0.7 pad_maximum_fusion.1
  13.5 0.1 sine_multiply_fusion
  13.6 8.0 %broadcast_multiply_fusion = f32[32,32,32,32]{3,2,1,0:T(8,128)} fusion(f32[32,32]{1,0:T(8,128)S(1)} %sine_multiply_fusion), kind=kLoop, calls=%fused_computation.8 | loop fusion | flops 1048576 | bytes 4198400 | tf_op jit(solution)/shard_map/mul | solution.py:140
  21.6 13.7 %reshape.861 = f32[1024,1024,1]{1,0,2:T(8,128)} reshape(f32[32,32,32,32]{3,2,1,0:T(8,128)} %broadcast_multiply_fusion) | data formatting | bytes 8388608 | tf_op jit(solution)/shard_map/mul | solution.py:140
  35.3 0.1 broadcast_add_fusion
  35.4 0.2 add.232
  35.6 0.2 add.233
  36.0 45.5 %all-gather.2.cloned.1.call-done = bf16[2,32,32,1152]{3,2,1,0:T(8,128)(2,1)} async-done(((bf16[2,1,32,1152]{3,2,1,0:T(8,128)(2,1)}), bf16[2,32,32,1152]{3,2,1,0:T(8,128)(2,1)}) %all-gather.2.cloned.1.call-update) | async-done | bytes 4718608 | tf_op jit(solution)/shard_map/all_gather | solution.py:111
  81.5 0.9 slice_convert_fusion
  82.3 0.1 slice_add_fusion.2
  82.4 0.2 slice_reduce_fusion
  82.6 0.1 iota_compare_fusion.3
  82.7 0.1 lt.90
  82.8 0.3 reduce-window.9
  83.1 0.1 slice.79
  83.2 0.1 slice_reduce_fusion.6
  83.4 0.1 add_bitcast_fusion
  83.4 0.1 broadcast_in_dim.196
  83.6 0.2 fusion.57
  83.8 0.1 copy.23
  83.9 0.2 select_reduce_fusion.2
  84.1 0.2 fusion.42
  84.3 0.1 copy.25
  84.4 0.1 copy.26
  84.5 0.1 copy.28
  84.6 0.1 fusion.49
  84.7 0.1 iota_compare_fusion.4
  84.8 0.2 select_reduce_fusion
  85.0 0.2 slice_reduce_fusion.3
  85.3 0.1 broadcast_compare_fusion.1
  85.3 3.0 %gather_fusion = bf16[6,32,1152]{2,1,0:T(8,128)(2,1)S(1)} fusion(bf16[64,32,1152]{2,1,0:T(8,128)(2,1)} %bitcast.39, s32[1024]{0:T(1024)S(1)} %pad_clamp_fusion), kind=kCustom, calls=%fused_computation | custom fusion | bytes 884760 | tf_op jit(solution)/shard_map/jit(_take)/gather | solution.py:133
  88.3 0.1 broadcast_select_fusion
  88.6 3.0 %fusion.1 = f32[3,32,1024]{2,1,0:T(8,128)S(1)} fusion(s32[3,1024]{1,0:T(4,128)S(1)} %broadcast_subtract_fusion, s32[1024]{0:T(1024)S(1)} %get-tuple-element.60, s32[3,1024]{1,0:T(4,128)S(1)} %broadcast_subtract_fusion.1, s32[1024]{0:T(1024)S(1)} %get-tuple-element.61, bf16[6,32,1152]{2,1,0:T(8,128)(2,1)S(1)} %broadcast_select_fusion), kind=kOutput, calls=%fused_computation.7 | convolution fusion | flops 210763776 | bytes 630784 | tf_op jit(solution)/shard_map/pxc,pyc->pxy/dot_general | solution.py:45
  91.5 0.4 fusion.22
  91.9 0.6 convolution_bitcast_fusion.1
  92.5 2.5 %convolution_multiply_fusion.1 = f32[3,32,1024]{2,1,0:T(8,128)S(1)} fusion(f32[3,32,1024]{2,1,0:T(8,128)S(1)} %convolution_bitcast_fusion.1, f32[1024,1024,1]{1,0,2:T(8,128)S(1)} %copy-done, f32[32,1024]{1,0:T(8,128)S(1)} %add_divide_fusion), kind=kOutput, calls=%fused_computation.20 | convolution fusion | flops 1208057856 | bytes 5111808 | tf_op jit(solution)/shard_map/dot_general | solution.py:67
  95.1 0.6 convolution_bitcast_fusion
  95.7 2.6 %fusion.59 = (f32[3,32,1024]{2,1,0:T(8,128)S(1)}, f32[3,32,1024]{2,1,0:T(8,128)S(1)}) fusion(f32[3,32,1024]{2,1,0:T(8,128)S(1)} %fusion.22, f32[3]{0:T(128)S(1)} %get-tuple-element.51, f32[3,32,1024]{2,1,0:T(8,128)S(1)} %convolution_bitcast_fusion, f32[1024,1024,1]{1,0,2:T(8,128)S(1)} %copy-done), kind=kOutput, calls=%fused_computation.166 | convolution fusion | flops 1208156160 | bytes 5767180 | tf_op jit(solution)/shard_map/dot_general | solution.py:67
  98.3 0.4 reduce-precision_convert_fusion.1
  98.7 3.3 %fusion = f32[3,96,1024]{2,1,0:T(8,128)S(1)} fusion(s32[3,1024]{1,0:T(4,128)S(1)} %broadcast_subtract_fusion, s32[1024]{0:T(1024)S(1)} %get-tuple-element.60, s32[3,1024]{1,0:T(4,128)S(1)} %broadcast_subtract_fusion.1, s32[1024]{0:T(1024)S(1)} %get-tuple-element.61, bf16[3,32,1024]{2,1,0:T(8,128)(2,1)S(1)} %get-tuple-element.45, ...), kind=kOutput, calls=%fused_computation.6 | convolution fusion | flops 615186432 | bytes 1802240 | tf_op jit(solution)/shard_map/pxc,pcy->pxy/dot_general | solution.py:56
  101.9 0.9 broadcast_select_fusion.3
  102.8 3.2 %collective-permute-start.2 = (f32[3,32,1024]{2,1,0:T(8,128)}, f32[3,32,1024]{2,1,0:T(8,128)S(1)}, u32[]{:S(2)}, u32[]{:S(2)}) collective-permute-start(f32[3,32,1024]{2,1,0:T(8,128)} %get-tuple-element.38), channel_id=1, source_target_pairs={{0,32},{32,64},{64,96},{96,128},{128,160},{160,192},{192,224},{224... | collective-permute-start | bytes 1179656 | tf_op jit(solution)/shard_map/ppermute | solution.py:14
  106.0 3.2 %collective-permute-start.1 = (s32[3]{0:T(128)S(1)}, s32[3]{0:T(128)S(1)}, u32[]{:S(2)}, u32[]{:S(2)}) collective-permute-start(s32[3]{0:T(128)S(1)} %get-tuple-element.30), channel_id=1, source_target_pairs={{0,32},{32,64},{64,96},{96,128},{128,160},{160,192},{192,224},{224... | collective-permute-start | bytes 44 | tf_op jit(solution)/shard_map/ppermute | solution.py:14
  109.2 1.1 fusion.10
  110.3 0.2 broadcast_in_dim.191
  110.6 2.2 %scatter_fusion = f32[16,32,1024]{2,1,0:T(8,128)S(1)} fusion(f32[16,32,1024]{2,1,0:T(8,128)S(1)} %broadcast_in_dim.191, s32[6]{0:T(128)S(1)} %get-tuple-element.55, f32[6,32,1024]{2,1,0:T(8,128)} %get-tuple-element.41), kind=kCustom, calls=%fused_computation.1 | custom fusion | flops 196608 | bytes 2359320 | tf_op jit(solution)/shard_map/scatter-add | solution.py:164
  112.8 1.7 collective-permute-done.1
  114.6 0.7 copy-done.1
  115.3 1.9 %broadcast_select_fusion.1 = (f32[3,32,1024]{2,1,0:T(8,128)S(1)}, f32[3,32,1024]{2,1,0:T(8,128)}) fusion(f32[3,32,1024]{2,1,0:T(8,128)} %copy-done.1, pred[3]{0:T(512)(128)(4,1)S(1)} %get-tuple-element.26, pred[3]{0:T(512)(128)(4,1)S(1)} %broadcast_compare_fusion.2), kind=kLoop, calls=%fused_computation.41 | loop fusion | flops 196608 | bytes 1179654 | tf_op jit(solution)/shard_map/jit(_where)/select_n | solution.py:163
  117.2 1.7 %scatter_fusion.1 = f32[16,32,1024]{2,1,0:T(8,128)S(1)} fusion(f32[16,32,1024]{2,1,0:T(8,128)S(1)} %scatter_fusion, s32[3]{0:T(128)S(1)} %compare_select_fusion.1, f32[3,32,1024]{2,1,0:T(8,128)} %get-tuple-element.43), kind=kCustom, calls=%fused_computation.2 | custom fusion | flops 98304 | bytes 1179660 | tf_op jit(solution)/shard_map/scatter-add | solution.py:164
  118.9 3.1 %collective-permute-start.3 = (f32[16,32,1024]{2,1,0:T(8,128)S(1)}, f32[16,32,1024]{2,1,0:T(8,128)}, u32[]{:S(2)}, u32[]{:S(2)}) collective-permute-start(f32[16,32,1024]{2,1,0:T(8,128)S(1)} %scatter_fusion.1), channel_id=1, source_target_pairs={{0,1},{1,0},{2,3},{3,2},{4,5},{5,4},{6,7},{7,6},{8,9},{9,8},{10,11... | collective-permute-start | bytes 6291464 | tf_op jit(solution)/shard_map/ppermute | solution.py:171
  122.0 3.9 %collective-permute-done.3 = f32[16,32,1024]{2,1,0:T(8,128)} collective-permute-done((f32[16,32,1024]{2,1,0:T(8,128)S(1)}, f32[16,32,1024]{2,1,0:T(8,128)}, u32[]{:S(2)}, u32[]{:S(2)}) %collective-permute-start.3) | collective-permute-done | bytes 2097184 | tf_op jit(solution)/shard_map/ppermute | solution.py:171
  125.9 3.0 %scatter_fusion.2 = f32[16,32,1024]{2,1,0:T(8,128)} fusion(f32[16,32,1024]{2,1,0:T(8,128)} %collective-permute-done.3, s32[6]{0:T(128)S(1)} %get-tuple-element.55, f32[6,32,1024]{2,1,0:T(8,128)S(1)} %get-tuple-element.40), kind=kCustom, calls=%fused_computation.3 | custom fusion | flops 196608 | bytes 2359320 | tf_op jit(solution)/shard_map/scatter-add | solution.py:164
  128.9 2.5 %scatter_fusion.3 = f32[16,32,1024]{2,1,0:T(8,128)} fusion(f32[16,32,1024]{2,1,0:T(8,128)} %scatter_fusion.2, s32[3]{0:T(128)S(1)} %compare_select_fusion.1, f32[3,32,1024]{2,1,0:T(8,128)S(1)} %get-tuple-element.42), kind=kCustom, calls=%fused_computation.4 | custom fusion | flops 98304 | bytes 1179660 | tf_op jit(solution)/shard_map/scatter-add | solution.py:164
  131.4 32.3 %all_to_all.5 = f32[16,32,1024]{2,1,0:T(8,128)S(1)} all-to-all(f32[16,32,1024]{2,1,0:T(8,128)} %scatter_fusion.3), channel_id=1, replica_groups=mesh['grp'=16,'yx'=16,'core'=2] {'yx'}, dimensions={0} | all-to-all | bytes 4194304 | tf_op jit(solution)/shard_map/all_to_all | solution.py:172
  163.7 0.8 reduce_sum.39
  (35 shorter events, 0.6 us)
Async XLA Ops:
  6.5 75.0 %all-gather.2.cloned.1.call-start = ((), (), s32[]{:S(2)}) async-start(), calls=%async_computation.1 | async-start | bytes 4866048 | tf_op jit(solution)/shard_map/all_gather | solution.py:111
  6.5 6.2 %collective-permute-start = (bf16[1,32,1024]{2,1,0:T(8,128)(2,1)}, bf16[1,32,1024]{2,1,0:T(8,128)(2,1)S(1)}, u32[]{:S(2)}, u32[]{:S(2)}) collective-permute-start(bf16[1,32,1024]{2,1,0:T(8,128)(2,1)} %param.6), channel_id=1, source_target_pairs={{32,0},{64,32},{96,64},{128,96},{160,128},{192,160},{224,192},{256... | collective-permute-start | bytes 196616 | tf_op jit(solution)/shard_map/ppermute | solution.py:14
  21.6 63.2 %copy-start.2 = (s32[512,3]{0,1:T(4,128)S(1)}, s32[512,3]{0,1:T(4,128)}, u32[]{:S(2)}) copy-start(s32[512,3]{0,1:T(4,128)} %param.7) | copy-start | bytes 18436
  88.6 4.0 %copy-start = (f32[1024,1024,1]{1,0,2:T(8,128)S(1)}, f32[1024,1024,1]{1,0,2:T(8,128)}, u32[]{:S(2)}) copy-start(f32[1024,1024,1]{1,0,2:T(8,128)} %reshape.861) | copy-start | bytes 12582916
  102.8 11.7 %collective-permute-start.2 = (f32[3,32,1024]{2,1,0:T(8,128)}, f32[3,32,1024]{2,1,0:T(8,128)S(1)}, u32[]{:S(2)}, u32[]{:S(2)}) collective-permute-start(f32[3,32,1024]{2,1,0:T(8,128)} %get-tuple-element.38), channel_id=1, source_target_pairs={{0,32},{32,64},{64,96},{96,128},{128,160},{160,192},{192,224},{224... | collective-permute-start | bytes 1179656 | tf_op jit(solution)/shard_map/ppermute | solution.py:14
  106.0 8.5 %collective-permute-start.1 = (s32[3]{0:T(128)S(1)}, s32[3]{0:T(128)S(1)}, u32[]{:S(2)}, u32[]{:S(2)}) collective-permute-start(s32[3]{0:T(128)S(1)} %get-tuple-element.30), channel_id=1, source_target_pairs={{0,32},{32,64},{64,96},{96,128},{128,160},{160,192},{192,224},{224... | collective-permute-start | bytes 44 | tf_op jit(solution)/shard_map/ppermute | solution.py:14
  114.5 0.7 copy-start.1
  118.9 7.0 %collective-permute-start.3 = (f32[16,32,1024]{2,1,0:T(8,128)S(1)}, f32[16,32,1024]{2,1,0:T(8,128)}, u32[]{:S(2)}, u32[]{:S(2)}) collective-permute-start(f32[16,32,1024]{2,1,0:T(8,128)S(1)} %scatter_fusion.1), channel_id=1, source_target_pairs={{0,1},{1,0},{2,3},{3,2},{4,5},{5,4},{6,7},{7,6},{8,9},{9,8},{10,11... | collective-permute-start | bytes 6291464 | tf_op jit(solution)/shard_map/ppermute | solution.py:171
Sparse Core Ops, SparseCore 0:
  13.6 67.8 all-gather.1

commit v7 on v6

--- a/solution.py
+++ b/solution.py
@@ -103,16 +103,29 @@
     grp_orbs = orb_dev * workers
     lanes = 128
     slot_cap = pair_slots.shape[2]
-    table = table_lanes(pair_slots, pair_count, box_edge, lanes)
+    table = table_lanes(pair_slots, pair_count, box_edge, lanes)[0]
+    cores = lax.axis_size("core")
+    chips = lax.axis_size("yx")
+    swap = [(0, 1), (1, 0)]
     upper_set = passed_along(orbitals, "grp", -1)
-    own_part = jnp.concatenate([orbitals, table], axis=-1)
-    upper_part = jnp.concatenate([upper_set, jnp.zeros_like(table)], axis=-1)
-    local_set = jnp.stack([own_part, upper_part], axis=0)
-    gathered = lax.all_gather(local_set, WORKER_AXES, axis=1, tiled=True)
-    group_set = gathered.reshape(2 * grp_orbs, box_edge, plane_size + lanes)
+    own_part = jnp.concatenate([orbitals[0], table], axis=-1)
+    upper_part = jnp.concatenate([upper_set[0], jnp.zeros_like(table)], axis=-1)
+    first = core == 0
+    keep = jnp.where(first, own_part, upper_part)
+    got = lax.ppermute(jnp.where(first, upper_part, own_part), "core", swap)
+    chip_pair = jnp.where(first, jnp.stack([keep, got]), jnp.stack([got, keep]))
+    sent = jnp.broadcast_to(chip_pair[None], (chips,) + chip_pair.shape)
+    collected = lax.all_to_all(sent, "yx", 0, 0, tiled=True).reshape(
+        (grp_orbs, box_edge, plane_size + lanes)
+    )
+    other = lax.ppermute(collected, "core", swap)
 
     entries = 2 * slot_cap + 1
-    digits = gathered[0, :, 0, plane_size : plane_size + 2 * entries].astype(jnp.int32)
+    digits = jnp.where(
+        first,
+        collected[:, 0, plane_size : plane_size + 2 * entries],
+        other[:, 0, plane_size : plane_size + 2 * entries],
+    ).astype(jnp.int32)
     values = digits[:, :entries] * box_edge + digits[:, entries:]
     group_slots = values[:, : 2 * slot_cap].reshape(-1, 2)
     group_count = values[:, 2 * slot_cap]
@@ -130,7 +143,14 @@
     offset_diff = corner_of(right_orb, offsets) - corner_of(left_orb, offsets)
     left_row = jnp.clip(left_orb - base, 0, 2 * grp_orbs - 1)
     right_row = jnp.clip(right_orb - base, 0, 2 * grp_orbs - 1)
-    both_boxes = jnp.take(group_set, jnp.concatenate([left_row, right_row]), axis=0)[:, :, :plane_size]
+    wanted_rows = jnp.concatenate([left_row, right_row])
+    in_collected = (wanted_rows < grp_orbs) == first
+    slot = wanted_rows % grp_orbs
+    both_boxes = jnp.where(
+        in_collected[:, None, None],
+        jnp.take(collected, slot, axis=0)[:, :, :plane_size],
+        jnp.take(other, slot, axis=0)[:, :, :plane_size],
+    )
     left_boxes = both_boxes[:per_worker]
     right_boxes = both_boxes[per_worker:]
     row_shift, plane_shift = shift_matrices(offset_diff, box_edge)
@@ -155,7 +175,6 @@
 
     kept_right = jnp.where(upper[:, None, None], 0.0, to_right)
     kept_rows = jnp.where(upper, 0, right_row)
-    cores = lax.axis_size("core")
     halves = workers // cores
 
     def add_into(target, fields, rows, on_core):

time: 173 us -> 160 us (0.925)
  the two profiles are of different devices: /device:TPU:1 before, /device:TPU:384 now
where the time goes in v7:
time: 160 us; the launch traced here: 159 us
  blocking collectives  71.2 us (44%)
  other arithmetic  26.4 us (16%)
  local copies, waits for them, and re-layouts  19.6 us (12%)
  starting transfers between devices  15.7 us (10%)
  matrix products  13.2 us (8%)
  waiting for transfers between devices  11.7 us (7%)
    all_to_all x1, blocking collectives, local(): lax.all_to_all(sent, 'yx', 0, 0, tiled=True)  38.4 us
    all_to_all x1, blocking collectives, local(): pieces = lax.all_to_all(half, 'yx', 0, 0, tiled=True)  32.8 us
    mul x1, local copies, waits for them, and re-layouts, local(): sine_rows[:, None, :, None] * sine_rows[None, :, None, :]  13.7 us
    ppermute x3, starting transfers between devices, passed_along(): lax.ppermute(value, axis, [(source, source + steps) for source in range(i...  9.96 us
    scatter-add x4, other arithmetic, add_into(): return target.at[rows // cores].add(placed)  9.42 us
    mul x1, other arithmetic, local(): sine_rows[:, None, :, None] * sine_rows[None, :, None, :]  7.97 us
    ppermute x3, waiting for transfers between devices, passed_along(): lax.ppermute(value, axis, [(source, source + steps) for source in range(i...  6.18 us
    dot_general x2, matrix products, apply_sines(): jnp.dot(flat_rows, plane_sines, precision=highest, preferred_element_type...  5.12 us
  transfers between devices with their start and end apart: 6, of which 4 were waited for; matrix products, arithmetic and copies ran while one was open for 17% of the time, Pallas kernels for 0%

profile of v7, /device:TPU:384, one launch (start us, length us, event | category | flops | bytes accessed | tf_op | source)
XLA Modules:
  0.0 158.7 jit_solution(5836874903953970992)
XLA Ops:
  0.0 4.1 %collective-permute-start = (bf16[1,32,1024]{2,1,0:T(8,128)(2,1)}, bf16[1,32,1024]{2,1,0:T(8,128)(2,1)S(1)}, u32[]{:S(2)}, u32[]{:S(2)}) collective-permute-start(bf16[1,32,1024]{2,1,0:T(8,128)(2,1)} %param.8), channel_id=1, source_target_pairs={{32,0},{64,32},{96,64},{128,96},{160,128},{192,160},{224,192},{256... | collective-permute-start | bytes 196616 | tf_op jit(solution)/shard_map/ppermute | solution.py:14
  4.1 0.8 copy.25
  4.9 0.1 reshape_squeeze.6
  5.6 0.1 fusion.51
  5.7 0.1 fusion.46
  5.8 0.1 broadcast_select_fusion.6
  5.9 0.5 collective-permute-done
  6.4 0.9 select_bitcast_fusion
  7.2 1.9 %collective-permute-start.1 = (bf16[32,1152]{1,0:T(8,128)(2,1)S(1)}, bf16[32,1152]{1,0:T(8,128)(2,1)S(1)}, u32[]{:S(2)}, u32[]{:S(2)}) collective-permute-start(bf16[32,1152]{1,0:T(8,128)(2,1)S(1)} %get-tuple-element.49), channel_id=1, source_target_pairs={{0,1},{1,0},{2,3},{3,2},{4,5},{5,4},{6,7},{7,6},{8,9},{9,8},{10,11... | collective-permute-start | bytes 221192 | tf_op jit(solution)/shard_map/ppermute | solution.py:115
  9.2 1.2 collective-permute-done.1
  10.4 0.2 broadcast_in_dim.208
  10.7 38.4 %all_to_all.10 = bf16[16,2,32,1152]{3,2,1,0:T(8,128)(2,1)S(1)} all-to-all(bf16[16,2,32,1152]{3,2,1,0:T(8,128)(2,1)S(1)} %broadcast_in_dim.208), channel_id=1, replica_groups=mesh['grp'=16,'yx'=16,'core'=2] {'yx'}, dimensions={0} | all-to-all | bytes 4718592 | tf_op jit(solution)/shard_map/all_to_all | solution.py:118
  49.0 1.9 %collective-permute-start.2 = (bf16[32,32,1152]{2,1,0:T(8,128)(2,1)S(1)}, bf16[32,32,1152]{2,1,0:T(8,128)(2,1)}, u32[]{:S(2)}, u32[]{:S(2)}) collective-permute-start(bf16[32,32,1152]{2,1,0:T(8,128)(2,1)S(1)} %bitcast.37), channel_id=1, source_target_pairs={{0,1},{1,0},{2,3},{3,2},{4,5},{5,4},{6,7},{7,6},{8,9},{9,8},{10,11... | collective-permute-start | bytes 7077896 | tf_op jit(solution)/shard_map/ppermute | solution.py:121
  51.0 0.1 sine_multiply_fusion
  51.1 8.0 %broadcast_multiply_fusion = f32[32,32,32,32]{3,2,1,0:T(8,128)} fusion(f32[32,32]{1,0:T(8,128)S(1)} %sine_multiply_fusion), kind=kLoop, calls=%fused_computation.9 | loop fusion | flops 1048576 | bytes 4198400 | tf_op jit(solution)/shard_map/mul | solution.py:160
  59.1 13.7 %reshape.808 = f32[1024,1024,1]{1,0,2:T(8,128)} reshape(f32[32,32,32,32]{3,2,1,0:T(8,128)} %broadcast_multiply_fusion) | data formatting | bytes 8388608 | tf_op jit(solution)/shard_map/mul | solution.py:160
  72.8 0.1 broadcast_add_fusion
  72.9 0.2 add.223
  73.1 0.2 add.224
  73.5 0.9 fusion.25
  74.4 0.2 slice_reduce_fusion
  74.6 0.1 iota_compare_fusion.3
  74.7 0.1 lt.89
  74.8 0.3 reduce-window.9
  75.1 0.1 slice.86
  75.2 0.1 slice_reduce_fusion.6
  75.4 0.1 broadcast_in_dim.210
  75.6 0.2 fusion.58
  75.8 0.1 copy.27
  75.9 0.2 select_reduce_fusion.2
  76.1 0.2 fusion.43
  76.3 0.1 broadcast_compare_fusion.1
  76.4 0.6 gather_fusion
  77.1 0.1 iota_compare_fusion.4
  77.1 0.2 select_reduce_fusion
  77.4 0.2 slice_reduce_fusion.3
  77.8 2.3 %gather_fusion.1 = bf16[6,32,1152]{2,1,0:T(8,128)(2,1)S(1)} fusion(bf16[32,32,1152]{2,1,0:T(8,128)(2,1)} %collective-permute-done.2, s32[1024]{0:T(1024)S(1)} %pad_clamp_fusion), kind=kCustom, calls=%fused_computation.1.clone | custom fusion | bytes 884760 | tf_op jit(solution)/shard_map/jit(_take)/gather | solution.py:152
  80.0 0.1 fusion.19
  80.2 2.9 %fusion.1 = f32[3,32,1024]{2,1,0:T(8,128)S(1)} fusion(bf16[6,32,1024]{2,1,0:T(8,128)(2,1)S(1)} %fusion.19, s32[3,1024]{1,0:T(4,128)S(1)} %broadcast_subtract_fusion, s32[1024]{0:T(1024)S(1)} %get-tuple-element.63, s32[3,1024]{1,0:T(4,128)S(1)} %broadcast_subtract_fusion.1, s32[1024]{0:T(1024)S(1)} %get-tuple-element.64), kind=kOutput, calls=%fused_computation.8 | convolution fusion | flops 210763776 | bytes 819200 | tf_op jit(solution)/shard_map/pxc,pyc->pxy/dot_general | solution.py:45
  83.0 0.4 fusion.22
  83.4 0.6 convolution_bitcast_fusion.1
  84.1 2.6 %convolution_multiply_fusion.1 = f32[3,32,1024]{2,1,0:T(8,128)S(1)} fusion(f32[3,32,1024]{2,1,0:T(8,128)S(1)} %convolution_bitcast_fusion.1, f32[1024,1024,1]{1,0,2:T(8,128)S(1)} %copy-done, f32[32,1024]{1,0:T(8,128)S(1)} %add_divide_fusion), kind=kOutput, calls=%fused_computation.21 | convolution fusion | flops 1208057856 | bytes 5111808 | tf_op jit(solution)/shard_map/dot_general | solution.py:67
  86.6 0.6 convolution_bitcast_fusion
  87.2 2.6 %fusion.60 = (f32[3,32,1024]{2,1,0:T(8,128)S(1)}, f32[3,32,1024]{2,1,0:T(8,128)S(1)}) fusion(f32[3,32,1024]{2,1,0:T(8,128)S(1)} %fusion.22, f32[3]{0:T(128)S(1)} %get-tuple-element.56, f32[3,32,1024]{2,1,0:T(8,128)S(1)} %convolution_bitcast_fusion, f32[1024,1024,1]{1,0,2:T(8,128)S(1)} %copy-done), kind=kOutput, calls=%fused_computation.173 | convolution fusion | flops 1208156160 | bytes 5767180 | tf_op jit(solution)/shard_map/dot_general | solution.py:67
  89.8 0.4 reduce-precision_convert_fusion.1
  90.2 3.3 %fusion = f32[3,96,1024]{2,1,0:T(8,128)S(1)} fusion(s32[3,1024]{1,0:T(4,128)S(1)} %broadcast_subtract_fusion, s32[1024]{0:T(1024)S(1)} %get-tuple-element.63, s32[3,1024]{1,0:T(4,128)S(1)} %broadcast_subtract_fusion.1, s32[1024]{0:T(1024)S(1)} %get-tuple-element.64, bf16[3,32,1024]{2,1,0:T(8,128)(2,1)S(1)} %get-tuple-element.46, ...), kind=kOutput, calls=%fused_computation.7 | convolution fusion | flops 615186432 | bytes 1802240 | tf_op jit(solution)/shard_map/pxc,pcy->pxy/dot_general | solution.py:56
  93.4 0.9 broadcast_select_fusion.2
  94.4 2.9 %collective-permute-start.4 = (f32[3,32,1024]{2,1,0:T(8,128)}, f32[3,32,1024]{2,1,0:T(8,128)}, u32[]{:S(2)}, u32[]{:S(2)}) collective-permute-start(f32[3,32,1024]{2,1,0:T(8,128)} %get-tuple-element.39), channel_id=1, source_target_pairs={{0,32},{32,64},{64,96},{96,128},{128,160},{160,192},{192,224},{224... | collective-permute-start | bytes 1179656 | tf_op jit(solution)/shard_map/ppermute | solution.py:14
  97.3 2.9 %collective-permute-start.3 = (s32[3]{0:T(128)S(1)}, s32[3]{0:T(128)S(1)}, u32[]{:S(2)}, u32[]{:S(2)}) collective-permute-start(s32[3]{0:T(128)S(1)} %get-tuple-element.31), channel_id=1, source_target_pairs={{0,32},{32,64},{64,96},{96,128},{128,160},{160,192},{192,224},{224... | collective-permute-start | bytes 44 | tf_op jit(solution)/shard_map/ppermute | solution.py:14
  100.2 0.1 copy.29
  100.3 0.1 copy.30
  100.4 0.1 fusion.50
  100.5 1.1 fusion.10
  101.6 0.2 broadcast_in_dim.204
  101.9 2.2 %scatter_fusion = f32[16,32,1024]{2,1,0:T(8,128)S(1)} fusion(f32[16,32,1024]{2,1,0:T(8,128)S(1)} %broadcast_in_dim.204, s32[6]{0:T(128)S(1)} %fusion.50, f32[6,32,1024]{2,1,0:T(8,128)} %get-tuple-element.42), kind=kCustom, calls=%fused_computation.2 | custom fusion | flops 196608 | bytes 2359320 | tf_op jit(solution)/shard_map/scatter-add | solution.py:183
  104.1 5.7 %collective-permute-done.3 = s32[3]{0:T(128)S(1)} collective-permute-done((s32[3]{0:T(128)S(1)}, s32[3]{0:T(128)S(1)}, u32[]{:S(2)}, u32[]{:S(2)}) %collective-permute-start.3) | collective-permute-done | bytes 44 | tf_op jit(solution)/shard_map/ppermute | solution.py:14
  109.8 1.9 %broadcast_select_fusion = (f32[3,32,1024]{2,1,0:T(8,128)S(1)}, f32[3,32,1024]{2,1,0:T(8,128)}) fusion(f32[3,32,1024]{2,1,0:T(8,128)} %collective-permute-done.4, pred[3]{0:T(512)(128)(4,1)S(1)} %get-tuple-element.27, pred[3]{0:T(512)(128)(4,1)S(1)} %broadcast_compare_fusion.2), kind=kLoop, calls=%fused_computation.43 | loop fusion | flops 196608 | bytes 1179654 | tf_op jit(solution)/shard_map/jit(_where)/select_n | solution.py:182
  111.7 1.7 %scatter_fusion.1 = f32[16,32,1024]{2,1,0:T(8,128)S(1)} fusion(f32[16,32,1024]{2,1,0:T(8,128)S(1)} %scatter_fusion, s32[3]{0:T(128)S(1)} %compare_select_fusion.2, f32[3,32,1024]{2,1,0:T(8,128)} %get-tuple-element.44), kind=kCustom, calls=%fused_computation.3 | custom fusion | flops 98304 | bytes 1179660 | tf_op jit(solution)/shard_map/scatter-add | solution.py:183
  113.5 1.9 %collective-permute-start.5 = (f32[16,32,1024]{2,1,0:T(8,128)S(1)}, f32[16,32,1024]{2,1,0:T(8,128)}, u32[]{:S(2)}, u32[]{:S(2)}) collective-permute-start(f32[16,32,1024]{2,1,0:T(8,128)S(1)} %scatter_fusion.1), channel_id=1, source_target_pairs={{0,1},{1,0},{2,3},{3,2},{4,5},{5,4},{6,7},{7,6},{8,9},{9,8},{10,11... | collective-permute-start | bytes 6291464 | tf_op jit(solution)/shard_map/ppermute | solution.py:190
  115.4 4.3 %collective-permute-done.5 = f32[16,32,1024]{2,1,0:T(8,128)} collective-permute-done((f32[16,32,1024]{2,1,0:T(8,128)S(1)}, f32[16,32,1024]{2,1,0:T(8,128)}, u32[]{:S(2)}, u32[]{:S(2)}) %collective-permute-start.5) | collective-permute-done | bytes 2097184 | tf_op jit(solution)/shard_map/ppermute | solution.py:190
  119.7 3.0 %scatter_fusion.2 = f32[16,32,1024]{2,1,0:T(8,128)} fusion(f32[16,32,1024]{2,1,0:T(8,128)} %collective-permute-done.5, s32[6]{0:T(128)S(1)} %fusion.50, f32[6,32,1024]{2,1,0:T(8,128)S(1)} %get-tuple-element.41), kind=kCustom, calls=%fused_computation.4 | custom fusion | flops 196608 | bytes 2359320 | tf_op jit(solution)/shard_map/scatter-add | solution.py:183
  122.7 2.5 %scatter_fusion.3 = f32[16,32,1024]{2,1,0:T(8,128)} fusion(f32[16,32,1024]{2,1,0:T(8,128)} %scatter_fusion.2, s32[3]{0:T(128)S(1)} %compare_select_fusion.2, f32[3,32,1024]{2,1,0:T(8,128)S(1)} %get-tuple-element.43), kind=kCustom, calls=%fused_computation.5 | custom fusion | flops 98304 | bytes 1179660 | tf_op jit(solution)/shard_map/scatter-add | solution.py:183
  125.1 32.8 %all_to_all.11 = f32[16,32,1024]{2,1,0:T(8,128)S(1)} all-to-all(f32[16,32,1024]{2,1,0:T(8,128)} %scatter_fusion.3), channel_id=1, replica_groups=mesh['grp'=16,'yx'=16,'core'=2] {'yx'}, dimensions={0} | all-to-all | bytes 4194304 | tf_op jit(solution)/shard_map/all_to_all | solution.py:191
  158.0 0.8 reduce_sum.39
  (35 shorter events, 0.8 us)
Async XLA Ops:
  0.0 6.4 %collective-permute-start = (bf16[1,32,1024]{2,1,0:T(8,128)(2,1)}, bf16[1,32,1024]{2,1,0:T(8,128)(2,1)S(1)}, u32[]{:S(2)}, u32[]{:S(2)}) collective-permute-start(bf16[1,32,1024]{2,1,0:T(8,128)(2,1)} %param.8), channel_id=1, source_target_pairs={{32,0},{64,32},{96,64},{128,96},{160,128},{192,160},{224,192},{256... | collective-permute-start | bytes 196616 | tf_op jit(solution)/shard_map/ppermute | solution.py:14
  7.2 3.2 %collective-permute-start.1 = (bf16[32,1152]{1,0:T(8,128)(2,1)S(1)}, bf16[32,1152]{1,0:T(8,128)(2,1)S(1)}, u32[]{:S(2)}, u32[]{:S(2)}) collective-permute-start(bf16[32,1152]{1,0:T(8,128)(2,1)S(1)} %get-tuple-element.49), channel_id=1, source_target_pairs={{0,1},{1,0},{2,3},{3,2},{4,5},{5,4},{6,7},{7,6},{8,9},{9,8},{10,11... | collective-permute-start | bytes 221192 | tf_op jit(solution)/shard_map/ppermute | solution.py:115
  49.0 24.4 %collective-permute-start.2 = (bf16[32,32,1152]{2,1,0:T(8,128)(2,1)S(1)}, bf16[32,32,1152]{2,1,0:T(8,128)(2,1)}, u32[]{:S(2)}, u32[]{:S(2)}) collective-permute-start(bf16[32,32,1152]{2,1,0:T(8,128)(2,1)S(1)} %bitcast.37), channel_id=1, source_target_pairs={{0,1},{1,0},{2,3},{3,2},{4,5},{5,4},{6,7},{7,6},{8,9},{9,8},{10,11... | collective-permute-start | bytes 7077896 | tf_op jit(solution)/shard_map/ppermute | solution.py:121
  72.8 4.4 %copy-start.1 = (s32[512,3]{0,1:T(4,128)S(1)}, s32[512,3]{0,1:T(4,128)}, u32[]{:S(2)}) copy-start(s32[512,3]{0,1:T(4,128)} %param.9) | copy-start | bytes 18436
  80.2 3.9 %copy-start = (f32[1024,1024,1]{1,0,2:T(8,128)S(1)}, f32[1024,1024,1]{1,0,2:T(8,128)}, u32[]{:S(2)}) copy-start(f32[1024,1024,1]{1,0,2:T(8,128)} %reshape.808) | copy-start | bytes 12582916
  94.4 15.5 %collective-permute-start.4 = (f32[3,32,1024]{2,1,0:T(8,128)}, f32[3,32,1024]{2,1,0:T(8,128)}, u32[]{:S(2)}, u32[]{:S(2)}) collective-permute-start(f32[3,32,1024]{2,1,0:T(8,128)} %get-tuple-element.39), channel_id=1, source_target_pairs={{0,32},{32,64},{64,96},{96,128},{128,160},{160,192},{192,224},{224... | collective-permute-start | bytes 1179656 | tf_op jit(solution)/shard_map/ppermute | solution.py:14
  97.3 12.5 %collective-permute-start.3 = (s32[3]{0:T(128)S(1)}, s32[3]{0:T(128)S(1)}, u32[]{:S(2)}, u32[]{:S(2)}) collective-permute-start(s32[3]{0:T(128)S(1)} %get-tuple-element.31), channel_id=1, source_target_pairs={{0,32},{32,64},{64,96},{96,128},{128,160},{160,192},{192,224},{224... | collective-permute-start | bytes 44 | tf_op jit(solution)/shard_map/ppermute | solution.py:14
  113.5 6.2 %collective-permute-start.5 = (f32[16,32,1024]{2,1,0:T(8,128)S(1)}, f32[16,32,1024]{2,1,0:T(8,128)}, u32[]{:S(2)}, u32[]{:S(2)}) collective-permute-start(f32[16,32,1024]{2,1,0:T(8,128)S(1)} %scatter_fusion.1), channel_id=1, source_target_pairs={{0,1},{1,0},{2,3},{3,2},{4,5},{5,4},{6,7},{7,6},{8,9},{9,8},{10,11... | collective-permute-start | bytes 6291464 | tf_op jit(solution)/shard_map/ppermute | solution.py:190

commit v8 on v7

--- a/solution.py
+++ b/solution.py
@@ -56,6 +56,20 @@
     moved = jnp.einsum("pxc,pcy->pxy", parts, plane_shift, preferred_element_type=jnp.float32)
     box_edge = fields.shape[1]
     return (moved[:, :box_edge] + moved[:, box_edge : 2 * box_edge]) + moved[:, 2 * box_edge :]
+
+
+def plane_table(sine_rows, box_edge):
+    plane = jnp.arange(box_edge * box_edge, dtype=jnp.int32)
+    cell = jnp.arange(box_edge, dtype=jnp.int32)
+
+    def spread(pick):
+        picked = pick.astype(jnp.float32)
+        rows = jnp.dot(picked, sine_rows, precision=highest)
+        return jnp.dot(rows, picked.T, precision=highest)
+
+    outer = plane[:, None] // box_edge == cell[None, :]
+    inner = plane[:, None] % box_edge == cell[None, :]
+    return spread(outer) * spread(inner)
 
 
 def solve_boxes(density, sine_rows, plane_sines, symbol):
@@ -157,9 +171,7 @@
     right_field = move_bf16(right_boxes, row_shift, plane_shift)
 
     sine_rows = sine_table(box_edge)
-    plane_sines = (sine_rows[:, None, :, None] * sine_rows[None, :, None, :]).reshape(
-        plane_size, plane_size
-    )
+    plane_sines = plane_table(sine_rows, box_edge)
     symbol = inverse_symbol(box_edge).reshape(box_edge, plane_size)
     left_field = left_boxes.astype(jnp.float32)
     potential = solve_boxes(left_field * right_field, sine_rows, plane_sines, symbol)

time: 160 us -> 145 us (0.906)
  the two profiles are of different devices: /device:TPU:384 before, /device:TPU:1 now
where the time goes in v8:
time: 145 us; the launch traced here: 142 us
  blocking collectives  65 us (45%)
  starting transfers between devices  21.9 us (15%)
  matrix products  20.5 us (14%)
  other arithmetic  18.3 us (13%)
  waiting for transfers between devices  9.31 us (6%)
  local copies, waits for them, and re-layouts  5.89 us (4%)
    all_to_all x1, blocking collectives, local(): lax.all_to_all(sent, 'yx', 0, 0, tiled=True)  33.4 us
    all_to_all x1, blocking collectives, local(): pieces = lax.all_to_all(half, 'yx', 0, 0, tiled=True)  31.6 us
    scatter-add x4, other arithmetic, add_into(): return target.at[rows // cores].add(placed)  9.46 us
    ppermute x1, starting transfers between devices, local(): got = lax.ppermute(jnp.where(first, upper_part, own_part), 'core', swap)  8.89 us
    ppermute x3, starting transfers between devices, passed_along(): lax.ppermute(value, axis, [(source, source + steps) for source in range(i...  6.82 us
    dot_general x2, matrix products, spread(): return jnp.dot(rows, picked.T, precision=highest)  6.24 us
    dot_general x2, matrix products, apply_sines(): jnp.dot(flat_rows, plane_sines, precision=highest, preferred_element_type...  5.29 us
    ppermute x3, waiting for transfers between devices, passed_along(): lax.ppermute(value, axis, [(source, source + steps) for source in range(i...  4.52 us
  transfers between devices with their start and end apart: 6, of which 4 were waited for; matrix products, arithmetic and copies ran while one was open for 9% of the time, Pallas kernels for 0%

profile of v8, /device:TPU:1, one launch (start us, length us, event | category | flops | bytes accessed | tf_op | source)
XLA Modules:
  0.0 142.0 jit_solution(5703904305225003573)
XLA Ops:
  0.0 1.3 collective-permute-start
  1.3 0.8 copy.25
  2.1 0.1 reshape_squeeze.6
  2.8 0.1 fusion.76
  2.9 0.1 fusion.71
  3.0 0.1 broadcast_select_fusion.6
  3.1 3.2 %collective-permute-done = bf16[1,32,1024]{2,1,0:T(8,128)(2,1)S(1)} collective-permute-done((bf16[1,32,1024]{2,1,0:T(8,128)(2,1)}, bf16[1,32,1024]{2,1,0:T(8,128)(2,1)S(1)}, u32[]{:S(2)}, u32[]{:S(2)}) %collective-permute-start) | collective-permute-done | bytes 65568 | tf_op jit(solution)/shard_map/ppermute | solution.py:14
  6.2 0.9 select_bitcast_fusion
  7.1 8.9 %collective-permute-start.1 = (bf16[32,1152]{1,0:T(8,128)(2,1)S(1)}, bf16[32,1152]{1,0:T(8,128)(2,1)S(1)}, u32[]{:S(2)}, u32[]{:S(2)}) collective-permute-start(bf16[32,1152]{1,0:T(8,128)(2,1)S(1)} %get-tuple-element.49), channel_id=1, source_target_pairs={{0,1},{1,0},{2,3},{3,2},{4,5},{5,4},{6,7},{7,6},{8,9},{9,8},{10,11... | collective-permute-start | bytes 221192 | tf_op jit(solution)/shard_map/ppermute | solution.py:129
  16.0 0.9 collective-permute-done.1
  16.9 0.2 broadcast_in_dim.210
  17.2 33.4 %all_to_all.10 = bf16[16,2,32,1152]{3,2,1,0:T(8,128)(2,1)S(1)} all-to-all(bf16[16,2,32,1152]{3,2,1,0:T(8,128)(2,1)S(1)} %broadcast_in_dim.210), channel_id=1, replica_groups=mesh['grp'=16,'yx'=16,'core'=2] {'yx'}, dimensions={0} | all-to-all | bytes 4718592 | tf_op jit(solution)/shard_map/all_to_all | solution.py:132
  50.6 3.4 %collective-permute-start.2 = (bf16[32,32,1152]{2,1,0:T(8,128)(2,1)S(1)}, bf16[32,32,1152]{2,1,0:T(8,128)(2,1)}, u32[]{:S(2)}, u32[]{:S(2)}) collective-permute-start(bf16[32,32,1152]{2,1,0:T(8,128)(2,1)S(1)} %bitcast.46), channel_id=1, source_target_pairs={{0,1},{1,0},{2,3},{3,2},{4,5},{5,4},{6,7},{7,6},{8,9},{9,8},{10,11... | collective-permute-start | bytes 7077896 | tf_op jit(solution)/shard_map/ppermute | solution.py:135
  54.1 0.2 add.242
  54.3 0.2 add.243
  54.7 0.6 fusion.29
  55.2 0.6 fusion.27
  55.9 2.1 %fusion.28 = f32[1024,1024]{1,0:T(8,128)S(1)} fusion(f32[1024,32]{0,1:T(8,128)S(1)} %fusion.29, s32[1024]{0:T(1024)S(1)} %get-tuple-element.64), kind=kOutput, calls=%fused_computation.41 | convolution fusion | flops 402685952 | bytes 4329472 | tf_op jit(solution)/shard_map/dot_general | solution.py:68
  57.9 4.2 %convolution_multiply_fusion = f32[1024,1024]{1,0:T(8,128)} fusion(f32[1024,1024]{1,0:T(8,128)S(1)} %fusion.28, f32[1024,32]{0,1:T(8,128)S(1)} %fusion.27, s32[1024]{0:T(1024)S(1)} %get-tuple-element.63), kind=kOutput, calls=%fused_computation.21 | convolution fusion | flops 403734528 | bytes 8523776 | tf_op jit(solution)/shard_map/dot_general | solution.py:68
  62.1 0.9 fusion.42
  63.1 0.2 slice_reduce_fusion
  63.2 0.1 iota_compare_fusion.9
  63.3 0.1 lt.97
  63.5 0.3 reduce-window.9
  63.8 0.1 slice.86
  63.9 0.1 slice_reduce_fusion.6
  64.1 0.1 broadcast_in_dim.212
  64.2 0.2 fusion.87
  64.5 0.1 copy.27
  64.6 0.2 select_reduce_fusion.2
  64.7 0.2 fusion.68
  65.0 0.1 broadcast_compare_fusion.1
  65.1 0.6 gather_fusion
  65.7 0.1 iota_compare_fusion.10
  65.8 0.2 select_reduce_fusion
  66.0 0.2 slice_reduce_fusion.3
  66.4 2.3 %gather_fusion.1 = bf16[6,32,1152]{2,1,0:T(8,128)(2,1)S(1)} fusion(bf16[32,32,1152]{2,1,0:T(8,128)(2,1)} %collective-permute-done.2, s32[1024]{0:T(1024)S(1)} %pad_clamp_fusion), kind=kCustom, calls=%fused_computation.1.clone | custom fusion | bytes 884760 | tf_op jit(solution)/shard_map/jit(_take)/gather | solution.py:166
  68.7 0.1 fusion.32
  68.8 2.9 %fusion.1 = f32[3,32,1024]{2,1,0:T(8,128)S(1)} fusion(bf16[6,32,1024]{2,1,0:T(8,128)(2,1)S(1)} %fusion.32, s32[3,1024]{1,0:T(4,128)S(1)} %broadcast_subtract_fusion, s32[1024]{0:T(1024)S(1)} %get-tuple-element.63, s32[3,1024]{1,0:T(4,128)S(1)} %broadcast_subtract_fusion.1, s32[1024]{0:T(1024)S(1)} %get-tuple-element.64), kind=kOutput, calls=%fused_computation.8 | convolution fusion | flops 210763776 | bytes 819200 | tf_op jit(solution)/shard_map/pxc,pyc->pxy/dot_general | solution.py:45
  71.7 0.4 fusion.39
  72.1 0.6 convolution_bitcast_fusion.1
  72.7 2.7 %fusion.14 = f32[3,32,1024]{2,1,0:T(8,128)S(1)} fusion(f32[3,32,1024]{2,1,0:T(8,128)S(1)} %convolution_bitcast_fusion.1, f32[1024,1024]{1,0:T(8,128)S(1)} %copy-done, f32[32,1024]{1,0:T(8,128)S(1)} %add_divide_fusion), kind=kOutput, calls=%fused_computation.24 | convolution fusion | flops 1208057856 | bytes 5111808 | tf_op jit(solution)/shard_map/dot_general | solution.py:81
  75.4 0.6 convolution_bitcast_fusion
  76.0 2.6 %fusion.89 = (f32[3,32,1024]{2,1,0:T(8,128)S(1)}, f32[3,32,1024]{2,1,0:T(8,128)S(1)}) fusion(f32[3,32,1024]{2,1,0:T(8,128)S(1)} %fusion.39, f32[3]{0:T(128)S(1)} %get-tuple-element.56, f32[3,32,1024]{2,1,0:T(8,128)S(1)} %convolution_bitcast_fusion, f32[1024,1024]{1,0:T(8,128)S(1)} %copy-done), kind=kOutput, calls=%fused_computation.198 | convolution fusion | flops 1208156160 | bytes 5767180 | tf_op jit(solution)/shard_map/dot_general | solution.py:81
  78.6 0.4 reduce-precision_convert_fusion.1
  79.0 3.0 %fusion = f32[3,96,1024]{2,1,0:T(8,128)S(1)} fusion(s32[3,1024]{1,0:T(4,128)S(1)} %broadcast_subtract_fusion, s32[1024]{0:T(1024)S(1)} %get-tuple-element.63, s32[3,1024]{1,0:T(4,128)S(1)} %broadcast_subtract_fusion.1, s32[1024]{0:T(1024)S(1)} %get-tuple-element.64, bf16[3,32,1024]{2,1,0:T(8,128)(2,1)S(1)} %get-tuple-element.46, ...), kind=kOutput, calls=%fused_computation.7 | convolution fusion | flops 615186432 | bytes 1802240 | tf_op jit(solution)/shard_map/pxc,pcy->pxy/dot_general | solution.py:56
  82.1 0.9 broadcast_select_fusion.2
  83.0 2.7 %collective-permute-start.4 = (f32[3,32,1024]{2,1,0:T(8,128)}, f32[3,32,1024]{2,1,0:T(8,128)}, u32[]{:S(2)}, u32[]{:S(2)}) collective-permute-start(f32[3,32,1024]{2,1,0:T(8,128)} %get-tuple-element.39), channel_id=1, source_target_pairs={{0,32},{32,64},{64,96},{96,128},{128,160},{160,192},{192,224},{224... | collective-permute-start | bytes 1179656 | tf_op jit(solution)/shard_map/ppermute | solution.py:14
  85.7 2.8 %collective-permute-start.3 = (s32[3]{0:T(128)S(1)}, s32[3]{0:T(128)S(1)}, u32[]{:S(2)}, u32[]{:S(2)}) collective-permute-start(s32[3]{0:T(128)S(1)} %get-tuple-element.31), channel_id=1, source_target_pairs={{0,32},{32,64},{64,96},{96,128},{128,160},{160,192},{192,224},{224... | collective-permute-start | bytes 44 | tf_op jit(solution)/shard_map/ppermute | solution.py:14
  88.5 0.1 copy.29
  88.6 0.1 copy.30
  88.7 0.1 fusion.75
  88.8 1.1 fusion.20
  89.9 0.2 broadcast_in_dim.206
  90.2 2.2 %scatter_fusion = f32[16,32,1024]{2,1,0:T(8,128)S(1)} fusion(f32[16,32,1024]{2,1,0:T(8,128)S(1)} %broadcast_in_dim.206, s32[6]{0:T(128)S(1)} %fusion.75, f32[6,32,1024]{2,1,0:T(8,128)} %get-tuple-element.42), kind=kCustom, calls=%fused_computation.2 | custom fusion | flops 196608 | bytes 2359320 | tf_op jit(solution)/shard_map/scatter-add | solution.py:195
  92.4 1.4 collective-permute-done.3
  93.8 1.9 %broadcast_select_fusion = (f32[3,32,1024]{2,1,0:T(8,128)S(1)}, f32[3,32,1024]{2,1,0:T(8,128)}) fusion(f32[3,32,1024]{2,1,0:T(8,128)} %collective-permute-done.4, pred[3]{0:T(512)(128)(4,1)S(1)} %get-tuple-element.27, pred[3]{0:T(512)(128)(4,1)S(1)} %broadcast_compare_fusion.2), kind=kLoop, calls=%fused_computation.56 | loop fusion | flops 196608 | bytes 1179654 | tf_op jit(solution)/shard_map/jit(_where)/select_n | solution.py:194
  95.7 1.7 %scatter_fusion.1 = f32[16,32,1024]{2,1,0:T(8,128)S(1)} fusion(f32[16,32,1024]{2,1,0:T(8,128)S(1)} %scatter_fusion, s32[3]{0:T(128)S(1)} %compare_select_fusion.2, f32[3,32,1024]{2,1,0:T(8,128)} %get-tuple-element.44), kind=kCustom, calls=%fused_computation.3 | custom fusion | flops 98304 | bytes 1179660 | tf_op jit(solution)/shard_map/scatter-add | solution.py:195
  97.4 2.8 %collective-permute-start.5 = (f32[16,32,1024]{2,1,0:T(8,128)S(1)}, f32[16,32,1024]{2,1,0:T(8,128)}, u32[]{:S(2)}, u32[]{:S(2)}) collective-permute-start(f32[16,32,1024]{2,1,0:T(8,128)S(1)} %scatter_fusion.1), channel_id=1, source_target_pairs={{0,1},{1,0},{2,3},{3,2},{4,5},{5,4},{6,7},{7,6},{8,9},{9,8},{10,11... | collective-permute-start | bytes 6291464 | tf_op jit(solution)/shard_map/ppermute | solution.py:202
  100.2 3.9 %collective-permute-done.5 = f32[16,32,1024]{2,1,0:T(8,128)} collective-permute-done((f32[16,32,1024]{2,1,0:T(8,128)S(1)}, f32[16,32,1024]{2,1,0:T(8,128)}, u32[]{:S(2)}, u32[]{:S(2)}) %collective-permute-start.5) | collective-permute-done | bytes 2097184 | tf_op jit(solution)/shard_map/ppermute | solution.py:202
  104.1 3.0 %scatter_fusion.2 = f32[16,32,1024]{2,1,0:T(8,128)} fusion(f32[16,32,1024]{2,1,0:T(8,128)} %collective-permute-done.5, s32[6]{0:T(128)S(1)} %fusion.75, f32[6,32,1024]{2,1,0:T(8,128)S(1)} %get-tuple-element.41), kind=kCustom, calls=%fused_computation.4 | custom fusion | flops 196608 | bytes 2359320 | tf_op jit(solution)/shard_map/scatter-add | solution.py:195
  107.2 2.5 %scatter_fusion.3 = f32[16,32,1024]{2,1,0:T(8,128)} fusion(f32[16,32,1024]{2,1,0:T(8,128)} %scatter_fusion.2, s32[3]{0:T(128)S(1)} %compare_select_fusion.2, f32[3,32,1024]{2,1,0:T(8,128)S(1)} %get-tuple-element.43), kind=kCustom, calls=%fused_computation.5 | custom fusion | flops 98304 | bytes 1179660 | tf_op jit(solution)/shard_map/scatter-add | solution.py:195
  109.6 31.6 %all_to_all.11 = f32[16,32,1024]{2,1,0:T(8,128)S(1)} all-to-all(f32[16,32,1024]{2,1,0:T(8,128)} %scatter_fusion.3), channel_id=1, replica_groups=mesh['grp'=16,'yx'=16,'core'=2] {'yx'}, dimensions={0} | all-to-all | bytes 4194304 | tf_op jit(solution)/shard_map/all_to_all | solution.py:203
  141.2 0.8 reduce_sum.39
  (36 shorter events, 0.9 us)
Async XLA Ops:
  0.0 6.2 %collective-permute-start = (bf16[1,32,1024]{2,1,0:T(8,128)(2,1)}, bf16[1,32,1024]{2,1,0:T(8,128)(2,1)S(1)}, u32[]{:S(2)}, u32[]{:S(2)}) collective-permute-start(bf16[1,32,1024]{2,1,0:T(8,128)(2,1)} %param.8), channel_id=1, source_target_pairs={{32,0},{64,32},{96,64},{128,96},{160,128},{192,160},{224,192},{256... | collective-permute-start | bytes 196616 | tf_op jit(solution)/shard_map/ppermute | solution.py:14
  7.1 9.8 %collective-permute-start.1 = (bf16[32,1152]{1,0:T(8,128)(2,1)S(1)}, bf16[32,1152]{1,0:T(8,128)(2,1)S(1)}, u32[]{:S(2)}, u32[]{:S(2)}) collective-permute-start(bf16[32,1152]{1,0:T(8,128)(2,1)S(1)} %get-tuple-element.49), channel_id=1, source_target_pairs={{0,1},{1,0},{2,3},{3,2},{4,5},{5,4},{6,7},{7,6},{8,9},{9,8},{10,11... | collective-permute-start | bytes 221192 | tf_op jit(solution)/shard_map/ppermute | solution.py:129
  50.6 11.6 %collective-permute-start.2 = (bf16[32,32,1152]{2,1,0:T(8,128)(2,1)S(1)}, bf16[32,32,1152]{2,1,0:T(8,128)(2,1)}, u32[]{:S(2)}, u32[]{:S(2)}) collective-permute-start(bf16[32,32,1152]{2,1,0:T(8,128)(2,1)S(1)} %bitcast.46), channel_id=1, source_target_pairs={{0,1},{1,0},{2,3},{3,2},{4,5},{5,4},{6,7},{7,6},{8,9},{9,8},{10,11... | collective-permute-start | bytes 7077896 | tf_op jit(solution)/shard_map/ppermute | solution.py:135
  57.9 7.9 %copy-start.1 = (s32[512,3]{0,1:T(4,128)S(1)}, s32[512,3]{0,1:T(4,128)}, u32[]{:S(2)}) copy-start(s32[512,3]{0,1:T(4,128)} %param.9) | copy-start | bytes 18436
  68.8 3.9 %copy-start = (f32[1024,1024]{1,0:T(8,128)S(1)}, f32[1024,1024]{1,0:T(8,128)}, u32[]{:S(2)}) copy-start(f32[1024,1024]{1,0:T(8,128)} %convolution_multiply_fusion) | copy-start | bytes 12582916
  83.0 10.8 %collective-permute-start.4 = (f32[3,32,1024]{2,1,0:T(8,128)}, f32[3,32,1024]{2,1,0:T(8,128)}, u32[]{:S(2)}, u32[]{:S(2)}) collective-permute-start(f32[3,32,1024]{2,1,0:T(8,128)} %get-tuple-element.39), channel_id=1, source_target_pairs={{0,32},{32,64},{64,96},{96,128},{128,160},{160,192},{192,224},{224... | collective-permute-start | bytes 1179656 | tf_op jit(solution)/shard_map/ppermute | solution.py:14
  85.7 8.0 %collective-permute-start.3 = (s32[3]{0:T(128)S(1)}, s32[3]{0:T(128)S(1)}, u32[]{:S(2)}, u32[]{:S(2)}) collective-permute-start(s32[3]{0:T(128)S(1)} %get-tuple-element.31), channel_id=1, source_target_pairs={{0,32},{32,64},{64,96},{96,128},{128,160},{160,192},{192,224},{224... | collective-permute-start | bytes 44 | tf_op jit(solution)/shard_map/ppermute | solution.py:14
  97.4 6.7 %collective-permute-start.5 = (f32[16,32,1024]{2,1,0:T(8,128)S(1)}, f32[16,32,1024]{2,1,0:T(8,128)}, u32[]{:S(2)}, u32[]{:S(2)}) collective-permute-start(f32[16,32,1024]{2,1,0:T(8,128)S(1)} %scatter_fusion.1), channel_id=1, source_target_pairs={{0,1},{1,0},{2,3},{3,2},{4,5},{5,4},{6,7},{7,6},{8,9},{9,8},{10,11... | collective-permute-start | bytes 6291464 | tf_op jit(solution)/shard_map/ppermute | solution.py:202

commit v9 on v8

--- a/solution.py
+++ b/solution.py
@@ -121,13 +121,18 @@
     cores = lax.axis_size("core")
     chips = lax.axis_size("yx")
     swap = [(0, 1), (1, 0)]
-    upper_set = passed_along(orbitals, "grp", -1)
+    groups = lax.axis_size("grp")
     own_part = jnp.concatenate([orbitals[0], table], axis=-1)
-    upper_part = jnp.concatenate([upper_set[0], jnp.zeros_like(table)], axis=-1)
+    upper_same = passed_along(orbitals, "grp", -1)[0]
+    upper_first = lax.ppermute(
+        orbitals, ("grp", "core"), [((g + 1) * cores, g * cores + 1) for g in range(groups - 1)]
+    )[0]
+    own_second = lax.ppermute(own_part, "core", [(1, 0)])
     first = core == 0
-    keep = jnp.where(first, own_part, upper_part)
-    got = lax.ppermute(jnp.where(first, upper_part, own_part), "core", swap)
-    chip_pair = jnp.where(first, jnp.stack([keep, got]), jnp.stack([got, keep]))
+    upper_pair = jnp.concatenate(
+        [jnp.stack([upper_first, upper_same]), jnp.zeros((2, box_edge, lanes), jnp.bfloat16)], axis=-1
+    )
+    chip_pair = jnp.where(first, jnp.stack([own_part, own_second]), upper_pair)
     sent = jnp.broadcast_to(chip_pair[None], (chips,) + chip_pair.shape)
     collected = lax.all_to_all(sent, "yx", 0, 0, tiled=True).reshape(
         (grp_orbs, box_edge, plane_size + lanes)

time: 145 us -> 146 us (level)
  the two profiles are of different devices: /device:TPU:1 before, /device:TPU:256 now
where the time goes in v9:
time: 146 us
  blocking collectives  70.3 us (48%)
  matrix products  20.5 us (14%)
  other arithmetic  18.4 us (13%)
  starting transfers between devices  14.9 us (10%)
  waiting for transfers between devices  14.7 us (10%)
  local copies, waits for them, and re-layouts  5.89 us (4%)
    all_to_all x1, blocking collectives, local(): lax.all_to_all(sent, 'yx', 0, 0, tiled=True)  37.7 us
    all_to_all x1, blocking collectives, local(): pieces = lax.all_to_all(half, 'yx', 0, 0, tiled=True)  32.6 us
    ppermute x3, waiting for transfers between devices, passed_along(): lax.ppermute(value, axis, [(source, source + steps) for source in range(i...  10.2 us
    scatter-add x4, other arithmetic, add_into(): return target.at[rows // cores].add(placed)  9.55 us
    ppermute x3, starting transfers between devices, passed_along(): lax.ppermute(value, axis, [(source, source + steps) for source in range(i...  7.03 us
    dot_general x2, matrix products, spread(): return jnp.dot(rows, picked.T, precision=highest)  6.24 us
    dot_general x2, matrix products, apply_sines(): jnp.dot(flat_rows, plane_sines, precision=highest, preferred_element_type...  5.29 us
    ppermute x1, waiting for transfers between devices, local(): half = mine + lax.ppermute(theirs, 'core', [(0, 1), (1, 0)])  4.26 us
  transfers between devices with their start and end apart: 7, of which 4 were waited for; matrix products, arithmetic and copies ran while one was open for 8% of the time, Pallas kernels for 0%

profile of v9, /device:TPU:256, one launch (start us, length us, event | category | flops | bytes accessed | tf_op | source)
XLA Modules:
  0.0 145.7 jit_solution(1325887654014636269)
XLA Ops:
  0.0 0.8 copy.25
  0.8 0.1 reshape_squeeze.6
  1.5 0.1 fusion.80
  1.6 0.1 fusion.75
  1.7 0.1 broadcast_select_fusion.5
  1.8 0.9 fusion.91
  2.6 1.3 collective-permute-start
  3.9 2.7 %collective-permute-start.1 = (bf16[1,32,1024]{2,1,0:T(8,128)(2,1)}, bf16[1,32,1024]{2,1,0:T(8,128)(2,1)S(1)}, u32[]{:S(2)}, u32[]{:S(2)}) collective-permute-start(bf16[1,32,1024]{2,1,0:T(8,128)(2,1)} %param.8), channel_id=1, source_target_pairs={{32,1},{64,33},{96,65},{128,97},{160,129},{192,161},{224,193},{256... | collective-permute-start | bytes 196616 | tf_op jit(solution)/shard_map/ppermute | solution.py:127
  6.7 2.0 %collective-permute-start.2 = (bf16[1,32,1024]{2,1,0:T(8,128)(2,1)}, bf16[1,32,1024]{2,1,0:T(8,128)(2,1)S(1)}, u32[]{:S(2)}, u32[]{:S(2)}) collective-permute-start(bf16[1,32,1024]{2,1,0:T(8,128)(2,1)} %param.8), channel_id=1, source_target_pairs={{32,0},{64,32},{96,64},{128,96},{160,128},{192,160},{224,192},{256... | collective-permute-start | bytes 196616 | tf_op jit(solution)/shard_map/ppermute | solution.py:14
  8.7 0.2 collective-permute-done.1
  8.9 4.2 %collective-permute-done.2 = bf16[1,32,1024]{2,1,0:T(8,128)(2,1)S(1)} collective-permute-done((bf16[1,32,1024]{2,1,0:T(8,128)(2,1)}, bf16[1,32,1024]{2,1,0:T(8,128)(2,1)S(1)}, u32[]{:S(2)}, u32[]{:S(2)}) %collective-permute-start.2) | collective-permute-done | bytes 65568 | tf_op jit(solution)/shard_map/ppermute | solution.py:14
  13.1 0.2 broadcast_in_dim.210
  13.3 37.7 %all_to_all.10 = bf16[16,2,32,1152]{3,2,1,0:T(8,128)(2,1)S(1)} all-to-all(bf16[16,2,32,1152]{3,2,1,0:T(8,128)(2,1)S(1)} %broadcast_in_dim.210), channel_id=1, replica_groups=mesh['grp'=16,'yx'=16,'core'=2] {'yx'}, dimensions={0} | all-to-all | bytes 4718592 | tf_op jit(solution)/shard_map/all_to_all | solution.py:137
  51.0 1.9 %collective-permute-start.3 = (bf16[32,32,1152]{2,1,0:T(8,128)(2,1)S(1)}, bf16[32,32,1152]{2,1,0:T(8,128)(2,1)}, u32[]{:S(2)}, u32[]{:S(2)}) collective-permute-start(bf16[32,32,1152]{2,1,0:T(8,128)(2,1)S(1)} %bitcast.45), channel_id=1, source_target_pairs={{0,1},{1,0},{2,3},{3,2},{4,5},{5,4},{6,7},{7,6},{8,9},{9,8},{10,11... | collective-permute-start | bytes 7077896 | tf_op jit(solution)/shard_map/ppermute | solution.py:140
  53.1 0.2 add.242
  53.3 0.2 add.243
  53.6 0.6 fusion.29
  54.2 0.6 fusion.27
  54.8 2.1 %fusion.28 = f32[1024,1024]{1,0:T(8,128)S(1)} fusion(f32[1024,32]{0,1:T(8,128)S(1)} %fusion.29, s32[1024]{0:T(1024)S(1)} %get-tuple-element.64), kind=kOutput, calls=%fused_computation.41 | convolution fusion | flops 402685952 | bytes 4329472 | tf_op jit(solution)/shard_map/dot_general | solution.py:68
  56.9 4.2 %convolution_multiply_fusion = f32[1024,1024]{1,0:T(8,128)} fusion(f32[1024,1024]{1,0:T(8,128)S(1)} %fusion.28, f32[1024,32]{0,1:T(8,128)S(1)} %fusion.27, s32[1024]{0:T(1024)S(1)} %get-tuple-element.63), kind=kOutput, calls=%fused_computation.21 | convolution fusion | flops 403734528 | bytes 8523776 | tf_op jit(solution)/shard_map/dot_general | solution.py:68
  61.1 0.9 fusion.46
  62.0 0.2 slice_reduce_fusion
  62.2 0.1 iota_compare_fusion.10
  62.3 0.1 lt.97
  62.4 0.3 reduce-window.9
  62.8 0.1 slice_reduce_fusion.6
  63.0 0.1 broadcast_in_dim.212
  63.2 0.2 fusion.92
  63.4 0.1 copy.27
  63.5 0.2 select_reduce_fusion.2
  63.7 0.2 fusion.72
  64.0 0.1 broadcast_compare_fusion.1
  64.1 0.6 gather_fusion
  64.7 0.1 iota_compare_fusion.11
  64.8 0.2 select_reduce_fusion
  65.0 0.2 slice_reduce_fusion.3
  65.4 2.3 %gather_fusion.1 = bf16[6,32,1152]{2,1,0:T(8,128)(2,1)S(1)} fusion(bf16[32,32,1152]{2,1,0:T(8,128)(2,1)} %collective-permute-done.3, s32[1024]{0:T(1024)S(1)} %pad_clamp_fusion), kind=kCustom, calls=%fused_computation.1.clone | custom fusion | bytes 884760 | tf_op jit(solution)/shard_map/jit(_take)/gather | solution.py:171
  67.7 0.1 fusion.32
  67.8 2.9 %fusion.1 = f32[3,32,1024]{2,1,0:T(8,128)S(1)} fusion(bf16[6,32,1024]{2,1,0:T(8,128)(2,1)S(1)} %fusion.32, s32[3,1024]{1,0:T(4,128)S(1)} %broadcast_subtract_fusion, s32[1024]{0:T(1024)S(1)} %get-tuple-element.63, s32[3,1024]{1,0:T(4,128)S(1)} %broadcast_subtract_fusion.1, s32[1024]{0:T(1024)S(1)} %get-tuple-element.64), kind=kOutput, calls=%fused_computation.8 | convolution fusion | flops 210763776 | bytes 819200 | tf_op jit(solution)/shard_map/pxc,pyc->pxy/dot_general | solution.py:45
  70.7 0.4 fusion.43
  71.0 0.6 convolution_bitcast_fusion.1
  71.7 2.7 %fusion.14 = f32[3,32,1024]{2,1,0:T(8,128)S(1)} fusion(f32[3,32,1024]{2,1,0:T(8,128)S(1)} %convolution_bitcast_fusion.1, f32[1024,1024]{1,0:T(8,128)S(1)} %copy-done, f32[32,1024]{1,0:T(8,128)S(1)} %add_divide_fusion), kind=kOutput, calls=%fused_computation.24 | convolution fusion | flops 1208057856 | bytes 5111808 | tf_op jit(solution)/shard_map/dot_general | solution.py:81
  74.4 0.6 convolution_bitcast_fusion
  75.0 2.6 %fusion.94 = (f32[3,32,1024]{2,1,0:T(8,128)S(1)}, f32[3,32,1024]{2,1,0:T(8,128)S(1)}) fusion(f32[3,32,1024]{2,1,0:T(8,128)S(1)} %fusion.43, f32[3]{0:T(128)S(1)} %get-tuple-element.56, f32[3,32,1024]{2,1,0:T(8,128)S(1)} %convolution_bitcast_fusion, f32[1024,1024]{1,0:T(8,128)S(1)} %copy-done), kind=kOutput, calls=%fused_computation.201 | convolution fusion | flops 1208156160 | bytes 5767180 | tf_op jit(solution)/shard_map/dot_general | solution.py:81
  77.6 0.4 reduce-precision_convert_fusion.1
  78.0 3.0 %fusion = f32[3,96,1024]{2,1,0:T(8,128)S(1)} fusion(s32[3,1024]{1,0:T(4,128)S(1)} %broadcast_subtract_fusion, s32[1024]{0:T(1024)S(1)} %get-tuple-element.63, s32[3,1024]{1,0:T(4,128)S(1)} %broadcast_subtract_fusion.1, s32[1024]{0:T(1024)S(1)} %get-tuple-element.64, bf16[3,32,1024]{2,1,0:T(8,128)(2,1)S(1)} %get-tuple-element.46, ...), kind=kOutput, calls=%fused_computation.7 | convolution fusion | flops 615186432 | bytes 1802240 | tf_op jit(solution)/shard_map/pxc,pcy->pxy/dot_general | solution.py:56
  81.0 0.9 broadcast_select_fusion.2
  82.0 2.1 %collective-permute-start.5 = (f32[3,32,1024]{2,1,0:T(8,128)}, f32[3,32,1024]{2,1,0:T(8,128)}, u32[]{:S(2)}, u32[]{:S(2)}) collective-permute-start(f32[3,32,1024]{2,1,0:T(8,128)} %get-tuple-element.39), channel_id=1, source_target_pairs={{0,32},{32,64},{64,96},{96,128},{128,160},{160,192},{192,224},{224... | collective-permute-start | bytes 1179656 | tf_op jit(solution)/shard_map/ppermute | solution.py:14
  84.0 2.9 %collective-permute-start.4 = (s32[3]{0:T(128)S(1)}, s32[3]{0:T(128)S(1)}, u32[]{:S(2)}, u32[]{:S(2)}) collective-permute-start(s32[3]{0:T(128)S(1)} %get-tuple-element.31), channel_id=1, source_target_pairs={{0,32},{32,64},{64,96},{96,128},{128,160},{160,192},{192,224},{224... | collective-permute-start | bytes 44 | tf_op jit(solution)/shard_map/ppermute | solution.py:14
  87.0 0.1 copy.29
  87.1 0.1 copy.30
  87.2 0.1 fusion.79
  87.3 1.1 fusion.20
  88.4 0.2 broadcast_in_dim.206
  88.6 2.2 %scatter_fusion = f32[16,32,1024]{2,1,0:T(8,128)S(1)} fusion(f32[16,32,1024]{2,1,0:T(8,128)S(1)} %broadcast_in_dim.206, s32[6]{0:T(128)S(1)} %fusion.79, f32[6,32,1024]{2,1,0:T(8,128)} %get-tuple-element.42), kind=kCustom, calls=%fused_computation.2 | custom fusion | flops 196608 | bytes 2359320 | tf_op jit(solution)/shard_map/scatter-add | solution.py:200
  90.8 6.1 %collective-permute-done.4 = s32[3]{0:T(128)S(1)} collective-permute-done((s32[3]{0:T(128)S(1)}, s32[3]{0:T(128)S(1)}, u32[]{:S(2)}, u32[]{:S(2)}) %collective-permute-start.4) | collective-permute-done | bytes 44 | tf_op jit(solution)/shard_map/ppermute | solution.py:14
  97.0 1.9 %broadcast_select_fusion = (f32[3,32,1024]{2,1,0:T(8,128)S(1)}, f32[3,32,1024]{2,1,0:T(8,128)}) fusion(f32[3,32,1024]{2,1,0:T(8,128)} %collective-permute-done.5, pred[3]{0:T(512)(128)(4,1)S(1)} %get-tuple-element.27, pred[3]{0:T(512)(128)(4,1)S(1)} %broadcast_compare_fusion.2), kind=kLoop, calls=%fused_computation.59 | loop fusion | flops 196608 | bytes 1179654 | tf_op jit(solution)/shard_map/jit(_where)/select_n | solution.py:199
  98.8 1.7 %scatter_fusion.1 = f32[16,32,1024]{2,1,0:T(8,128)S(1)} fusion(f32[16,32,1024]{2,1,0:T(8,128)S(1)} %scatter_fusion, s32[3]{0:T(128)S(1)} %compare_select_fusion.2, f32[3,32,1024]{2,1,0:T(8,128)} %get-tuple-element.44), kind=kCustom, calls=%fused_computation.3 | custom fusion | flops 98304 | bytes 1179660 | tf_op jit(solution)/shard_map/scatter-add | solution.py:200
  100.6 1.9 %collective-permute-start.6 = (f32[16,32,1024]{2,1,0:T(8,128)S(1)}, f32[16,32,1024]{2,1,0:T(8,128)}, u32[]{:S(2)}, u32[]{:S(2)}) collective-permute-start(f32[16,32,1024]{2,1,0:T(8,128)S(1)} %scatter_fusion.1), channel_id=1, source_target_pairs={{0,1},{1,0},{2,3},{3,2},{4,5},{5,4},{6,7},{7,6},{8,9},{9,8},{10,11... | collective-permute-start | bytes 6291464 | tf_op jit(solution)/shard_map/ppermute | solution.py:207
  102.5 4.3 %collective-permute-done.6 = f32[16,32,1024]{2,1,0:T(8,128)} collective-permute-done((f32[16,32,1024]{2,1,0:T(8,128)S(1)}, f32[16,32,1024]{2,1,0:T(8,128)}, u32[]{:S(2)}, u32[]{:S(2)}) %collective-permute-start.6) | collective-permute-done | bytes 2097184 | tf_op jit(solution)/shard_map/ppermute | solution.py:207
  106.8 3.1 %scatter_fusion.2 = f32[16,32,1024]{2,1,0:T(8,128)} fusion(f32[16,32,1024]{2,1,0:T(8,128)} %collective-permute-done.6, s32[6]{0:T(128)S(1)} %fusion.79, f32[6,32,1024]{2,1,0:T(8,128)S(1)} %get-tuple-element.41), kind=kCustom, calls=%fused_computation.4 | custom fusion | flops 196608 | bytes 2359320 | tf_op jit(solution)/shard_map/scatter-add | solution.py:200
  109.9 2.5 %scatter_fusion.3 = f32[16,32,1024]{2,1,0:T(8,128)} fusion(f32[16,32,1024]{2,1,0:T(8,128)} %scatter_fusion.2, s32[3]{0:T(128)S(1)} %compare_select_fusion.2, f32[3,32,1024]{2,1,0:T(8,128)S(1)} %get-tuple-element.43), kind=kCustom, calls=%fused_computation.5 | custom fusion | flops 98304 | bytes 1179660 | tf_op jit(solution)/shard_map/scatter-add | solution.py:200
  112.4 32.6 %all_to_all.11 = f32[16,32,1024]{2,1,0:T(8,128)S(1)} all-to-all(f32[16,32,1024]{2,1,0:T(8,128)} %scatter_fusion.3), channel_id=1, replica_groups=mesh['grp'=16,'yx'=16,'core'=2] {'yx'}, dimensions={0} | all-to-all | bytes 4194304 | tf_op jit(solution)/shard_map/all_to_all | solution.py:208
  145.0 0.8 reduce_sum.39
  (38 shorter events, 1.0 us)
Async XLA Ops:
  2.6 10.4 %collective-permute-start = (bf16[32,1152]{1,0:T(8,128)(2,1)S(1)}, bf16[32,1152]{1,0:T(8,128)(2,1)S(1)}, u32[]{:S(2)}, u32[]{:S(2)}) collective-permute-start(bf16[32,1152]{1,0:T(8,128)(2,1)S(1)} %get-tuple-element.49), channel_id=1, source_target_pairs={{1,0},{3,2},{5,4},{7,6},{9,8},{11,10},{13,12},{15,14},{17,16},{19,... | collective-permute-start | bytes 221192 | tf_op jit(solution)/shard_map/ppermute | solution.py:130
  3.9 5.0 %collective-permute-start.1 = (bf16[1,32,1024]{2,1,0:T(8,128)(2,1)}, bf16[1,32,1024]{2,1,0:T(8,128)(2,1)S(1)}, u32[]{:S(2)}, u32[]{:S(2)}) collective-permute-start(bf16[1,32,1024]{2,1,0:T(8,128)(2,1)} %param.8), channel_id=1, source_target_pairs={{32,1},{64,33},{96,65},{128,97},{160,129},{192,161},{224,193},{256... | collective-permute-start | bytes 196616 | tf_op jit(solution)/shard_map/ppermute | solution.py:127
  6.7 6.4 %collective-permute-start.2 = (bf16[1,32,1024]{2,1,0:T(8,128)(2,1)}, bf16[1,32,1024]{2,1,0:T(8,128)(2,1)S(1)}, u32[]{:S(2)}, u32[]{:S(2)}) collective-permute-start(bf16[1,32,1024]{2,1,0:T(8,128)(2,1)} %param.8), channel_id=1, source_target_pairs={{32,0},{64,32},{96,64},{128,96},{160,128},{192,160},{224,192},{256... | collective-permute-start | bytes 196616 | tf_op jit(solution)/shard_map/ppermute | solution.py:14
  51.0 10.1 %collective-permute-start.3 = (bf16[32,32,1152]{2,1,0:T(8,128)(2,1)S(1)}, bf16[32,32,1152]{2,1,0:T(8,128)(2,1)}, u32[]{:S(2)}, u32[]{:S(2)}) collective-permute-start(bf16[32,32,1152]{2,1,0:T(8,128)(2,1)S(1)} %bitcast.45), channel_id=1, source_target_pairs={{0,1},{1,0},{2,3},{3,2},{4,5},{5,4},{6,7},{7,6},{8,9},{9,8},{10,11... | collective-permute-start | bytes 7077896 | tf_op jit(solution)/shard_map/ppermute | solution.py:140
  56.9 7.9 %copy-start.1 = (s32[512,3]{0,1:T(4,128)S(1)}, s32[512,3]{0,1:T(4,128)}, u32[]{:S(2)}) copy-start(s32[512,3]{0,1:T(4,128)} %param.9) | copy-start | bytes 18436
  67.8 3.9 %copy-start = (f32[1024,1024]{1,0:T(8,128)S(1)}, f32[1024,1024]{1,0:T(8,128)}, u32[]{:S(2)}) copy-start(f32[1024,1024]{1,0:T(8,128)} %convolution_multiply_fusion) | copy-start | bytes 12582916
  82.0 15.0 %collective-permute-start.5 = (f32[3,32,1024]{2,1,0:T(8,128)}, f32[3,32,1024]{2,1,0:T(8,128)}, u32[]{:S(2)}, u32[]{:S(2)}) collective-permute-start(f32[3,32,1024]{2,1,0:T(8,128)} %get-tuple-element.39), channel_id=1, source_target_pairs={{0,32},{32,64},{64,96},{96,128},{128,160},{160,192},{192,224},{224... | collective-permute-start | bytes 1179656 | tf_op jit(solution)/shard_map/ppermute | solution.py:14
  84.0 12.8 %collective-permute-start.4 = (s32[3]{0:T(128)S(1)}, s32[3]{0:T(128)S(1)}, u32[]{:S(2)}, u32[]{:S(2)}) collective-permute-start(s32[3]{0:T(128)S(1)} %get-tuple-element.31), channel_id=1, source_target_pairs={{0,32},{32,64},{64,96},{96,128},{128,160},{160,192},{192,224},{224... | collective-permute-start | bytes 44 | tf_op jit(solution)/shard_map/ppermute | solution.py:14
  100.6 6.2 %collective-permute-start.6 = (f32[16,32,1024]{2,1,0:T(8,128)S(1)}, f32[16,32,1024]{2,1,0:T(8,128)}, u32[]{:S(2)}, u32[]{:S(2)}) collective-permute-start(f32[16,32,1024]{2,1,0:T(8,128)S(1)} %scatter_fusion.1), channel_id=1, source_target_pairs={{0,1},{1,0},{2,3},{3,2},{4,5},{5,4},{6,7},{7,6},{8,9},{9,8},{10,11... | collective-permute-start | bytes 6291464 | tf_op jit(solution)/shard_map/ppermute | solution.py:207

commit v10 on v8

--- a/solution.py
+++ b/solution.py
@@ -182,8 +182,14 @@
     upper = right_row >= grp_orbs
     sent_fields = jnp.where(upper[:, None, None], to_right, 0.0)
     sent_rows = jnp.where(upper, right_row - grp_orbs, 0)
-    got_fields = passed_along(sent_fields, "grp", 1)
-    got_rows = passed_along(sent_rows, "grp", 1)
+    row_block = jnp.where(
+        (jnp.arange(box_edge)[:, None] == 0) & (jnp.arange(lanes)[None, :] == 0),
+        sent_rows[:, None, None].astype(jnp.float32),
+        0.0,
+    )
+    got = passed_along(jnp.concatenate([sent_fields, row_block], axis=-1), "grp", 1)
+    got_fields = got[:, :, :plane_size]
+    got_rows = got[:, 0, plane_size].astype(jnp.int32)
 
     kept_right = jnp.where(upper[:, None, None], 0.0, to_right)
     kept_rows = jnp.where(upper, 0, right_row)

time: 145 us -> 148 us (1.021)
  waiting for transfers between devices: 9.31 us -> 13.2 us
  starting transfers between devices: 21.9 us -> 19.1 us
  other arithmetic: 18.3 us -> 20.3 us
    ppermute x3 -> x2, waiting for transfers between devices: 4.52 us -> 8.37 us  [passed_along(): lax.ppermute(value, axis, [(source, source + steps) for source in range(i...]
    ppermute x3 -> x2, starting transfers between devices: 6.82 us -> 4.03 us  [passed_along(): lax.ppermute(value, axis, [(source, source + steps) for source in range(i...]
  transfers between devices with their start and end apart: 6 -> 5, of which waited for: 4 -> 4; matrix products, arithmetic and copies ran while one was open for 9% -> 9% of each run, Pallas kernels for 0% -> 0%
where the time goes in v10:
time: 148 us; the launch traced here: 145 us
  blocking collectives  65 us (44%)
  matrix products  20.5 us (14%)
  other arithmetic  20.3 us (14%)
  starting transfers between devices  19.1 us (13%)
  waiting for transfers between devices  13.2 us (9%)
  local copies, waits for them, and re-layouts  5.89 us (4%)
    all_to_all x1, blocking collectives, local(): lax.all_to_all(sent, 'yx', 0, 0, tiled=True)  33.4 us
    all_to_all x1, blocking collectives, local(): pieces = lax.all_to_all(half, 'yx', 0, 0, tiled=True)  31.6 us
    scatter-add x4, other arithmetic, add_into(): return target.at[rows // cores].add(placed)  9.46 us
    ppermute x1, starting transfers between devices, local(): got = lax.ppermute(jnp.where(first, upper_part, own_part), 'core', swap)  8.89 us
    ppermute x2, waiting for transfers between devices, passed_along(): lax.ppermute(value, axis, [(source, source + steps) for source in range(i...  8.37 us
    dot_general x2, matrix products, spread(): return jnp.dot(rows, picked.T, precision=highest)  6.24 us
    dot_general x2, matrix products, apply_sines(): jnp.dot(flat_rows, plane_sines, precision=highest, preferred_element_type...  5.29 us
    ppermute x2, starting transfers between devices, passed_along(): lax.ppermute(value, axis, [(source, source + steps) for source in range(i...  4.03 us
  transfers between devices with their start and end apart: 5, of which 4 were waited for; matrix products, arithmetic and copies ran while one was open for 9% of the time, Pallas kernels for 0%

profile of v10, /device:TPU:1, one launch (start us, length us, event | category | flops | bytes accessed | tf_op | source)
XLA Modules:
  0.0 145.0 jit_solution(7002033098400505203)
XLA Ops:
  0.0 1.3 collective-permute-start
  1.3 0.8 copy.33
  2.1 0.1 reshape_squeeze.6
  2.8 0.1 fusion.81
  2.9 0.1 fusion.76
  3.0 0.1 broadcast_select_fusion.5
  3.1 3.2 %collective-permute-done = bf16[1,32,1024]{2,1,0:T(8,128)(2,1)S(1)} collective-permute-done((bf16[1,32,1024]{2,1,0:T(8,128)(2,1)}, bf16[1,32,1024]{2,1,0:T(8,128)(2,1)S(1)}, u32[]{:S(2)}, u32[]{:S(2)}) %collective-permute-start) | collective-permute-done | bytes 65568 | tf_op jit(solution)/shard_map/ppermute | solution.py:14
  6.2 0.9 select_bitcast_fusion
  7.1 8.9 %collective-permute-start.1 = (bf16[32,1152]{1,0:T(8,128)(2,1)S(1)}, bf16[32,1152]{1,0:T(8,128)(2,1)S(1)}, u32[]{:S(2)}, u32[]{:S(2)}) collective-permute-start(bf16[32,1152]{1,0:T(8,128)(2,1)S(1)} %get-tuple-element.49), channel_id=1, source_target_pairs={{0,1},{1,0},{2,3},{3,2},{4,5},{5,4},{6,7},{7,6},{8,9},{9,8},{10,11... | collective-permute-start | bytes 221192 | tf_op jit(solution)/shard_map/ppermute | solution.py:129
  16.0 0.9 collective-permute-done.1
  16.9 0.2 broadcast_in_dim.233
  17.2 33.4 %all_to_all.10 = bf16[16,2,32,1152]{3,2,1,0:T(8,128)(2,1)S(1)} all-to-all(bf16[16,2,32,1152]{3,2,1,0:T(8,128)(2,1)S(1)} %broadcast_in_dim.233), channel_id=1, replica_groups=mesh['grp'=16,'yx'=16,'core'=2] {'yx'}, dimensions={0} | all-to-all | bytes 4718592 | tf_op jit(solution)/shard_map/all_to_all | solution.py:132
  50.6 3.4 %collective-permute-start.2 = (bf16[32,32,1152]{2,1,0:T(8,128)(2,1)S(1)}, bf16[32,32,1152]{2,1,0:T(8,128)(2,1)}, u32[]{:S(2)}, u32[]{:S(2)}) collective-permute-start(bf16[32,32,1152]{2,1,0:T(8,128)(2,1)S(1)} %bitcast.62), channel_id=1, source_target_pairs={{0,1},{1,0},{2,3},{3,2},{4,5},{5,4},{6,7},{7,6},{8,9},{9,8},{10,11... | collective-permute-start | bytes 7077896 | tf_op jit(solution)/shard_map/ppermute | solution.py:135
  54.1 0.2 add.262
  54.3 0.2 add.263
  54.7 0.6 fusion.29
  55.3 0.6 fusion.27
  55.9 2.1 %fusion.28 = f32[1024,1024]{1,0:T(8,128)S(1)} fusion(f32[1024,32]{0,1:T(8,128)S(1)} %fusion.29, s32[1024]{0:T(1024)S(1)} %get-tuple-element.64), kind=kOutput, calls=%fused_computation.41 | convolution fusion | flops 402685952 | bytes 4329472 | tf_op jit(solution)/shard_map/dot_general | solution.py:68
  58.0 4.2 %convolution_multiply_fusion = f32[1024,1024]{1,0:T(8,128)} fusion(f32[1024,1024]{1,0:T(8,128)S(1)} %fusion.28, f32[1024,32]{0,1:T(8,128)S(1)} %fusion.27, s32[1024]{0:T(1024)S(1)} %get-tuple-element.63), kind=kOutput, calls=%fused_computation.21 | convolution fusion | flops 403734528 | bytes 8523776 | tf_op jit(solution)/shard_map/dot_general | solution.py:68
  62.2 0.9 fusion.42
  63.1 0.2 slice_reduce_fusion
  63.4 0.1 lt.104
  63.5 0.3 reduce-window.9
  63.9 0.1 slice_reduce_fusion.6
  64.1 0.1 broadcast_in_dim.235
  64.3 0.2 fusion.92
  64.5 0.1 copy.35
  64.6 0.2 select_reduce_fusion.2
  64.8 0.2 fusion.73
  65.1 0.1 broadcast_compare_fusion
  65.2 0.6 gather_fusion
  65.9 0.2 select_reduce_fusion
  66.1 0.2 slice_reduce_fusion.3
  66.5 2.3 %gather_fusion.1 = bf16[6,32,1152]{2,1,0:T(8,128)(2,1)S(1)} fusion(bf16[32,32,1152]{2,1,0:T(8,128)(2,1)} %collective-permute-done.2, s32[1024]{0:T(1024)S(1)} %pad_clamp_fusion), kind=kCustom, calls=%fused_computation.1.clone | custom fusion | bytes 884760 | tf_op jit(solution)/shard_map/jit(_take)/gather | solution.py:166
  68.8 0.1 fusion.32
  68.9 2.9 %fusion.1 = f32[3,32,1024]{2,1,0:T(8,128)S(1)} fusion(bf16[6,32,1024]{2,1,0:T(8,128)(2,1)S(1)} %fusion.32, s32[3,1024]{1,0:T(4,128)S(1)} %broadcast_subtract_fusion, s32[1024]{0:T(1024)S(1)} %get-tuple-element.63, s32[3,1024]{1,0:T(4,128)S(1)} %broadcast_subtract_fusion.1, s32[1024]{0:T(1024)S(1)} %get-tuple-element.64), kind=kOutput, calls=%fused_computation.8 | convolution fusion | flops 210763776 | bytes 819200 | tf_op jit(solution)/shard_map/pxc,pyc->pxy/dot_general | solution.py:45
  71.8 0.4 fusion.39
  72.2 0.6 convolution_bitcast_fusion.1
  72.8 2.7 %fusion.14 = f32[3,32,1024]{2,1,0:T(8,128)S(1)} fusion(f32[3,32,1024]{2,1,0:T(8,128)S(1)} %convolution_bitcast_fusion.1, f32[1024,1024]{1,0:T(8,128)S(1)} %copy-done, f32[32,1024]{1,0:T(8,128)S(1)} %add_divide_fusion), kind=kOutput, calls=%fused_computation.24 | convolution fusion | flops 1208057856 | bytes 5111808 | tf_op jit(solution)/shard_map/dot_general | solution.py:81
  75.5 0.6 convolution_bitcast_fusion
  76.1 2.6 %fusion.94 = (f32[3,32,1024]{2,1,0:T(8,128)S(1)}, f32[3,32,1024]{2,1,0:T(8,128)S(1)}) fusion(f32[3,32,1024]{2,1,0:T(8,128)S(1)} %fusion.39, f32[3]{0:T(128)S(1)} %get-tuple-element.56, f32[3,32,1024]{2,1,0:T(8,128)S(1)} %convolution_bitcast_fusion, f32[1024,1024]{1,0:T(8,128)S(1)} %copy-done), kind=kOutput, calls=%fused_computation.212 | convolution fusion | flops 1208156160 | bytes 5767180 | tf_op jit(solution)/shard_map/dot_general | solution.py:81
  78.7 0.4 reduce-precision_convert_fusion.1
  79.1 3.0 %fusion = f32[3,96,1024]{2,1,0:T(8,128)S(1)} fusion(s32[3,1024]{1,0:T(4,128)S(1)} %broadcast_subtract_fusion, s32[1024]{0:T(1024)S(1)} %get-tuple-element.63, s32[3,1024]{1,0:T(4,128)S(1)} %broadcast_subtract_fusion.1, s32[1024]{0:T(1024)S(1)} %get-tuple-element.64, bf16[3,32,1024]{2,1,0:T(8,128)(2,1)S(1)} %get-tuple-element.46, ...), kind=kOutput, calls=%fused_computation.7 | convolution fusion | flops 615186432 | bytes 1802240 | tf_op jit(solution)/shard_map/pxc,pcy->pxy/dot_general | solution.py:56
  82.1 0.1 broadcast_select_fusion
  82.4 0.8 pad_maximum_fusion.1
  83.2 2.8 %collective-permute-start.3 = (f32[3,32,1152]{2,1,0:T(8,128)}, f32[3,32,1152]{2,1,0:T(8,128)}, u32[]{:S(2)}, u32[]{:S(2)}) collective-permute-start(f32[3,32,1152]{2,1,0:T(8,128)} %pad_maximum_fusion.1), channel_id=1, source_target_pairs={{0,32},{32,64},{64,96},{96,128},{128,160},{160,192},{192,224},{224... | collective-permute-start | bytes 1327112 | tf_op jit(solution)/shard_map/ppermute | solution.py:14
  85.9 0.1 copy.37
  86.0 0.1 copy.38
  86.1 0.1 fusion.80
  86.2 1.1 fusion.20
  87.3 0.2 broadcast_in_dim.229
  87.6 2.2 %scatter_fusion = f32[16,32,1024]{2,1,0:T(8,128)S(1)} fusion(f32[16,32,1024]{2,1,0:T(8,128)S(1)} %broadcast_in_dim.229, s32[6]{0:T(128)S(1)} %fusion.80, f32[6,32,1024]{2,1,0:T(8,128)} %get-tuple-element.42), kind=kCustom, calls=%fused_computation.2 | custom fusion | flops 196608 | bytes 2359320 | tf_op jit(solution)/shard_map/scatter-add | solution.py:201
  89.8 5.2 %collective-permute-done.3 = f32[3,32,1152]{2,1,0:T(8,128)} collective-permute-done((f32[3,32,1152]{2,1,0:T(8,128)}, f32[3,32,1152]{2,1,0:T(8,128)}, u32[]{:S(2)}, u32[]{:S(2)}) %collective-permute-start.3) | collective-permute-done | bytes 442400 | tf_op jit(solution)/shard_map/ppermute | solution.py:14
  95.0 0.7 slice_convert_fusion
  95.7 0.1 fusion.70
  95.8 0.9 compare_reduce_fusion
  96.7 1.9 %slice_select_fusion.2 = (f32[3,32,1024]{2,1,0:T(8,128)S(1)}, f32[3,32,1024]{2,1,0:T(8,128)}) fusion(f32[3,32,1152]{2,1,0:T(8,128)} %collective-permute-done.3, pred[3]{0:T(512)(128)(4,1)S(1)} %get-tuple-element.27, pred[3]{0:T(512)(128)(4,1)S(1)} %get-tuple-element.28), kind=kLoop, calls=%fused_computation.53 | loop fusion | flops 196608 | bytes 1179654 | tf_op jit(solution)/shard_map/jit(_where)/select_n | solution.py:200
  98.6 1.7 %scatter_fusion.1 = f32[16,32,1024]{2,1,0:T(8,128)S(1)} fusion(f32[16,32,1024]{2,1,0:T(8,128)S(1)} %scatter_fusion, s32[3]{0:T(128)S(1)} %fusion.70, f32[3,32,1024]{2,1,0:T(8,128)} %get-tuple-element.44), kind=kCustom, calls=%fused_computation.3 | custom fusion | flops 98304 | bytes 1179660 | tf_op jit(solution)/shard_map/scatter-add | solution.py:201
  100.4 2.8 %collective-permute-start.4 = (f32[16,32,1024]{2,1,0:T(8,128)S(1)}, f32[16,32,1024]{2,1,0:T(8,128)}, u32[]{:S(2)}, u32[]{:S(2)}) collective-permute-start(f32[16,32,1024]{2,1,0:T(8,128)S(1)} %scatter_fusion.1), channel_id=1, source_target_pairs={{0,1},{1,0},{2,3},{3,2},{4,5},{5,4},{6,7},{7,6},{8,9},{9,8},{10,11... | collective-permute-start | bytes 6291464 | tf_op jit(solution)/shard_map/ppermute | solution.py:208
  103.2 3.9 %collective-permute-done.4 = f32[16,32,1024]{2,1,0:T(8,128)} collective-permute-done((f32[16,32,1024]{2,1,0:T(8,128)S(1)}, f32[16,32,1024]{2,1,0:T(8,128)}, u32[]{:S(2)}, u32[]{:S(2)}) %collective-permute-start.4) | collective-permute-done | bytes 2097184 | tf_op jit(solution)/shard_map/ppermute | solution.py:208
  107.1 3.0 %scatter_fusion.2 = f32[16,32,1024]{2,1,0:T(8,128)} fusion(f32[16,32,1024]{2,1,0:T(8,128)} %collective-permute-done.4, s32[6]{0:T(128)S(1)} %fusion.80, f32[6,32,1024]{2,1,0:T(8,128)S(1)} %get-tuple-element.41), kind=kCustom, calls=%fused_computation.4 | custom fusion | flops 196608 | bytes 2359320 | tf_op jit(solution)/shard_map/scatter-add | solution.py:201
  110.1 2.5 %scatter_fusion.3 = f32[16,32,1024]{2,1,0:T(8,128)} fusion(f32[16,32,1024]{2,1,0:T(8,128)} %scatter_fusion.2, s32[3]{0:T(128)S(1)} %fusion.70, f32[3,32,1024]{2,1,0:T(8,128)S(1)} %get-tuple-element.43), kind=kCustom, calls=%fused_computation.5 | custom fusion | flops 98304 | bytes 1179660 | tf_op jit(solution)/shard_map/scatter-add | solution.py:201
  112.6 31.6 %all_to_all.11 = f32[16,32,1024]{2,1,0:T(8,128)S(1)} all-to-all(f32[16,32,1024]{2,1,0:T(8,128)} %scatter_fusion.3), channel_id=1, replica_groups=mesh['grp'=16,'yx'=16,'core'=2] {'yx'}, dimensions={0} | all-to-all | bytes 4194304 | tf_op jit(solution)/shard_map/all_to_all | solution.py:209
  144.2 0.8 reduce_sum.39
  (38 shorter events, 1.2 us)
Async XLA Ops:
  0.0 6.2 %collective-permute-start = (bf16[1,32,1024]{2,1,0:T(8,128)(2,1)}, bf16[1,32,1024]{2,1,0:T(8,128)(2,1)S(1)}, u32[]{:S(2)}, u32[]{:S(2)}) collective-permute-start(bf16[1,32,1024]{2,1,0:T(8,128)(2,1)} %param.8), channel_id=1, source_target_pairs={{32,0},{64,32},{96,64},{128,96},{160,128},{192,160},{224,192},{256... | collective-permute-start | bytes 196616 | tf_op jit(solution)/shard_map/ppermute | solution.py:14
  7.1 9.8 %collective-permute-start.1 = (bf16[32,1152]{1,0:T(8,128)(2,1)S(1)}, bf16[32,1152]{1,0:T(8,128)(2,1)S(1)}, u32[]{:S(2)}, u32[]{:S(2)}) collective-permute-start(bf16[32,1152]{1,0:T(8,128)(2,1)S(1)} %get-tuple-element.49), channel_id=1, source_target_pairs={{0,1},{1,0},{2,3},{3,2},{4,5},{5,4},{6,7},{7,6},{8,9},{9,8},{10,11... | collective-permute-start | bytes 221192 | tf_op jit(solution)/shard_map/ppermute | solution.py:129
  50.6 11.6 %collective-permute-start.2 = (bf16[32,32,1152]{2,1,0:T(8,128)(2,1)S(1)}, bf16[32,32,1152]{2,1,0:T(8,128)(2,1)}, u32[]{:S(2)}, u32[]{:S(2)}) collective-permute-start(bf16[32,32,1152]{2,1,0:T(8,128)(2,1)S(1)} %bitcast.62), channel_id=1, source_target_pairs={{0,1},{1,0},{2,3},{3,2},{4,5},{5,4},{6,7},{7,6},{8,9},{9,8},{10,11... | collective-permute-start | bytes 7077896 | tf_op jit(solution)/shard_map/ppermute | solution.py:135
  58.0 7.9 %copy-start.1 = (s32[512,3]{0,1:T(4,128)S(1)}, s32[512,3]{0,1:T(4,128)}, u32[]{:S(2)}) copy-start(s32[512,3]{0,1:T(4,128)} %param.9) | copy-start | bytes 18436
  68.9 3.9 %copy-start = (f32[1024,1024]{1,0:T(8,128)S(1)}, f32[1024,1024]{1,0:T(8,128)}, u32[]{:S(2)}) copy-start(f32[1024,1024]{1,0:T(8,128)} %convolution_multiply_fusion) | copy-start | bytes 12582916
  83.2 11.8 %collective-permute-start.3 = (f32[3,32,1152]{2,1,0:T(8,128)}, f32[3,32,1152]{2,1,0:T(8,128)}, u32[]{:S(2)}, u32[]{:S(2)}) collective-permute-start(f32[3,32,1152]{2,1,0:T(8,128)} %pad_maximum_fusion.1), channel_id=1, source_target_pairs={{0,32},{32,64},{64,96},{96,128},{128,160},{160,192},{192,224},{224... | collective-permute-start | bytes 1327112 | tf_op jit(solution)/shard_map/ppermute | solution.py:14
  100.4 6.7 %collective-permute-start.4 = (f32[16,32,1024]{2,1,0:T(8,128)S(1)}, f32[16,32,1024]{2,1,0:T(8,128)}, u32[]{:S(2)}, u32[]{:S(2)}) collective-permute-start(f32[16,32,1024]{2,1,0:T(8,128)S(1)} %scatter_fusion.1), channel_id=1, source_target_pairs={{0,1},{1,0},{2,3},{3,2},{4,5},{5,4},{6,7},{7,6},{8,9},{9,8},{10,11... | collective-permute-start | bytes 6291464 | tf_op jit(solution)/shard_map/ppermute | solution.py:208

commit v11 on v8

--- a/solution.py
+++ b/solution.py
@@ -199,7 +199,8 @@
     empty = jnp.zeros((halves, box_edge, plane_size), jnp.float32)
     theirs = add_into(add_into(empty, fields, rows, cores - 1 - core), got_fields, got_rows, cores - 1 - core)
     mine = add_into(add_into(empty, fields, rows, core), got_fields, got_rows, core)
-    half = mine + lax.ppermute(theirs, "core", [(0, 1), (1, 0)])
+    received = lax.ppermute(theirs, "core", [(0, 1), (1, 0)])
+    half = lax.optimization_barrier(mine) + received
     pieces = lax.all_to_all(half, "yx", 0, 0, tiled=True)
     return jnp.sum(pieces, axis=0, keepdims=True)
 

time: 145 us -> 139 us (0.959)
  the two profiles are of different devices: /device:TPU:1 before, /device:TPU:384 now
where the time goes in v11:
time: 139 us; the launch traced here: 138 us
  blocking collectives  70 us (50%)
  matrix products  20.5 us (15%)
  starting transfers between devices  15.7 us (11%)
  other arithmetic  14.9 us (11%)
  waiting for transfers between devices  8.36 us (6%)
  local copies, waits for them, and re-layouts  7.51 us (5%)
    all_to_all x1, blocking collectives, local(): lax.all_to_all(sent, 'yx', 0, 0, tiled=True)  38.4 us
    all_to_all x1, blocking collectives, local(): pieces = lax.all_to_all(half, 'yx', 0, 0, tiled=True)  31.6 us
    ppermute x3, starting transfers between devices, passed_along(): lax.ppermute(value, axis, [(source, source + steps) for source in range(i...  9.97 us
    scatter-add x4, other arithmetic, add_into(): return target.at[rows // cores].add(placed)  7.43 us
    dot_general x2, matrix products, spread(): return jnp.dot(rows, picked.T, precision=highest)  6.24 us
    dot_general x2, matrix products, apply_sines(): jnp.dot(flat_rows, plane_sines, precision=highest, preferred_element_type...  5.29 us
    ppermute x3, waiting for transfers between devices, passed_along(): lax.ppermute(value, axis, [(source, source + steps) for source in range(i...  4.86 us
    dot_general x1, matrix products, unmove_f32(): jnp.einsum('pxc,pcy->pxy', parts, plane_shift, preferred_element_type=jnp...  3.05 us
  transfers between devices with their start and end apart: 6, of which 4 were waited for; matrix products, arithmetic and copies ran while one was open for 12% of the time, Pallas kernels for 0%

profile of v11, /device:TPU:384, one launch (start us, length us, event | category | flops | bytes accessed | tf_op | source)
XLA Modules:
  0.0 138.0 jit_solution(9878847248714221083)
XLA Ops:
  0.0 4.1 %collective-permute-start = (bf16[1,32,1024]{2,1,0:T(8,128)(2,1)}, bf16[1,32,1024]{2,1,0:T(8,128)(2,1)S(1)}, u32[]{:S(2)}, u32[]{:S(2)}) collective-permute-start(bf16[1,32,1024]{2,1,0:T(8,128)(2,1)} %param.8), channel_id=1, source_target_pairs={{32,0},{64,32},{96,64},{128,96},{160,128},{192,160},{224,192},{256... | collective-permute-start | bytes 196616 | tf_op jit(solution)/shard_map/ppermute | solution.py:14
  4.1 0.8 copy.25
  4.9 0.1 reshape_squeeze.6
  5.6 0.1 fusion.76
  5.7 0.1 fusion.71
  5.8 0.1 broadcast_select_fusion.6
  5.9 0.5 collective-permute-done
  6.4 0.9 select_bitcast_fusion
  7.2 1.9 %collective-permute-start.1 = (bf16[32,1152]{1,0:T(8,128)(2,1)S(1)}, bf16[32,1152]{1,0:T(8,128)(2,1)S(1)}, u32[]{:S(2)}, u32[]{:S(2)}) collective-permute-start(bf16[32,1152]{1,0:T(8,128)(2,1)S(1)} %get-tuple-element.49), channel_id=1, source_target_pairs={{0,1},{1,0},{2,3},{3,2},{4,5},{5,4},{6,7},{7,6},{8,9},{9,8},{10,11... | collective-permute-start | bytes 221192 | tf_op jit(solution)/shard_map/ppermute | solution.py:129
  9.2 1.2 collective-permute-done.1
  10.4 0.2 broadcast_in_dim.210
  10.7 38.4 %all_to_all.10 = bf16[16,2,32,1152]{3,2,1,0:T(8,128)(2,1)S(1)} all-to-all(bf16[16,2,32,1152]{3,2,1,0:T(8,128)(2,1)S(1)} %broadcast_in_dim.210), channel_id=1, replica_groups=mesh['grp'=16,'yx'=16,'core'=2] {'yx'}, dimensions={0} | all-to-all | bytes 4718592 | tf_op jit(solution)/shard_map/all_to_all | solution.py:132
  49.0 1.9 %collective-permute-start.2 = (bf16[32,32,1152]{2,1,0:T(8,128)(2,1)S(1)}, bf16[32,32,1152]{2,1,0:T(8,128)(2,1)}, u32[]{:S(2)}, u32[]{:S(2)}) collective-permute-start(bf16[32,32,1152]{2,1,0:T(8,128)(2,1)S(1)} %bitcast.46), channel_id=1, source_target_pairs={{0,1},{1,0},{2,3},{3,2},{4,5},{5,4},{6,7},{7,6},{8,9},{9,8},{10,11... | collective-permute-start | bytes 7077896 | tf_op jit(solution)/shard_map/ppermute | solution.py:135
  51.1 0.2 add.242
  51.3 0.2 add.243
  51.6 0.6 fusion.29
  52.2 0.6 fusion.27
  52.8 2.1 %fusion.28 = f32[1024,1024]{1,0:T(8,128)S(1)} fusion(f32[1024,32]{0,1:T(8,128)S(1)} %fusion.29, s32[1024]{0:T(1024)S(1)} %get-tuple-element.64), kind=kOutput, calls=%fused_computation.41 | convolution fusion | flops 402685952 | bytes 4329472 | tf_op jit(solution)/shard_map/dot_general | solution.py:68
  54.9 4.2 %convolution_multiply_fusion = f32[1024,1024]{1,0:T(8,128)} fusion(f32[1024,1024]{1,0:T(8,128)S(1)} %fusion.28, f32[1024,32]{0,1:T(8,128)S(1)} %fusion.27, s32[1024]{0:T(1024)S(1)} %get-tuple-element.63), kind=kOutput, calls=%fused_computation.21 | convolution fusion | flops 403734528 | bytes 8523776 | tf_op jit(solution)/shard_map/dot_general | solution.py:68
  59.1 0.9 fusion.42
  60.0 0.2 slice_reduce_fusion
  60.2 0.1 iota_compare_fusion.9
  60.3 0.1 lt.97
  60.4 0.3 reduce-window.9
  60.9 0.1 slice_reduce_fusion.6
  61.1 0.1 broadcast_in_dim.212
  61.2 0.2 fusion.87
  61.4 0.1 copy.27
  61.5 0.2 select_reduce_fusion.2
  61.7 0.2 fusion.68
  62.0 0.1 broadcast_compare_fusion.1
  62.1 0.6 gather_fusion
  62.8 0.2 select_reduce_fusion
  63.0 0.2 slice_reduce_fusion.3
  63.4 2.3 %gather_fusion.1 = bf16[6,32,1152]{2,1,0:T(8,128)(2,1)S(1)} fusion(bf16[32,32,1152]{2,1,0:T(8,128)(2,1)} %collective-permute-done.2, s32[1024]{0:T(1024)S(1)} %pad_clamp_fusion), kind=kCustom, calls=%fused_computation.1.clone | custom fusion | bytes 884760 | tf_op jit(solution)/shard_map/jit(_take)/gather | solution.py:166
  65.7 0.1 fusion.32
  65.8 2.8 %fusion.1 = f32[3,32,1024]{2,1,0:T(8,128)S(1)} fusion(bf16[6,32,1024]{2,1,0:T(8,128)(2,1)S(1)} %fusion.32, s32[3,1024]{1,0:T(4,128)S(1)} %broadcast_subtract_fusion, s32[1024]{0:T(1024)S(1)} %get-tuple-element.63, s32[3,1024]{1,0:T(4,128)S(1)} %broadcast_subtract_fusion.1, s32[1024]{0:T(1024)S(1)} %get-tuple-element.64), kind=kOutput, calls=%fused_computation.8 | convolution fusion | flops 210763776 | bytes 819200 | tf_op jit(solution)/shard_map/pxc,pyc->pxy/dot_general | solution.py:45
  68.7 0.4 fusion.39
  69.1 0.6 convolution_bitcast_fusion.1
  69.7 2.7 %fusion.14 = f32[3,32,1024]{2,1,0:T(8,128)S(1)} fusion(f32[3,32,1024]{2,1,0:T(8,128)S(1)} %convolution_bitcast_fusion.1, f32[1024,1024]{1,0:T(8,128)S(1)} %copy-done, f32[32,1024]{1,0:T(8,128)S(1)} %add_divide_fusion), kind=kOutput, calls=%fused_computation.24 | convolution fusion | flops 1208057856 | bytes 5111808 | tf_op jit(solution)/shard_map/dot_general | solution.py:81
  72.4 0.6 convolution_bitcast_fusion
  73.0 2.6 %fusion.89 = (f32[3,32,1024]{2,1,0:T(8,128)S(1)}, f32[3,32,1024]{2,1,0:T(8,128)S(1)}) fusion(f32[3,32,1024]{2,1,0:T(8,128)S(1)} %fusion.39, f32[3]{0:T(128)S(1)} %get-tuple-element.56, f32[3,32,1024]{2,1,0:T(8,128)S(1)} %convolution_bitcast_fusion, f32[1024,1024]{1,0:T(8,128)S(1)} %copy-done), kind=kOutput, calls=%fused_computation.198 | convolution fusion | flops 1208156160 | bytes 5767180 | tf_op jit(solution)/shard_map/dot_general | solution.py:81
  75.6 0.4 reduce-precision_convert_fusion.1
  76.0 0.1 copy.29
  76.1 0.1 copy.30
  76.2 3.0 %fusion = f32[3,96,1024]{2,1,0:T(8,128)S(1)} fusion(s32[3,1024]{1,0:T(4,128)S(1)} %broadcast_subtract_fusion, s32[1024]{0:T(1024)S(1)} %get-tuple-element.63, s32[3,1024]{1,0:T(4,128)S(1)} %broadcast_subtract_fusion.1, s32[1024]{0:T(1024)S(1)} %get-tuple-element.64, bf16[3,32,1024]{2,1,0:T(8,128)(2,1)S(1)} %get-tuple-element.46, ...), kind=kOutput, calls=%fused_computation.7 | convolution fusion | flops 615186432 | bytes 1802240 | tf_op jit(solution)/shard_map/pxc,pcy->pxy/dot_general | solution.py:56
  79.2 0.1 broadcast_select_fusion.2
  79.4 2.9 %collective-permute-start.4 = (f32[3,32,1024]{2,1,0:T(8,128)S(1)}, f32[3,32,1024]{2,1,0:T(8,128)S(1)}, u32[]{:S(2)}, u32[]{:S(2)}) collective-permute-start(f32[3,32,1024]{2,1,0:T(8,128)S(1)} %get-tuple-element.39), channel_id=1, source_target_pairs={{0,32},{32,64},{64,96},{96,128},{128,160},{160,192},{192,224},{224... | collective-permute-start | bytes 1179656 | tf_op jit(solution)/shard_map/ppermute | solution.py:14
  82.3 2.9 %collective-permute-start.3 = (s32[3]{0:T(128)S(1)}, s32[3]{0:T(128)S(1)}, u32[]{:S(2)}, u32[]{:S(2)}) collective-permute-start(s32[3]{0:T(128)S(1)} %get-tuple-element.31), channel_id=1, source_target_pairs={{0,32},{32,64},{64,96},{96,128},{128,160},{160,192},{192,224},{224... | collective-permute-start | bytes 44 | tf_op jit(solution)/shard_map/ppermute | solution.py:14
  85.2 0.1 fusion.75
  85.3 0.2 fusion.20
  85.6 1.6 %broadcast_in_dim.206.clone.1 = f32[16,32,1024]{2,1,0:T(8,128)} broadcast(f32[]{:T(128)} %constant.210.clone.1), dimensions={} | broadcast | bytes 2097156 | tf_op jit(solution)/shard_map/broadcast_in_dim | solution.py:199
  87.2 3.0 %scatter_fusion.2 = f32[16,32,1024]{2,1,0:T(8,128)} fusion(f32[16,32,1024]{2,1,0:T(8,128)} %broadcast_in_dim.206.clone.1, s32[6]{0:T(128)S(1)} %fusion.75, f32[6,32,1024]{2,1,0:T(8,128)S(1)} %get-tuple-element.41), kind=kCustom, calls=%fused_computation.4 | custom fusion | flops 196608 | bytes 2359320 | tf_op jit(solution)/shard_map/scatter-add | solution.py:195
  90.2 4.4 %collective-permute-done.3 = s32[3]{0:T(128)S(1)} collective-permute-done((s32[3]{0:T(128)S(1)}, s32[3]{0:T(128)S(1)}, u32[]{:S(2)}, u32[]{:S(2)}) %collective-permute-start.3) | collective-permute-done | bytes 44 | tf_op jit(solution)/shard_map/ppermute | solution.py:14
  94.6 0.1 broadcast_select_fusion
  94.8 2.5 %scatter_fusion.3 = f32[16,32,1024]{2,1,0:T(8,128)} fusion(f32[16,32,1024]{2,1,0:T(8,128)} %scatter_fusion.2, s32[3]{0:T(128)S(1)} %compare_select_fusion.2, f32[3,32,1024]{2,1,0:T(8,128)S(1)} %get-tuple-element.43), kind=kCustom, calls=%fused_computation.5 | custom fusion | flops 98304 | bytes 1179660 | tf_op jit(solution)/shard_map/scatter-add | solution.py:195
  97.3 1.9 %collective-permute-start.5 = (f32[16,32,1024]{2,1,0:T(8,128)}, f32[16,32,1024]{2,1,0:T(8,128)}, u32[]{:S(2)}, u32[]{:S(2)}) collective-permute-start(f32[16,32,1024]{2,1,0:T(8,128)} %scatter_fusion.3), channel_id=1, source_target_pairs={{0,1},{1,0},{2,3},{3,2},{4,5},{5,4},{6,7},{7,6},{8,9},{9,8},{10,11... | collective-permute-start | bytes 6291464 | tf_op jit(solution)/shard_map/ppermute | solution.py:202
  99.2 0.2 broadcast_in_dim.206.clone
  99.4 1.1 scatter_fusion
  100.6 0.8 scatter_fusion.1
  101.4 2.3 %collective-permute-done.5 = f32[16,32,1024]{2,1,0:T(8,128)} collective-permute-done((f32[16,32,1024]{2,1,0:T(8,128)}, f32[16,32,1024]{2,1,0:T(8,128)}, u32[]{:S(2)}, u32[]{:S(2)}) %collective-permute-start.5) | collective-permute-done | bytes 2097184 | tf_op jit(solution)/shard_map/ppermute | solution.py:202
  103.7 2.0 %add.253 = f32[16,32,1024]{2,1,0:T(8,128)S(1)} add(f32[16,32,1024]{2,1,0:T(8,128)S(1)} %scatter_fusion.1, f32[16,32,1024]{2,1,0:T(8,128)} %collective-permute-done.5) | non-fusion elementwise | flops 524288 | bytes 6291456 | tf_op jit(solution)/shard_map/add | solution.py:203
  105.6 31.6 %all_to_all.11 = f32[16,32,1024]{2,1,0:T(8,128)S(1)} all-to-all(f32[16,32,1024]{2,1,0:T(8,128)S(1)} %add.253), channel_id=1, replica_groups=mesh['grp'=16,'yx'=16,'core'=2] {'yx'}, dimensions={0} | all-to-all | bytes 4194304 | tf_op jit(solution)/shard_map/all_to_all | solution.py:204
  137.3 0.8 reduce_sum.39
  (38 shorter events, 1.0 us)
Async XLA Ops:
  0.0 6.4 %collective-permute-start = (bf16[1,32,1024]{2,1,0:T(8,128)(2,1)}, bf16[1,32,1024]{2,1,0:T(8,128)(2,1)S(1)}, u32[]{:S(2)}, u32[]{:S(2)}) collective-permute-start(bf16[1,32,1024]{2,1,0:T(8,128)(2,1)} %param.8), channel_id=1, source_target_pairs={{32,0},{64,32},{96,64},{128,96},{160,128},{192,160},{224,192},{256... | collective-permute-start | bytes 196616 | tf_op jit(solution)/shard_map/ppermute | solution.py:14
  7.2 3.2 %collective-permute-start.1 = (bf16[32,1152]{1,0:T(8,128)(2,1)S(1)}, bf16[32,1152]{1,0:T(8,128)(2,1)S(1)}, u32[]{:S(2)}, u32[]{:S(2)}) collective-permute-start(bf16[32,1152]{1,0:T(8,128)(2,1)S(1)} %get-tuple-element.49), channel_id=1, source_target_pairs={{0,1},{1,0},{2,3},{3,2},{4,5},{5,4},{6,7},{7,6},{8,9},{9,8},{10,11... | collective-permute-start | bytes 221192 | tf_op jit(solution)/shard_map/ppermute | solution.py:129
  49.0 10.1 %collective-permute-start.2 = (bf16[32,32,1152]{2,1,0:T(8,128)(2,1)S(1)}, bf16[32,32,1152]{2,1,0:T(8,128)(2,1)}, u32[]{:S(2)}, u32[]{:S(2)}) collective-permute-start(bf16[32,32,1152]{2,1,0:T(8,128)(2,1)S(1)} %bitcast.46), channel_id=1, source_target_pairs={{0,1},{1,0},{2,3},{3,2},{4,5},{5,4},{6,7},{7,6},{8,9},{9,8},{10,11... | collective-permute-start | bytes 7077896 | tf_op jit(solution)/shard_map/ppermute | solution.py:135
  54.9 7.9 %copy-start.1 = (s32[512,3]{0,1:T(4,128)S(1)}, s32[512,3]{0,1:T(4,128)}, u32[]{:S(2)}) copy-start(s32[512,3]{0,1:T(4,128)} %param.9) | copy-start | bytes 18436
  65.8 3.9 %copy-start = (f32[1024,1024]{1,0:T(8,128)S(1)}, f32[1024,1024]{1,0:T(8,128)}, u32[]{:S(2)}) copy-start(f32[1024,1024]{1,0:T(8,128)} %convolution_multiply_fusion) | copy-start | bytes 12582916
  79.4 15.3 %collective-permute-start.4 = (f32[3,32,1024]{2,1,0:T(8,128)S(1)}, f32[3,32,1024]{2,1,0:T(8,128)S(1)}, u32[]{:S(2)}, u32[]{:S(2)}) collective-permute-start(f32[3,32,1024]{2,1,0:T(8,128)S(1)} %get-tuple-element.39), channel_id=1, source_target_pairs={{0,32},{32,64},{64,96},{96,128},{128,160},{160,192},{192,224},{224... | collective-permute-start | bytes 1179656 | tf_op jit(solution)/shard_map/ppermute | solution.py:14
  82.3 12.3 %collective-permute-start.3 = (s32[3]{0:T(128)S(1)}, s32[3]{0:T(128)S(1)}, u32[]{:S(2)}, u32[]{:S(2)}) collective-permute-start(s32[3]{0:T(128)S(1)} %get-tuple-element.31), channel_id=1, source_target_pairs={{0,32},{32,64},{64,96},{96,128},{128,160},{160,192},{192,224},{224... | collective-permute-start | bytes 44 | tf_op jit(solution)/shard_map/ppermute | solution.py:14
  97.3 6.4 %collective-permute-start.5 = (f32[16,32,1024]{2,1,0:T(8,128)}, f32[16,32,1024]{2,1,0:T(8,128)}, u32[]{:S(2)}, u32[]{:S(2)}) collective-permute-start(f32[16,32,1024]{2,1,0:T(8,128)} %scatter_fusion.3), channel_id=1, source_target_pairs={{0,1},{1,0},{2,3},{3,2},{4,5},{5,4},{6,7},{7,6},{8,9},{9,8},{10,11... | collective-permute-start | bytes 6291464 | tf_op jit(solution)/shard_map/ppermute | solution.py:202

commit v12 on v11

--- a/solution.py
+++ b/solution.py
@@ -128,6 +128,9 @@
     keep = jnp.where(first, own_part, upper_part)
     got = lax.ppermute(jnp.where(first, upper_part, own_part), "core", swap)
     chip_pair = jnp.where(first, jnp.stack([keep, got]), jnp.stack([got, keep]))
+    sine_rows = sine_table(box_edge)
+    plane_sines = plane_table(sine_rows, box_edge)
+    plane_sines, chip_pair = lax.optimization_barrier((plane_sines, chip_pair))
     sent = jnp.broadcast_to(chip_pair[None], (chips,) + chip_pair.shape)
     collected = lax.all_to_all(sent, "yx", 0, 0, tiled=True).reshape(
         (grp_orbs, box_edge, plane_size + lanes)
@@ -170,8 +173,6 @@
     row_shift, plane_shift = shift_matrices(offset_diff, box_edge)
     right_field = move_bf16(right_boxes, row_shift, plane_shift)
 
-    sine_rows = sine_table(box_edge)
-    plane_sines = plane_table(sine_rows, box_edge)
     symbol = inverse_symbol(box_edge).reshape(box_edge, plane_size)
     left_field = left_boxes.astype(jnp.float32)
     potential = solve_boxes(left_field * right_field, sine_rows, plane_sines, symbol)

time: 139 us -> 144 us (1.036)
  matrix products: 20.5 us -> 24.5 us
  waiting for transfers between devices: 8.36 us -> 10.8 us
    dot_general x2, matrix products: 6.24 us -> 10.2 us  [spread(): return jnp.dot(rows, picked.T, precision=highest)]
    ppermute x1, waiting for transfers between devices: 0.01 us -> 3.75 us  [local(): other = lax.ppermute(collected, 'core', swap)]
  transfers between devices with their start and end apart: 6 -> 6, of which waited for: 4 -> 3; matrix products, arithmetic and copies ran while one was open for 12% -> 14% of each run, Pallas kernels for 0% -> 0%
where the time goes in v12:
time: 144 us; the launch traced here: 143 us
  blocking collectives  70.5 us (49%)
  matrix products  24.5 us (17%)
  starting transfers between devices  14.8 us (10%)
  other arithmetic  14.1 us (10%)
  waiting for transfers between devices  10.8 us (8%)
  local copies, waits for them, and re-layouts  7.54 us (5%)
    all_to_all x1, blocking collectives, local(): lax.all_to_all(sent, 'yx', 0, 0, tiled=True)  38.8 us
    all_to_all x1, blocking collectives, local(): pieces = lax.all_to_all(half, 'yx', 0, 0, tiled=True)  31.6 us
    dot_general x2, matrix products, spread(): return jnp.dot(rows, picked.T, precision=highest)  10.2 us
    ppermute x3, starting transfers between devices, passed_along(): lax.ppermute(value, axis, [(source, source + steps) for source in range(i...  8.76 us
    scatter-add x4, other arithmetic, add_into(): return target.at[rows // cores].add(placed)  7.41 us
    dot_general x2, matrix products, apply_sines(): jnp.dot(flat_rows, plane_sines, precision=highest, preferred_element_type...  5.12 us
    ppermute x3, waiting for transfers between devices, passed_along(): lax.ppermute(value, axis, [(source, source + steps) for source in range(i...  4.77 us
    ppermute x1, waiting for transfers between devices, local(): other = lax.ppermute(collected, 'core', swap)  3.75 us
  transfers between devices with their start and end apart: 6, of which 3 were waited for; matrix products, arithmetic and copies ran while one was open for 14% of the time, Pallas kernels for 0%

profile of v12, /device:TPU:384, one launch (start us, length us, event | category | flops | bytes accessed | tf_op | source)
XLA Modules:
  0.0 143.3 jit_solution(6321385957559506958)
XLA Ops:
  0.0 4.1 %collective-permute-start = (bf16[1,32,1024]{2,1,0:T(8,128)(2,1)}, bf16[1,32,1024]{2,1,0:T(8,128)(2,1)S(1)}, u32[]{:S(2)}, u32[]{:S(2)}) collective-permute-start(bf16[1,32,1024]{2,1,0:T(8,128)(2,1)} %param.8), channel_id=1, source_target_pairs={{32,0},{64,32},{96,64},{128,96},{160,128},{192,160},{224,192},{256... | collective-permute-start | bytes 196616 | tf_op jit(solution)/shard_map/ppermute | solution.py:14
  4.2 0.8 copy.25
  5.0 0.1 reshape_squeeze.6
  5.7 0.1 fusion.76
  5.8 0.6 fusion.29
  6.4 4.0 %fusion.28 = f32[1024,1024]{1,0:T(8,128)} fusion(f32[1024,32]{0,1:T(8,128)S(1)} %fusion.29, s32[1024]{0:T(1024)S(1)} %add_select_fusion), kind=kOutput, calls=%fused_computation.41 | convolution fusion | flops 402685952 | bytes 4329472 | tf_op jit(solution)/shard_map/dot_general | solution.py:68
  10.4 0.6 fusion.27
  10.9 0.1 fusion.71
  11.0 0.1 broadcast_select_fusion.6
  11.1 1.9 %collective-permute-start.1 = (bf16[32,1152]{1,0:T(8,128)(2,1)S(1)}, bf16[32,1152]{1,0:T(8,128)(2,1)S(1)}, u32[]{:S(2)}, u32[]{:S(2)}) collective-permute-start(bf16[32,1152]{1,0:T(8,128)(2,1)S(1)} %get-tuple-element.53), channel_id=1, source_target_pairs={{0,1},{1,0},{2,3},{3,2},{4,5},{5,4},{6,7},{7,6},{8,9},{9,8},{10,11... | collective-permute-start | bytes 221192 | tf_op jit(solution)/shard_map/ppermute | solution.py:129
  13.1 6.2 %convolution_multiply_fusion = f32[1024,1024]{1,0:T(8,128)} fusion(f32[1024,1024]{1,0:T(8,128)} %fusion.28, f32[1024,32]{0,1:T(8,128)S(1)} %fusion.27, s32[1024]{0:T(1024)S(1)} %fusion.61), kind=kOutput, calls=%fused_computation.21 | convolution fusion | flops 403734528 | bytes 8523776 | tf_op jit(solution)/shard_map/dot_general | solution.py:68
  19.3 0.2 broadcast_in_dim.210
  19.6 38.8 %all_to_all.10 = bf16[16,2,32,1152]{3,2,1,0:T(8,128)(2,1)S(1)} all-to-all(bf16[16,2,32,1152]{3,2,1,0:T(8,128)(2,1)S(1)} %broadcast_in_dim.210), channel_id=1, replica_groups=mesh['grp'=16,'yx'=16,'core'=2] {'yx'}, dimensions={0} | all-to-all | bytes 4718592 | tf_op jit(solution)/shard_map/all_to_all | solution.py:135
  58.4 2.2 %collective-permute-start.2 = (bf16[32,32,1152]{2,1,0:T(8,128)(2,1)S(1)}, bf16[32,32,1152]{2,1,0:T(8,128)(2,1)}, u32[]{:S(2)}, u32[]{:S(2)}) collective-permute-start(bf16[32,32,1152]{2,1,0:T(8,128)(2,1)S(1)} %bitcast.46), channel_id=1, source_target_pairs={{0,1},{1,0},{2,3},{3,2},{4,5},{5,4},{6,7},{7,6},{8,9},{9,8},{10,11... | collective-permute-start | bytes 7077896 | tf_op jit(solution)/shard_map/ppermute | solution.py:138
  60.8 0.2 add.242
  61.0 0.2 add.243
  61.3 3.7 %collective-permute-done.2 = bf16[32,32,1152]{2,1,0:T(8,128)(2,1)} collective-permute-done((bf16[32,32,1152]{2,1,0:T(8,128)(2,1)S(1)}, bf16[32,32,1152]{2,1,0:T(8,128)(2,1)}, u32[]{:S(2)}, u32[]{:S(2)}) %collective-permute-start.2) | collective-permute-done | bytes 2359328 | tf_op jit(solution)/shard_map/ppermute | solution.py:138
  65.1 0.9 fusion.42
  66.0 0.2 slice_reduce_fusion
  66.2 0.1 iota_compare_fusion.9
  66.3 0.1 lt.98
  66.4 0.3 reduce-window.9
  66.7 0.1 slice.86
  66.8 0.1 slice_reduce_fusion.6
  67.0 0.1 broadcast_in_dim.212
  67.2 0.2 fusion.87
  67.4 0.1 copy.27
  67.5 0.2 select_reduce_fusion.2
  67.7 0.2 fusion.68
  68.0 0.1 broadcast_compare_fusion.1
  68.1 0.6 gather_fusion
  68.8 0.2 select_reduce_fusion
  69.0 0.2 slice_reduce_fusion.3
  69.2 0.1 broadcast_subtract_fusion.1
  69.4 2.3 %gather_fusion.1 = bf16[6,32,1152]{2,1,0:T(8,128)(2,1)S(1)} fusion(bf16[32,32,1152]{2,1,0:T(8,128)(2,1)} %collective-permute-done.2, s32[1024]{0:T(1024)S(1)} %pad_clamp_fusion), kind=kCustom, calls=%fused_computation.1.clone | custom fusion | bytes 884760 | tf_op jit(solution)/shard_map/jit(_take)/gather | solution.py:169
  71.7 0.1 fusion.32
  71.9 2.9 %fusion.1 = f32[3,32,1024]{2,1,0:T(8,128)S(1)} fusion(bf16[6,32,1024]{2,1,0:T(8,128)(2,1)S(1)} %fusion.32, s32[3,1024]{1,0:T(4,128)S(1)} %broadcast_subtract_fusion, s32[1024]{0:T(1024)S(1)} %fusion.61, s32[3,1024]{1,0:T(4,128)S(1)} %broadcast_subtract_fusion.1, s32[1024]{0:T(1024)S(1)} %add_select_fusion), kind=kOutput, calls=%fused_computation.8 | convolution fusion | flops 210763776 | bytes 819200 | tf_op jit(solution)/shard_map/pxc,pyc->pxy/dot_general | solution.py:45
  74.7 0.4 fusion.39
  75.1 0.6 convolution_bitcast_fusion.1
  75.8 2.6 %fusion.14 = f32[3,32,1024]{2,1,0:T(8,128)S(1)} fusion(f32[3,32,1024]{2,1,0:T(8,128)S(1)} %convolution_bitcast_fusion.1, f32[1024,1024]{1,0:T(8,128)S(1)} %copy-done, f32[32,1024]{1,0:T(8,128)S(1)} %add_divide_fusion), kind=kOutput, calls=%fused_computation.24 | convolution fusion | flops 1208057856 | bytes 5111808 | tf_op jit(solution)/shard_map/dot_general | solution.py:81
  78.3 0.6 convolution_bitcast_fusion
  78.9 2.6 %fusion.89 = (f32[3,32,1024]{2,1,0:T(8,128)S(1)}, f32[3,32,1024]{2,1,0:T(8,128)S(1)}) fusion(f32[3,32,1024]{2,1,0:T(8,128)S(1)} %fusion.39, f32[3]{0:T(128)S(1)} %get-tuple-element.60, f32[3,32,1024]{2,1,0:T(8,128)S(1)} %convolution_bitcast_fusion, f32[1024,1024]{1,0:T(8,128)S(1)} %copy-done), kind=kOutput, calls=%fused_computation.198 | convolution fusion | flops 1208156160 | bytes 5767180 | tf_op jit(solution)/shard_map/dot_general | solution.py:81
  81.5 0.4 reduce-precision_convert_fusion.1
  81.9 0.1 copy.29
  82.0 0.1 copy.30
  82.1 3.3 %fusion = f32[3,96,1024]{2,1,0:T(8,128)S(1)} fusion(s32[3,1024]{1,0:T(4,128)S(1)} %broadcast_subtract_fusion, s32[1024]{0:T(1024)S(1)} %fusion.61, s32[3,1024]{1,0:T(4,128)S(1)} %broadcast_subtract_fusion.1, s32[1024]{0:T(1024)S(1)} %add_select_fusion, bf16[3,32,1024]{2,1,0:T(8,128)(2,1)S(1)} %get-tuple-element.50, ...), kind=kOutput, calls=%fused_computation.7 | convolution fusion | flops 615186432 | bytes 1802240 | tf_op jit(solution)/shard_map/pxc,pcy->pxy/dot_general | solution.py:56
  85.3 0.1 broadcast_select_fusion.2
  85.5 1.9 %collective-permute-start.4 = (f32[3,32,1024]{2,1,0:T(8,128)S(1)}, f32[3,32,1024]{2,1,0:T(8,128)S(1)}, u32[]{:S(2)}, u32[]{:S(2)}) collective-permute-start(f32[3,32,1024]{2,1,0:T(8,128)S(1)} %get-tuple-element.43), channel_id=1, source_target_pairs={{0,32},{32,64},{64,96},{96,128},{128,160},{160,192},{192,224},{224... | collective-permute-start | bytes 1179656 | tf_op jit(solution)/shard_map/ppermute | solution.py:14
  87.4 2.7 %collective-permute-start.3 = (s32[3]{0:T(128)S(1)}, s32[3]{0:T(128)S(1)}, u32[]{:S(2)}, u32[]{:S(2)}) collective-permute-start(s32[3]{0:T(128)S(1)} %get-tuple-element.35), channel_id=1, source_target_pairs={{0,32},{32,64},{64,96},{96,128},{128,160},{160,192},{192,224},{224... | collective-permute-start | bytes 44 | tf_op jit(solution)/shard_map/ppermute | solution.py:14
  90.1 0.1 fusion.75
  90.2 0.2 fusion.20
  90.5 1.6 %broadcast_in_dim.206.clone.1 = f32[16,32,1024]{2,1,0:T(8,128)} broadcast(f32[]{:T(128)} %constant.210.clone.1), dimensions={} | broadcast | bytes 2097156 | tf_op jit(solution)/shard_map/broadcast_in_dim | solution.py:200
  92.1 3.0 %scatter_fusion.2 = f32[16,32,1024]{2,1,0:T(8,128)} fusion(f32[16,32,1024]{2,1,0:T(8,128)} %broadcast_in_dim.206.clone.1, s32[6]{0:T(128)S(1)} %fusion.75, f32[6,32,1024]{2,1,0:T(8,128)S(1)} %get-tuple-element.45), kind=kCustom, calls=%fused_computation.4 | custom fusion | flops 196608 | bytes 2359320 | tf_op jit(solution)/shard_map/scatter-add | solution.py:196
  95.1 4.8 %collective-permute-done.3 = s32[3]{0:T(128)S(1)} collective-permute-done((s32[3]{0:T(128)S(1)}, s32[3]{0:T(128)S(1)}, u32[]{:S(2)}, u32[]{:S(2)}) %collective-permute-start.3) | collective-permute-done | bytes 44 | tf_op jit(solution)/shard_map/ppermute | solution.py:14
  99.9 0.1 broadcast_select_fusion
  100.0 2.5 %scatter_fusion.3 = f32[16,32,1024]{2,1,0:T(8,128)} fusion(f32[16,32,1024]{2,1,0:T(8,128)} %scatter_fusion.2, s32[3]{0:T(128)S(1)} %compare_select_fusion.2, f32[3,32,1024]{2,1,0:T(8,128)S(1)} %get-tuple-element.47), kind=kCustom, calls=%fused_computation.5 | custom fusion | flops 98304 | bytes 1179660 | tf_op jit(solution)/shard_map/scatter-add | solution.py:196
  102.5 1.9 %collective-permute-start.5 = (f32[16,32,1024]{2,1,0:T(8,128)}, f32[16,32,1024]{2,1,0:T(8,128)}, u32[]{:S(2)}, u32[]{:S(2)}) collective-permute-start(f32[16,32,1024]{2,1,0:T(8,128)} %scatter_fusion.3), channel_id=1, source_target_pairs={{0,1},{1,0},{2,3},{3,2},{4,5},{5,4},{6,7},{7,6},{8,9},{9,8},{10,11... | collective-permute-start | bytes 6291464 | tf_op jit(solution)/shard_map/ppermute | solution.py:203
  104.4 0.2 broadcast_in_dim.206.clone
  104.7 1.1 scatter_fusion
  105.8 0.8 scatter_fusion.1
  106.6 2.3 %collective-permute-done.5 = f32[16,32,1024]{2,1,0:T(8,128)} collective-permute-done((f32[16,32,1024]{2,1,0:T(8,128)}, f32[16,32,1024]{2,1,0:T(8,128)}, u32[]{:S(2)}, u32[]{:S(2)}) %collective-permute-start.5) | collective-permute-done | bytes 2097184 | tf_op jit(solution)/shard_map/ppermute | solution.py:203
  108.9 2.0 %add.253 = f32[16,32,1024]{2,1,0:T(8,128)S(1)} add(f32[16,32,1024]{2,1,0:T(8,128)S(1)} %scatter_fusion.1, f32[16,32,1024]{2,1,0:T(8,128)} %collective-permute-done.5) | non-fusion elementwise | flops 524288 | bytes 6291456 | tf_op jit(solution)/shard_map/add | solution.py:204
  110.9 31.6 %all_to_all.11 = f32[16,32,1024]{2,1,0:T(8,128)S(1)} all-to-all(f32[16,32,1024]{2,1,0:T(8,128)S(1)} %add.253), channel_id=1, replica_groups=mesh['grp'=16,'yx'=16,'core'=2] {'yx'}, dimensions={0} | all-to-all | bytes 4194304 | tf_op jit(solution)/shard_map/all_to_all | solution.py:205
  142.5 0.8 reduce_sum.39
  (42 shorter events, 1.0 us)
Async XLA Ops:
  0.0 11.1 %collective-permute-start = (bf16[1,32,1024]{2,1,0:T(8,128)(2,1)}, bf16[1,32,1024]{2,1,0:T(8,128)(2,1)S(1)}, u32[]{:S(2)}, u32[]{:S(2)}) collective-permute-start(bf16[1,32,1024]{2,1,0:T(8,128)(2,1)} %param.8), channel_id=1, source_target_pairs={{32,0},{64,32},{96,64},{128,96},{160,128},{192,160},{224,192},{256... | collective-permute-start | bytes 196616 | tf_op jit(solution)/shard_map/ppermute | solution.py:14
  4.2 6.9 %copy-start.1 = (bf16[1,32,1024]{2,1,0:T(8,128)(2,1)S(1)}, bf16[1,32,1024]{2,1,0:T(8,128)(2,1)}, u32[]{:S(2)}) copy-start(bf16[1,32,1024]{2,1,0:T(8,128)(2,1)} %param.8) | copy-start | bytes 196612
  11.1 8.2 %collective-permute-start.1 = (bf16[32,1152]{1,0:T(8,128)(2,1)S(1)}, bf16[32,1152]{1,0:T(8,128)(2,1)S(1)}, u32[]{:S(2)}, u32[]{:S(2)}) collective-permute-start(bf16[32,1152]{1,0:T(8,128)(2,1)S(1)} %get-tuple-element.53), channel_id=1, source_target_pairs={{0,1},{1,0},{2,3},{3,2},{4,5},{5,4},{6,7},{7,6},{8,9},{9,8},{10,11... | collective-permute-start | bytes 221192 | tf_op jit(solution)/shard_map/ppermute | solution.py:129
  58.4 10.4 %copy-start.2 = (s32[512,3]{0,1:T(4,128)S(1)}, s32[512,3]{0,1:T(4,128)}, u32[]{:S(2)}) copy-start(s32[512,3]{0,1:T(4,128)} %param.9) | copy-start | bytes 18436
  58.4 6.7 %collective-permute-start.2 = (bf16[32,32,1152]{2,1,0:T(8,128)(2,1)S(1)}, bf16[32,32,1152]{2,1,0:T(8,128)(2,1)}, u32[]{:S(2)}, u32[]{:S(2)}) collective-permute-start(bf16[32,32,1152]{2,1,0:T(8,128)(2,1)S(1)} %bitcast.46), channel_id=1, source_target_pairs={{0,1},{1,0},{2,3},{3,2},{4,5},{5,4},{6,7},{7,6},{8,9},{9,8},{10,11... | collective-permute-start | bytes 7077896 | tf_op jit(solution)/shard_map/ppermute | solution.py:138
  71.9 3.9 %copy-start = (f32[1024,1024]{1,0:T(8,128)S(1)}, f32[1024,1024]{1,0:T(8,128)}, u32[]{:S(2)}) copy-start(f32[1024,1024]{1,0:T(8,128)} %convolution_multiply_fusion) | copy-start | bytes 12582916
  85.5 14.4 %collective-permute-start.4 = (f32[3,32,1024]{2,1,0:T(8,128)S(1)}, f32[3,32,1024]{2,1,0:T(8,128)S(1)}, u32[]{:S(2)}, u32[]{:S(2)}) collective-permute-start(f32[3,32,1024]{2,1,0:T(8,128)S(1)} %get-tuple-element.43), channel_id=1, source_target_pairs={{0,32},{32,64},{64,96},{96,128},{128,160},{160,192},{192,224},{224... | collective-permute-start | bytes 1179656 | tf_op jit(solution)/shard_map/ppermute | solution.py:14
  87.4 12.4 %collective-permute-start.3 = (s32[3]{0:T(128)S(1)}, s32[3]{0:T(128)S(1)}, u32[]{:S(2)}, u32[]{:S(2)}) collective-permute-start(s32[3]{0:T(128)S(1)} %get-tuple-element.35), channel_id=1, source_target_pairs={{0,32},{32,64},{64,96},{96,128},{128,160},{160,192},{192,224},{224... | collective-permute-start | bytes 44 | tf_op jit(solution)/shard_map/ppermute | solution.py:14
  102.5 6.4 %collective-permute-start.5 = (f32[16,32,1024]{2,1,0:T(8,128)}, f32[16,32,1024]{2,1,0:T(8,128)}, u32[]{:S(2)}, u32[]{:S(2)}) collective-permute-start(f32[16,32,1024]{2,1,0:T(8,128)} %scatter_fusion.3), channel_id=1, source_target_pairs={{0,1},{1,0},{2,3},{3,2},{4,5},{5,4},{6,7},{7,6},{8,9},{9,8},{10,11... | collective-permute-start | bytes 6291464 | tf_op jit(solution)/shard_map/ppermute | solution.py:203
